TPU v7x, 512 devices: a whole 4x4x16 slice. The times are simulated.
512 devices in a mesh: ctx: 32 (over z_hi, x, y), exp: 16 (over z_lo, core).
Axes of the slice: x: 4, y: 4, z: 16 (z_hi: 2, z_lo: 8; z = z_hi * 8 + z_lo), core: 2. Of those that a mesh axis runs over, the one named last changes fastest.
Arguments:
- residual: bfloat16 [4096, 4096], P(('ctx', 'exp')), may hold values from -6 to 6
- queries: bfloat16 [4096, 4096], P('ctx', 'exp'), may hold values from -8 to 8
- keys: bfloat16 [4096, 256], P('ctx'), may hold values from -8 to 8
- values: bfloat16 [4096, 256], P('ctx'), may hold values from -6 to 6
- span_pos: int32 [64], replicated, may hold values from 0 to 63, each once
- out_proj: bfloat16 [4096, 4096], P('exp'), may hold values from -0.71875 to 0.71875
- norm_gain: float32 [4096], replicated, may hold values from 0.25 to 1.75
- expert_gate: bfloat16 [16, 4096, 768], P('exp', None, 'ctx'), may hold values from -0.09375 to 0.09375
- expert_up: bfloat16 [16, 4096, 768], P('exp', None, 'ctx'), may hold values from -0.09375 to 0.09375
- expert_ids: int32 [4096, 8], P(('ctx', 'exp')), may hold values from 0 to 15, all different within a row; in each aligned block of 8 rows (0 to 7, 8 to 15, ...) at most 6 rows name the same one
- route_weight: float32 [4096, 8], P(('ctx', 'exp')), may hold values from 0.25 to 2
Outputs:
- mixed: bfloat16 [4096, 4096], P(('ctx', 'exp'))
- routed: bfloat16 [4096, 8, 768], P(('ctx', 'exp'))
Inputs may be any that keep to these rules, and one draw needn't show every extreme that they name: `span_pos`: every span number appears once. `expert_ids`: each row names 8 different experts; among the rows of one device (8 rows in a row, aligned) no expert is named more than 6 times, and in some device's rows some expert is named exactly 6 times.
All inputs are finite; a program needn't handle non-finite values.
Results may differ from a plain program's by a relative error of at most 0.035.
Values may be sent and summed in bfloat16 or wider, within the bound.
No kernel may reach another device: no remote copies, remote signals or barrier semaphores. Data moves between devices by JAX's collectives and lax.ppermute only.
A program may use at most 128 MiB of HBM per device.

v0:
```python
import math

import jax
import jax.numpy as jnp
from jax import lax
from jax.sharding import PartitionSpec as P

D = 4096
HQ = 32
KVH = 2
HD = 128
FE = 768
EXPERTS = 16
TOPK = 8
CH = 64


def stored_positions(span_pos, first, count):
    rows = first + jnp.arange(count, dtype=jnp.int32)
    span = rows // CH
    table = span[:, None] == jnp.arange(span_pos.shape[0], dtype=jnp.int32)[None, :]
    base = jnp.sum(jnp.where(table, span_pos[None, :], 0), axis=1)
    return base * CH + rows % CH


def hidden_units(rows_in, weight_pair):
    gate = jnp.einsum(
        "esd,edf->esf", rows_in, weight_pair[:, 0], preferred_element_type=jnp.float32
    )
    upper = jnp.einsum(
        "esd,edf->esf", rows_in, weight_pair[:, 1], preferred_element_type=jnp.float32
    )
    return jax.nn.silu(gate) * upper


def shards(
    residual,
    queries,
    keys,
    values,
    span_pos,
    out_proj,
    norm_gain,
    expert_gate,
    expert_up,
    expert_ids,
    route_weight,
):
    weight_pair = jnp.stack((expert_gate, expert_up), axis=1)
    tok_rows = queries.shape[0]
    per_device = queries.shape[1] // HD
    group = HQ // KVH
    ctx_index = lax.axis_index("ctx")
    exp_index = lax.axis_index("exp")
    kv_head = exp_index * per_device // group
    own_keys = lax.dynamic_slice_in_dim(keys, kv_head * HD, HD, 1)
    own_values = lax.dynamic_slice_in_dim(values, kv_head * HD, HD, 1)
    query_pos = stored_positions(span_pos, ctx_index * tok_rows, tok_rows)
    query_heads = queries.reshape(tok_rows, per_device, HD)
    scale = 1.0 / math.sqrt(HD)
    start_carry = (
        jnp.full((per_device, tok_rows), -1e30, jnp.float32),
        jnp.zeros((per_device, tok_rows), jnp.float32),
        jnp.zeros((per_device, tok_rows, HD), jnp.float32),
    )
    carry = start_carry
    start = jnp.int32(0)
    key_piece = lax.all_gather(own_keys, "ctx", axis=0, tiled=True)
    value_piece = lax.all_gather(own_values, "ctx", axis=0, tiled=True)
    length = key_piece.shape[0]
    block = min(length, 1024)
    for begin in range(0, length, block):
        stop = min(begin + block, length)
        attend_key_piece = key_piece[begin:stop]
        attend_value_piece = value_piece[begin:stop]
        attend_start = start + begin
        attend_running, attend_total, attend_accum = carry
        key_pos = stored_positions(span_pos, attend_start, attend_key_piece.shape[0])
        scores = (
            jnp.einsum(
                "tqd,nd->qtn", query_heads, attend_key_piece, preferred_element_type=jnp.float32
            )
            * scale
        )
        visible = key_pos[None, None, :] <= query_pos[None, :, None]
        block_top = jnp.max(jnp.where(visible, scores, -1e30), axis=2)
        new_top = jnp.maximum(attend_running, block_top)
        factor = jnp.exp(attend_running - new_top)
        probs = jnp.where(visible, jnp.exp(scores - new_top[:, :, None]), 0.0)
        attend_total = attend_total * factor + jnp.sum(probs, axis=2)
        summed = jnp.einsum(
            "qtn,nd->qtd",
            probs.astype(jnp.bfloat16),
            attend_value_piece,
            preferred_element_type=jnp.float32,
        )
        attend_accum = attend_accum * factor[:, :, None] + summed
        carry = (new_top, attend_total, attend_accum)
    running, total, accum = carry
    attn = (accum / total[:, :, None]).astype(jnp.bfloat16)
    attn = jnp.transpose(attn, (1, 0, 2)).reshape(tok_rows, per_device * HD)
    tok_dev = residual.shape[0]
    head_total = lax.psum_scatter(
        jnp.dot(attn, out_proj, preferred_element_type=jnp.float32).astype(jnp.bfloat16),
        "exp",
        scatter_dimension=0,
        tiled=True,
    ).astype(jnp.float32)
    mixed = (residual.astype(jnp.float32) + head_total).astype(jnp.bfloat16)
    mixed_f = mixed.astype(jnp.float32)
    square = jnp.mean(mixed_f * mixed_f, axis=1, keepdims=True)
    normed = (mixed_f * lax.rsqrt(square + 1e-06) * norm_gain[None, :]).astype(jnp.bfloat16)
    most_slots = 3 * tok_dev // 4
    ids_flat = expert_ids.reshape(-1)
    onehot = (ids_flat[:, None] == jnp.arange(EXPERTS, dtype=jnp.int32)[None, :]).astype(jnp.int32)
    earlier = jnp.cumsum(onehot, axis=0) - onehot
    slot = jnp.sum(earlier * onehot, axis=1)
    target = ids_flat * most_slots + slot
    placing = (
        target[:, None] == jnp.arange(EXPERTS * most_slots, dtype=jnp.int32)[None, :]
    ).astype(jnp.bfloat16)
    placing = jnp.sum(placing.reshape(tok_dev, TOPK, EXPERTS * most_slots), axis=1)
    outgoing = jnp.einsum("ts,td->sd", placing, normed, preferred_element_type=jnp.float32).astype(
        jnp.bfloat16
    )
    outgoing = outgoing.reshape(EXPERTS, most_slots, D)
    received = lax.all_to_all(outgoing, "exp", split_axis=0, concat_axis=1, tiled=True)
    hidden = hidden_units(received, lax.all_gather(weight_pair, "ctx", axis=3, tiled=True))
    returned = (
        lax.all_to_all(hidden.astype(jnp.bfloat16), "exp", split_axis=1, concat_axis=0, tiled=True)
        .astype(hidden.dtype)
        .reshape(EXPERTS * most_slots, FE)
    )
    picked = jnp.take(returned, target, axis=0)
    routed = (picked * route_weight.reshape(-1)[:, None]).astype(jnp.bfloat16)
    return (mixed, routed.reshape(tok_dev, TOPK, FE))


def solution(mesh):
    in_specs = (
        P(("ctx", "exp"), None),
        P("ctx", "exp"),
        P("ctx", None),
        P("ctx", None),
        P(),
        P("exp", None),
        P(),
        P("exp", None, "ctx"),
        P("exp", None, "ctx"),
        P(("ctx", "exp"), None),
        P(("ctx", "exp"), None),
    )
    out_specs = (P(("ctx", "exp"), None), P(("ctx", "exp"), None, None))
    return jax.shard_map(shards, mesh=mesh, in_specs=in_specs, out_specs=out_specs, check_vma=False)
```

profile of v0, /device:TPU:1, one launch (start us, length us, event | category | flops | bytes accessed | tf_op | source)
XLA Modules:
  0.0 739.2 jit_solution(4810153758489183769)
XLA Ops:
  7.2 1.5 constant_dynamic-slice_fusion.1
  12.1 1.8 broadcast_compare_fusion.1
  14.0 114.5 %all-gather.4.cloned.1.call-done = bf16[4096,128]{1,0:T(8,128)(2,1)} async-done(((bf16[128,128]{1,0:T(8,128)(2,1)}), bf16[4096,128]{1,0:T(8,128)(2,1)}) %all-gather.4.cloned.1.call-update) | async-done | bytes 1048592 | tf_op jit(solution)/shard_map/all_gather | solution.py:68
  128.5 1.3 select_reduce_fusion
  131.1 1.5 select_reduce_fusion.2
  132.6 1.7 select_reduce_fusion.3
  136.2 102.0 %all-gather.6.cloned.1.call-done = bf16[4096,128]{0,1:T(8,128)(2,1)} async-done(((bf16[128,128]{0,1:T(8,128)(2,1)}), bf16[4096,128]{0,1:T(8,128)(2,1)}) %all-gather.6.cloned.1.call-update) | async-done | bytes 1048592 | tf_op jit(solution)/shard_map/all_gather | solution.py:69
  238.2 1.7 fusion.16
  239.8 1.6 fusion.14
  241.4 1.6 fusion.12
  243.1 1.3 fusion.17
  244.4 1.5 convolution_convert_fusion
  246.0 1.7 pad_maximum_fusion
  248.4 88.6 %reduce-scatter.2.cloned.1.call-done = bf16[8,4096]{1,0:T(8,128)(2,1)} async-done(((bf16[128,4096]{1,0:T(8,128)(2,1)}), bf16[8,4096]{1,0:T(8,128)(2,1)}) %reduce-scatter.2.cloned.1.call-update) | async-done | bytes 65552 | tf_op jit(solution)/shard_map/reduce_scatter | solution.py:103
  338.0 2.1 convolution_convert_fusion.1
  340.1 1.4 reshape.501
  341.5 72.5 %all_to_all.8 = bf16[16,6,4096]{2,1,0:T(8,128)(2,1)} all-to-all(bf16[16,6,4096]{2,1,0:T(8,128)(2,1)S(1)} %reshape.501), channel_id=1, replica_groups=mesh['ctx'=32,'exp'=16] {'exp'}, dimensions={0} | all-to-all | bytes 1572864 | tf_op jit(solution)/shard_map/all_to_all | solution.py:127
  414.0 1.4 reshape.502
  415.4 265.9 %all-gather.8.cloned.1.call-done = bf16[1,2,4096,768]{2,3,1,0:T(8,128)(2,1)} async-done(((bf16[1,2,4096,24]{2,3,1,0:T(8,128)(2,1)}), bf16[1,2,4096,768]{2,3,1,0:T(8,128)(2,1)}) %all-gather.8.cloned.1.call-update) | async-done | bytes 12582928 | tf_op jit(solution)/shard_map/all_gather | solution.py:128
  681.3 4.8 fusion.1
  686.2 4.9 fusion.8
  691.8 1.5 reduce.1
  694.0 24.6 %all-to-all-start.1 = ((bf16[16,2,2304]{2,1,0:T(2,128)(2,1)}), bf16[16,2,2304]{2,1,0:T(2,128)(2,1)S(1)}, u32[]{:S(2)}, u32[]{:S(2)}) async-start(bf16[16,2,2304]{2,1,0:T(2,128)(2,1)} %reshape.522), calls=%async_computation.2 | async-start | bytes 294912 | tf_op jit(solution)/shard_map/all_to_all | solution.py:130
  718.7 12.4 %all-to-all-done.1 = bf16[16,2,2304]{2,1,0:T(2,128)(2,1)S(1)} async-done(((bf16[16,2,2304]{2,1,0:T(2,128)(2,1)}), bf16[16,2,2304]{2,1,0:T(2,128)(2,1)S(1)}, u32[]{:S(2)}, u32[]{:S(2)}) %all-to-all-start.1) | async-done | bytes 147488 | tf_op jit(solution)/shard_map/all_to_all | solution.py:130
  (67 shorter events, 11.3 us)
Async XLA Ops:
  7.2 237.2 %copy-start = (bf16[256,4096]{1,0:T(8,128)(2,1)S(1)}, bf16[256,4096]{1,0:T(8,128)(2,1)}, u32[]{:S(2)}) copy-start(bf16[256,4096]{1,0:T(8,128)(2,1)} %param.16) | copy-start | bytes 6291460
  7.2 121.3 %all-gather.4.cloned.1.call-start = ((), (), s32[]{:S(2)}) async-start(), calls=%async_computation.3 | async-start | bytes 1081344 | tf_op jit(solution)/shard_map/all_gather | solution.py:68
  8.8 229.4 %all-gather.6.cloned.1.call-start = ((), (), s32[]{:S(2)}) async-start(), calls=%async_computation.4 | async-start | bytes 1081344 | tf_op jit(solution)/shard_map/all_gather | solution.py:69
  10.4 326.6 %reduce-scatter.2.cloned.1.call-start = ((), (), s32[]{:S(2)}) async-start(), calls=%async_computation.5 | async-start | bytes 1114112 | tf_op jit(solution)/shard_map/reduce_scatter | solution.py:103
  128.5 5.9 copy-start.4
  131.1 3.8 copy-start.1
  132.6 2.5 copy-start.2
  134.4 1.0 copy-start.3
  134.4 103.8 %copy-start.9 = (f32[2,128]{1,0:T(2,128)}, f32[2,128]{1,0:T(2,128)S(1)}, u32[]{:S(2)}) copy-start(f32[2,128]{1,0:T(2,128)S(1)} %get-tuple-element.18) | copy-start | bytes 3076
  238.2 9.6 %copy-start.7 = (s32[8,8]{1,0:T(8,128)S(1)}, s32[8,8]{1,0:T(8,128)}, u32[]{:S(2)}) copy-start(s32[8,8]{1,0:T(8,128)} %param.20) | copy-start | bytes 772
  243.1 3.0 copy-start.6
  246.0 435.3 %all-gather.8.cloned.1.call-start = ((), (), s32[]{:S(2)}) async-start(), calls=%async_computation.6 | async-start | bytes 12976128 | tf_op jit(solution)/shard_map/all_gather | solution.py:128
  338.0 348.1 %copy-start.5 = (bf16[8,4096]{1,0:T(8,128)(2,1)}, bf16[8,4096]{1,0:T(8,128)(2,1)S(1)}, u32[]{:S(2)}) copy-start(bf16[8,4096]{1,0:T(8,128)(2,1)S(1)} %get-tuple-element.9) | copy-start | bytes 196612
  686.1 45.8 %copy-start.8 = (f32[8,8]{1,0:T(8,128)S(1)}, f32[8,8]{1,0:T(8,128)}, u32[]{:S(2)}) copy-start(f32[8,8]{1,0:T(8,128)} %param.21) | copy-start | bytes 772
  694.0 37.1 %all-to-all-start.1 = ((bf16[16,2,2304]{2,1,0:T(2,128)(2,1)}), bf16[16,2,2304]{2,1,0:T(2,128)(2,1)S(1)}, u32[]{:S(2)}, u32[]{:S(2)}) async-start(bf16[16,2,2304]{2,1,0:T(2,128)(2,1)} %reshape.522), calls=%async_computation.2 | async-start | bytes 294912 | tf_op jit(solution)/shard_map/all_to_all | solution.py:130
Sparse Core Ops, SparseCore 0:
  12.9 115.5 all-gather.3
  133.1 105.0 all-gather.5
  246.1 90.8 reduce-scatter.1
  341.9 339.3 all-gather.7
where the time goes:
time: 740 us; the launch traced here: 739 us
  waiting for transfers between devices  583 us (79%)
  blocking collectives  72.5 us (10%)
  matrix products  25.4 us (3%)
  starting transfers between devices  24.8 us (3%)
  between operations  14.1 us (2%)
  other arithmetic  10.5 us (1%)
  local copies, waits for them, and re-layouts  8.63 us (1%)
    all_gather x1, waiting for transfers between devices, shards(): lax.all_gather(weight_pair, 'ctx', axis=3, tiled=True)  266 us
    all_gather x1, waiting for transfers between devices, shards(): key_piece = lax.all_gather(own_keys, 'ctx', axis=0, tiled=True)  114 us
    all_gather x1, waiting for transfers between devices, shards(): value_piece = lax.all_gather(own_values, 'ctx', axis=0, tiled=True)  102 us
    reduce_scatter x1, waiting for transfers between devices, shards(): lax.psum_scatter(jnp.dot(attn, out_proj, preferred_element_type=jnp.float...  88.6 us
    all_to_all x1, blocking collectives, shards(): lax.all_to_all(outgoing, 'exp', split_axis=0, concat_axis=1, tiled=True)  72.5 us
    all_to_all x1, starting transfers between devices, shards(): lax.all_to_all(hidden.astype(jnp.bfloat16), 'exp', split_axis=1, concat_a...  24.6 us
  transfers between devices with their start and end apart: 5, of which 5 were waited for; matrix products, arithmetic and copies ran while one was open for 3% of the time, Pallas kernels for 0%

commit v1 on v0

v1 whole, which is shorter than its diff:
```python
import math

import jax
import jax.numpy as jnp
import numpy as np
from jax import lax
from jax.sharding import Mesh
from jax.sharding import PartitionSpec as P

D = 4096
HQ = 32
KVH = 2
HD = 128
FE = 768
EXPERTS = 16
TOPK = 8
CH = 64

CTX = ("zh", "x", "y")
EXP = ("zl", "c")


def stored_positions(span_pos, rows):
    span = rows // CH
    table = span[:, None] == jnp.arange(span_pos.shape[0], dtype=jnp.int32)[None, :]
    base = jnp.sum(jnp.where(table, span_pos[None, :], 0), axis=1)
    return base * CH + rows % CH


def doubling_bits(n):
    bits = []
    b = n // 2
    while b >= 1:
        bits.append(b)
        b //= 2
    return bits


def gather_by_doubling(piece, n):
    idx = lax.axis_index(CTX)
    cur = piece
    order = [0]
    for bit in doubling_bits(n):
        other = lax.ppermute(cur, CTX, [(i, i ^ bit) for i in range(n)])
        low = (idx & bit) == 0
        cur = jnp.where(low, jnp.concatenate([cur, other]), jnp.concatenate([other, cur]))
        order = order + [o + bit for o in order]
    return cur, order


def shards(
    residual,
    queries,
    keys,
    values,
    span_pos,
    out_proj,
    norm_gain,
    expert_gate,
    expert_up,
    expert_ids,
    route_weight,
    n_ctx,
    n_xy,
    n_zh,
):
    tok_rows = queries.shape[0]
    per_device = queries.shape[1] // HD
    group = HQ // KVH
    ctx_index = lax.axis_index(CTX)
    exp_index = lax.axis_index(EXP)
    n_exp = EXPERTS

    fe_dev = expert_gate.shape[2]
    w_local = jnp.concatenate([expert_gate[0].T, expert_up[0].T], axis=0)
    w_all = lax.all_gather(w_local, "zh", axis=0, tiled=True)
    w_all = lax.all_gather(w_all, ("x", "y"), axis=0, tiled=True)

    kv_head = exp_index * per_device // group
    own_keys = lax.dynamic_slice_in_dim(keys, kv_head * HD, HD, 1)
    own_values = lax.dynamic_slice_in_dim(values, kv_head * HD, HD, 1)
    kv_local = jnp.concatenate([own_keys, own_values], axis=1)
    kv_all, order = gather_by_doubling(kv_local, n_ctx)
    key_piece = kv_all[:, :HD]
    value_piece = kv_all[:, HD:]
    length = key_piece.shape[0]
    block_ctx = jnp.asarray(np.array(order, np.int32))
    key_rows_all = (
        jnp.repeat(block_ctx, tok_rows) * tok_rows
        + jnp.tile(jnp.arange(tok_rows, dtype=jnp.int32), n_ctx)
    )

    query_pos = stored_positions(
        span_pos, ctx_index * tok_rows + jnp.arange(tok_rows, dtype=jnp.int32)
    )
    query_heads = queries.reshape(tok_rows, per_device, HD)
    scale = 1.0 / math.sqrt(HD)
    carry = (
        jnp.full((per_device, tok_rows), -1e30, jnp.float32),
        jnp.zeros((per_device, tok_rows), jnp.float32),
        jnp.zeros((per_device, tok_rows, HD), jnp.float32),
    )
    block = min(length, 1024)
    for begin in range(0, length, block):
        stop = min(begin + block, length)
        attend_key_piece = key_piece[begin:stop]
        attend_value_piece = value_piece[begin:stop]
        attend_running, attend_total, attend_accum = carry
        key_pos = stored_positions(span_pos, key_rows_all[begin:stop])
        scores = (
            jnp.einsum(
                "tqd,nd->qtn", query_heads, attend_key_piece, preferred_element_type=jnp.float32
            )
            * scale
        )
        visible = key_pos[None, None, :] <= query_pos[None, :, None]
        block_top = jnp.max(jnp.where(visible, scores, -1e30), axis=2)
        new_top = jnp.maximum(attend_running, block_top)
        factor = jnp.exp(attend_running - new_top)
        probs = jnp.where(visible, jnp.exp(scores - new_top[:, :, None]), 0.0)
        attend_total = attend_total * factor + jnp.sum(probs, axis=2)
        summed = jnp.einsum(
            "qtn,nd->qtd",
            probs.astype(jnp.bfloat16),
            attend_value_piece,
            preferred_element_type=jnp.float32,
        )
        attend_accum = attend_accum * factor[:, :, None] + summed
        carry = (new_top, attend_total, attend_accum)
    running, total, accum = carry
    attn = (accum / total[:, :, None]).astype(jnp.bfloat16)
    attn = jnp.transpose(attn, (1, 0, 2)).reshape(tok_rows, per_device * HD)
    tok_dev = residual.shape[0]

    share = jnp.dot(attn, out_proj, preferred_element_type=jnp.float32).astype(jnp.bfloat16)
    shares = lax.all_to_all(
        share.reshape(n_exp, tok_dev, D), EXP, split_axis=0, concat_axis=0, tiled=True
    )
    head_total = jnp.sum(shares.astype(jnp.float32), axis=0)
    mixed = (residual.astype(jnp.float32) + head_total).astype(jnp.bfloat16)
    mixed_f = mixed.astype(jnp.float32)
    square = jnp.mean(mixed_f * mixed_f, axis=1, keepdims=True)
    normed = (mixed_f * lax.rsqrt(square + 1e-06) * norm_gain[None, :]).astype(jnp.bfloat16)

    most_slots = 3 * tok_dev // 4
    ids_flat = expert_ids.reshape(-1)
    onehot = (ids_flat[:, None] == jnp.arange(EXPERTS, dtype=jnp.int32)[None, :]).astype(jnp.int32)
    earlier = jnp.cumsum(onehot, axis=0) - onehot
    slot = jnp.sum(earlier * onehot, axis=1)
    target = ids_flat * most_slots + slot
    placing = (
        target[:, None] == jnp.arange(EXPERTS * most_slots, dtype=jnp.int32)[None, :]
    ).astype(jnp.bfloat16)
    placing = jnp.sum(placing.reshape(tok_dev, TOPK, EXPERTS * most_slots), axis=1)
    outgoing = jnp.einsum("ts,td->sd", placing, normed, preferred_element_type=jnp.float32).astype(
        jnp.bfloat16
    )
    outgoing = outgoing.reshape(EXPERTS, most_slots, D)
    received = lax.all_to_all(outgoing, EXP, split_axis=0, concat_axis=0, tiled=True)
    received = received.reshape(EXPERTS * most_slots, D)

    proj = jnp.einsum("sd,fd->sf", received, w_all, preferred_element_type=jnp.float32)
    proj = proj.reshape(EXPERTS * most_slots, n_xy, n_zh, 2, fe_dev)
    hidden = jax.nn.silu(proj[:, :, :, 0]) * proj[:, :, :, 1]
    hidden = jnp.transpose(hidden, (0, 2, 1, 3)).reshape(EXPERTS, most_slots, FE)
    returned = (
        lax.all_to_all(hidden.astype(jnp.bfloat16), EXP, split_axis=0, concat_axis=0, tiled=True)
        .astype(jnp.float32)
        .reshape(EXPERTS * most_slots, FE)
    )
    picked = jnp.take(returned, target, axis=0)
    routed = (picked * route_weight.reshape(-1)[:, None]).astype(jnp.bfloat16)
    return (mixed, routed.reshape(tok_dev, TOPK, FE))


def solution(mesh):
    n_ctx = mesh.shape["ctx"]
    n_exp = mesh.shape["exp"]
    n_zh = 2
    n_xy = n_ctx // n_zh
    side = int(round(math.sqrt(n_xy)))
    n_zl = n_exp // 2
    fine = Mesh(mesh.devices.reshape(n_zh, side, n_xy // side, n_zl, 2), CTX + EXP)
    tok = CTX + EXP
    in_specs = (
        P(tok, None),
        P(CTX, EXP),
        P(CTX, None),
        P(CTX, None),
        P(),
        P(EXP, None),
        P(),
        P(EXP, None, CTX),
        P(EXP, None, CTX),
        P(tok, None),
        P(tok, None),
    )
    out_specs = (P(tok, None), P(tok, None, None))

    def body(*args):
        return shards(*args, n_ctx=n_ctx, n_xy=n_xy, n_zh=n_zh)

    return jax.shard_map(body, mesh=fine, in_specs=in_specs, out_specs=out_specs, check_vma=False)
```

time: 740 us -> 316 us (0.43)
  waiting for transfers between devices: 583 us -> 133 us
  starting transfers between devices: 24.8 us -> 54.6 us
  blocking collectives: 72.5 us -> 87.7 us
  matrix products: 25.4 us -> 12.1 us
    all_gather x3 -> x1, waiting for transfers between devices: 482 us -> 0.02 us  [shards(): w_all = lax.all_gather(w_all, ('x', 'y'), axis=0, tiled=True)]
    reduce_scatter x1 -> x0, waiting for transfers between devices: 88.6 us -> none  [shards(): lax.psum_scatter(jnp.dot(attn, out_proj, preferred_element_type=jnp.float...]
    ppermute x0 -> x5, waiting for transfers between devices: none -> 74.3 us  [gather_by_doubling(): other = lax.ppermute(cur, CTX, [(i, i ^ bit) for i in range(n)])]
    all_to_all x1 -> x2, waiting for transfers between devices: 12.4 us -> 58.3 us  [the longest x1 43.8 us: shards(): lax.all_to_all(share.reshape(n_exp, tok_dev, D), EXP, split_axis=0, conca...]
    ppermute x0 -> x5, starting transfers between devices: none -> 29 us  [gather_by_doubling(): other = lax.ppermute(cur, CTX, [(i, i ^ bit) for i in range(n)])]
    all_gather x0 -> x1, blocking collectives: none -> 27 us  [shards(): w_all = lax.all_gather(w_local, 'zh', axis=0, tiled=True)]
    all_to_all x1, blocking collectives: 72.5 us -> 60.6 us  [shards(): lax.all_to_all(outgoing, EXP, split_axis=0, concat_axis=0, tiled=True)]
    all_to_all x1 -> x2, starting transfers between devices: 24.6 us -> 25.6 us  [the longest x1 19.6 us: shards(): lax.all_to_all(share.reshape(n_exp, tok_dev, D), EXP, split_axis=0, conca...]
  transfers between devices with their start and end apart: 5 -> 8, of which waited for: 5 -> 7; matrix products, arithmetic and copies ran while one was open for 3% -> 4% of each run, Pallas kernels for 0% -> 0%
where the time goes in v1:
time: 316 us; the launch traced here: 314 us
  waiting for transfers between devices  133 us (42%)
  blocking collectives  87.7 us (28%)
  starting transfers between devices  54.6 us (17%)
  between operations  14.5 us (5%)
  matrix products  12.1 us (4%)
  local copies, waits for them, and re-layouts  6.76 us (2%)
  other arithmetic  6.11 us (2%)
    ppermute x5, waiting for transfers between devices, gather_by_doubling(): other = lax.ppermute(cur, CTX, [(i, i ^ bit) for i in range(n)])  74.3 us
    all_to_all x1, blocking collectives, shards(): lax.all_to_all(outgoing, EXP, split_axis=0, concat_axis=0, tiled=True)  60.6 us
    all_to_all x1, waiting for transfers between devices, shards(): lax.all_to_all(share.reshape(n_exp, tok_dev, D), EXP, split_axis=0, conca...  43.8 us
    ppermute x5, starting transfers between devices, gather_by_doubling(): other = lax.ppermute(cur, CTX, [(i, i ^ bit) for i in range(n)])  29 us
    all_gather x1, blocking collectives, shards(): w_all = lax.all_gather(w_local, 'zh', axis=0, tiled=True)  27 us
    all_to_all x1, starting transfers between devices, shards(): lax.all_to_all(share.reshape(n_exp, tok_dev, D), EXP, split_axis=0, conca...  19.6 us
    all_to_all x1, waiting for transfers between devices, shards(): lax.all_to_all(hidden.astype(jnp.bfloat16), EXP, split_axis=0, concat_axi...  14.6 us
    dot_general x1, matrix products, shards(): jnp.einsum('sd,fd->sf', received, w_all, preferred_element_type=jnp.float32)  6.41 us
  transfers between devices with their start and end apart: 8, of which 7 were waited for; matrix products, arithmetic and copies ran while one was open for 4% of the time, Pallas kernels for 0%

profile of v1, /device:TPU:1, one launch (start us, length us, event | category | flops | bytes accessed | tf_op | source)
XLA Modules:
  0.0 314.5 jit_solution(2825617987332319186)
XLA Ops:
  7.2 1.2 pad_maximum_fusion
  8.5 27.0 %all_gather.6 = bf16[96,4096]{1,0:T(8,128)(2,1)} all-gather(bf16[48,4096]{1,0:T(8,128)(2,1)S(1)} %pad_maximum_fusion), channel_id=1, replica_groups=mesh['zh'=2,'x'=4,'y'=4,'zl'=8,'c'=2] {'zh'}, dimensions={0}, use_global_device_ids=true | all-gather | bytes 1179648 | tf_op jit(solution)/shard_map/all_gather | solution.py:76
  35.6 13.1 %collective-permute-start = (bf16[128,256]{1,0:T(8,128)(2,1)S(1)}, bf16[128,256]{1,0:T(8,128)(2,1)S(1)}, u32[]{:S(2)}, u32[]{:S(2)}) collective-permute-start(bf16[128,256]{1,0:T(8,128)(2,1)S(1)} %pad_maximum_fusion.1), channel_id=1, source_target_pairs={{0,256},{16,272},{32,288},{48,304},{64,320},{80,336},{96,352},{112... | collective-permute-start | bytes 196616 | tf_op jit(solution)/shard_map/ppermute | solution.py:44
  48.7 17.1 %collective-permute-done = bf16[128,256]{1,0:T(8,128)(2,1)S(1)} collective-permute-done((bf16[128,256]{1,0:T(8,128)(2,1)S(1)}, bf16[128,256]{1,0:T(8,128)(2,1)S(1)}, u32[]{:S(2)}, u32[]{:S(2)}) %collective-permute-start) | collective-permute-done | bytes 65568 | tf_op jit(solution)/shard_map/ppermute | solution.py:44
  65.9 4.7 %collective-permute-start.1 = (bf16[256,256]{1,0:T(8,128)(2,1)S(1)}, bf16[256,256]{1,0:T(8,128)(2,1)S(1)}, u32[]{:S(2)}, u32[]{:S(2)}) collective-permute-start(bf16[256,256]{1,0:T(8,128)(2,1)S(1)} %maximum_select_fusion.4), channel_id=1, source_target_pairs={{0,128},{16,144},{32,160},{48,176},{64,192},{80,208},{96,224},{112... | collective-permute-start | bytes 393224 | tf_op jit(solution)/shard_map/ppermute | solution.py:44
  70.5 3.1 collective-permute-done.1
  73.7 3.1 collective-permute-start.2
  76.8 8.6 %collective-permute-done.2 = bf16[512,256]{1,0:T(8,128)(2,1)S(1)} collective-permute-done((bf16[512,256]{1,0:T(8,128)(2,1)S(1)}, bf16[512,256]{1,0:T(8,128)(2,1)S(1)}, u32[]{:S(2)}, u32[]{:S(2)}) %collective-permute-start.2) | collective-permute-done | bytes 262176 | tf_op jit(solution)/shard_map/ppermute | solution.py:44
  85.7 5.7 %collective-permute-start.3 = (bf16[1024,256]{1,0:T(8,128)(2,1)S(1)}, bf16[1024,256]{1,0:T(8,128)(2,1)S(1)}, u32[]{:S(2)}, u32[]{:S(2)}) collective-permute-start(bf16[1024,256]{1,0:T(8,128)(2,1)S(1)} %maximum_select_fusion.2), channel_id=1, source_target_pairs={{0,32},{16,48},{32,0},{48,16},{64,96},{80,112},{96,64},{112,80},{1... | collective-permute-start | bytes 1572872 | tf_op jit(solution)/shard_map/ppermute | solution.py:44
  91.6 15.4 %collective-permute-done.3 = bf16[1024,256]{1,0:T(8,128)(2,1)S(1)} collective-permute-done((bf16[1024,256]{1,0:T(8,128)(2,1)S(1)}, bf16[1024,256]{1,0:T(8,128)(2,1)S(1)}, u32[]{:S(2)}, u32[]{:S(2)}) %collective-permute-start.3) | collective-permute-done | bytes 524320 | tf_op jit(solution)/shard_map/ppermute | solution.py:44
  107.2 2.5 collective-permute-start.4
  110.8 30.2 %collective-permute-done.4 = bf16[2048,256]{1,0:T(8,128)(2,1)S(1)} collective-permute-done((bf16[2048,256]{1,0:T(8,128)(2,1)S(1)}, bf16[2048,256]{1,0:T(8,128)(2,1)S(1)}, u32[]{:S(2)}, u32[]{:S(2)}) %collective-permute-start.4) | collective-permute-done | bytes 1048608 | tf_op jit(solution)/shard_map/ppermute | solution.py:44
  145.3 1.5 fusion
  146.8 19.6 %all-to-all-start = ((bf16[16,8,4096]{2,1,0:T(8,128)(2,1)}), bf16[16,8,4096]{2,1,0:T(8,128)(2,1)S(1)}, u32[]{:S(2)}, u32[]{:S(2)}) async-start(bf16[16,8,4096]{2,1,0:T(8,128)(2,1)} %fusion), calls=%async_computation | async-start | bytes 2097152 | tf_op jit(solution)/shard_map/all_to_all | solution.py:136
  167.0 43.8 %all-to-all-done = bf16[16,8,4096]{2,1,0:T(8,128)(2,1)S(1)} async-done(((bf16[16,8,4096]{2,1,0:T(8,128)(2,1)}), bf16[16,8,4096]{2,1,0:T(8,128)(2,1)S(1)}, u32[]{:S(2)}, u32[]{:S(2)}) %all-to-all-start) | async-done | bytes 1048608 | tf_op jit(solution)/shard_map/all_to_all | solution.py:136
  211.1 1.3 convolution_convert_fusion.1
  212.5 1.4 reshape.361
  213.9 60.6 %all_to_all.15 = bf16[16,6,4096]{2,1,0:T(8,128)(2,1)} all-to-all(bf16[16,6,4096]{2,1,0:T(8,128)(2,1)S(1)} %reshape.361), channel_id=1, replica_groups=mesh['zh'=2,'x'=4,'y'=4,'zl'=8,'c'=2] {'zl','c'}, dimensions={0} | all-to-all | bytes 1572864 | tf_op jit(solution)/shard_map/all_to_all | solution.py:159
  274.5 1.4 reshape.383
  276.0 6.4 %fusion.22 = f32[96,16,2,2,24]{0,4,3,2,1:T(8,128)S(1)} fusion(bf16[16,2,2,24,4096]{4,3,2,1,0:T(8,128)(2,1)} %bitcast.294, bf16[96,4096,1,1,1]{1,0,2,3,4:T(8,128)(2,1)S(1)} %reshape.383), kind=kOutput, calls=%fused_computation.44 | convolution fusion | flops 1207959552 | bytes 13959168 | tf_op jit(solution)/shard_map/sd,fd->sf/dot_general | solution.py:162
  282.5 1.1 copy.54
  283.6 1.8 convert_element_type.76
  285.4 6.1 %all-to-all-start.2 = ((bf16[16,6,768]{2,1,0:T(8,128)(2,1)}), bf16[16,6,768]{2,1,0:T(8,128)(2,1)S(1)}, u32[]{:S(2)}, u32[]{:S(2)}) async-start(bf16[16,6,768]{2,1,0:T(8,128)(2,1)} %convert_element_type.76), calls=%async_computation.2 | async-start | bytes 393216 | tf_op jit(solution)/shard_map/all_to_all | solution.py:167
  291.6 14.6 %all-to-all-done.2 = bf16[16,6,768]{2,1,0:T(8,128)(2,1)S(1)} async-done(((bf16[16,6,768]{2,1,0:T(8,128)(2,1)}), bf16[16,6,768]{2,1,0:T(8,128)(2,1)S(1)}, u32[]{:S(2)}, u32[]{:S(2)}) %all-to-all-start.2) | async-done | bytes 147488 | tf_op jit(solution)/shard_map/all_to_all | solution.py:167
  (71 shorter events, 8.8 us)
Async XLA Ops:
  7.2 138.1 %copy-start = (bf16[256,4096]{1,0:T(8,128)(2,1)S(1)}, bf16[256,4096]{1,0:T(8,128)(2,1)}, u32[]{:S(2)}) copy-start(bf16[256,4096]{1,0:T(8,128)(2,1)} %param.17) | copy-start | bytes 6291460
  7.2 28.4 %copy-start.5 = (bf16[128,256]{1,0:T(8,128)(2,1)S(1)}, bf16[128,256]{1,0:T(8,128)(2,1)}, u32[]{:S(2)}) copy-start(bf16[128,256]{1,0:T(8,128)(2,1)} %param.15) | copy-start | bytes 196612
  7.2 28.4 %copy-start.6 = (bf16[128,256]{1,0:T(8,128)(2,1)S(1)}, bf16[128,256]{1,0:T(8,128)(2,1)}, u32[]{:S(2)}) copy-start(bf16[128,256]{1,0:T(8,128)(2,1)} %param.14) | copy-start | bytes 196612
  7.2 268.7 %all-gather.2.cloned.1.call-start = ((), (), s32[]{:S(2)}) async-start(), calls=%async_computation.3 | async-start | bytes 13369344 | tf_op jit(solution)/shard_map/all_gather | solution.py:77
  8.4 83.0 %copy-start.8 = (s32[64]{0:T(128)S(1)}, s32[64]{0:T(128)}, u32[]{:S(2)}) copy-start(s32[64]{0:T(128)} %param.16) | copy-start | bytes 772
  8.5 83.1 %copy-start.9 = (s32[32]{0:T(128)S(1)}, s32[32]{0:T(128)}, u32[]{:S(2)}) copy-start(s32[32]{0:T(128)} %constant.180) | copy-start | bytes 388
  35.6 30.2 %collective-permute-start = (bf16[128,256]{1,0:T(8,128)(2,1)S(1)}, bf16[128,256]{1,0:T(8,128)(2,1)S(1)}, u32[]{:S(2)}, u32[]{:S(2)}) collective-permute-start(bf16[128,256]{1,0:T(8,128)(2,1)S(1)} %pad_maximum_fusion.1), channel_id=1, source_target_pairs={{0,256},{16,272},{32,288},{48,304},{64,320},{80,336},{96,352},{112... | collective-permute-start | bytes 196616 | tf_op jit(solution)/shard_map/ppermute | solution.py:44
  65.9 7.7 %collective-permute-start.1 = (bf16[256,256]{1,0:T(8,128)(2,1)S(1)}, bf16[256,256]{1,0:T(8,128)(2,1)S(1)}, u32[]{:S(2)}, u32[]{:S(2)}) collective-permute-start(bf16[256,256]{1,0:T(8,128)(2,1)S(1)} %maximum_select_fusion.4), channel_id=1, source_target_pairs={{0,128},{16,144},{32,160},{48,176},{64,192},{80,208},{96,224},{112... | collective-permute-start | bytes 393224 | tf_op jit(solution)/shard_map/ppermute | solution.py:44
  73.7 11.8 %collective-permute-start.2 = (bf16[512,256]{1,0:T(8,128)(2,1)S(1)}, bf16[512,256]{1,0:T(8,128)(2,1)S(1)}, u32[]{:S(2)}, u32[]{:S(2)}) collective-permute-start(bf16[512,256]{1,0:T(8,128)(2,1)S(1)} %maximum_select_fusion.3), channel_id=1, source_target_pairs={{0,64},{16,80},{32,96},{48,112},{64,0},{80,16},{96,32},{112,48},{1... | collective-permute-start | bytes 786440 | tf_op jit(solution)/shard_map/ppermute | solution.py:44
  85.7 21.2 %collective-permute-start.3 = (bf16[1024,256]{1,0:T(8,128)(2,1)S(1)}, bf16[1024,256]{1,0:T(8,128)(2,1)S(1)}, u32[]{:S(2)}, u32[]{:S(2)}) collective-permute-start(bf16[1024,256]{1,0:T(8,128)(2,1)S(1)} %maximum_select_fusion.2), channel_id=1, source_target_pairs={{0,32},{16,48},{32,0},{48,16},{64,96},{80,112},{96,64},{112,80},{1... | collective-permute-start | bytes 1572872 | tf_op jit(solution)/shard_map/ppermute | solution.py:44
  107.2 33.8 %collective-permute-start.4 = (bf16[2048,256]{1,0:T(8,128)(2,1)S(1)}, bf16[2048,256]{1,0:T(8,128)(2,1)S(1)}, u32[]{:S(2)}, u32[]{:S(2)}) collective-permute-start(bf16[2048,256]{1,0:T(8,128)(2,1)S(1)} %maximum_select_fusion.1), channel_id=1, source_target_pairs={{0,16},{16,0},{32,48},{48,32},{64,80},{80,64},{96,112},{112,96},{1... | collective-permute-start | bytes 3145736 | tf_op jit(solution)/shard_map/ppermute | solution.py:44
  110.8 30.7 %copy-start.10 = (bf16[128,256]{1,0:T(8,128)(2,1)S(1)}, bf16[128,256]{1,0:T(8,128)(2,1)}, u32[]{:S(2)}) copy-start(bf16[128,256]{1,0:T(8,128)(2,1)} %param.13) | copy-start | bytes 196612
  145.3 21.1 %copy-start.3 = (s32[8,8]{1,0:T(8,128)S(1)}, s32[8,8]{1,0:T(8,128)}, u32[]{:S(2)}) copy-start(s32[8,8]{1,0:T(8,128)} %param.21) | copy-start | bytes 772
  146.8 64.1 %copy-start.2 = (bf16[8,4096]{1,0:T(8,128)(2,1)S(1)}, bf16[8,4096]{1,0:T(8,128)(2,1)}, u32[]{:S(2)}) copy-start(bf16[8,4096]{1,0:T(8,128)(2,1)} %param.12) | copy-start | bytes 196612
  146.8 64.3 %copy-start.4 = (f32[4096]{0:T(1024)S(1)}, f32[4096]{0:T(1024)}, u32[]{:S(2)}) copy-start(f32[4096]{0:T(1024)} %param.18) | copy-start | bytes 49156
  146.8 64.0 %all-to-all-start = ((bf16[16,8,4096]{2,1,0:T(8,128)(2,1)}), bf16[16,8,4096]{2,1,0:T(8,128)(2,1)S(1)}, u32[]{:S(2)}, u32[]{:S(2)}) async-start(bf16[16,8,4096]{2,1,0:T(8,128)(2,1)} %fusion), calls=%async_computation | async-start | bytes 2097152 | tf_op jit(solution)/shard_map/all_to_all | solution.py:136
  211.1 63.4 %copy-start.1 = (bf16[8,4096]{1,0:T(8,128)(2,1)}, bf16[8,4096]{1,0:T(8,128)(2,1)S(1)}, u32[]{:S(2)}) copy-start(bf16[8,4096]{1,0:T(8,128)(2,1)S(1)} %get-tuple-element.9) | copy-start | bytes 196612
  282.5 24.4 %copy-start.7 = (f32[8,8]{1,0:T(8,128)S(1)}, f32[8,8]{1,0:T(8,128)}, u32[]{:S(2)}) copy-start(f32[8,8]{1,0:T(8,128)} %param.22) | copy-start | bytes 772
  285.4 20.7 %all-to-all-start.2 = ((bf16[16,6,768]{2,1,0:T(8,128)(2,1)}), bf16[16,6,768]{2,1,0:T(8,128)(2,1)S(1)}, u32[]{:S(2)}, u32[]{:S(2)}) async-start(bf16[16,6,768]{2,1,0:T(8,128)(2,1)} %convert_element_type.76), calls=%async_computation.2 | async-start | bytes 393216 | tf_op jit(solution)/shard_map/all_to_all | solution.py:167
Sparse Core Ops, SparseCore 0:
  35.6 149.5 all-gather.1

commit v2 on v1

--- a/solution.py
+++ b/solution.py
@@ -73,8 +73,14 @@
 
     fe_dev = expert_gate.shape[2]
     w_local = jnp.concatenate([expert_gate[0].T, expert_up[0].T], axis=0)
-    w_all = lax.all_gather(w_local, "zh", axis=0, tiled=True)
-    w_all = lax.all_gather(w_all, ("x", "y"), axis=0, tiled=True)
+    zh_index = lax.axis_index("zh")
+    w_other = lax.ppermute(w_local, "zh", [(0, 1), (1, 0)])
+    w_pair = jnp.where(
+        zh_index == 0,
+        jnp.concatenate([w_local, w_other]),
+        jnp.concatenate([w_other, w_local]),
+    )
+    w_all = lax.all_gather(w_pair, ("x", "y"), axis=0, tiled=True)
 
     kv_head = exp_index * per_device // group
     own_keys = lax.dynamic_slice_in_dim(keys, kv_head * HD, HD, 1)
@@ -133,9 +139,13 @@
     tok_dev = residual.shape[0]
 
     share = jnp.dot(attn, out_proj, preferred_element_type=jnp.float32).astype(jnp.bfloat16)
-    shares = lax.all_to_all(
-        share.reshape(n_exp, tok_dev, D), EXP, split_axis=0, concat_axis=0, tiled=True
-    )
+    core_index = lax.axis_index("c")
+    by_core = jnp.transpose(share.reshape(n_exp // 2, 2, tok_dev, D), (1, 0, 2, 3))
+    keep = jnp.where(core_index == 0, by_core[0], by_core[1])
+    give = jnp.where(core_index == 0, by_core[1], by_core[0])
+    got = lax.ppermute(give, "c", [(0, 1), (1, 0)])
+    pair_sum = (keep.astype(jnp.float32) + got.astype(jnp.float32)).astype(jnp.bfloat16)
+    shares = lax.all_to_all(pair_sum, "zl", split_axis=0, concat_axis=0, tiled=True)
     head_total = jnp.sum(shares.astype(jnp.float32), axis=0)
     mixed = (residual.astype(jnp.float32) + head_total).astype(jnp.bfloat16)
     mixed_f = mixed.astype(jnp.float32)

time: 316 us -> 302 us (0.956)
  blocking collectives: 87.7 us -> 62.5 us
  starting transfers between devices: 54.6 us -> 78.8 us
  waiting for transfers between devices: 133 us -> 115 us
  other arithmetic: 6.11 us -> 9.39 us
    ppermute x0 -> x2, starting transfers between devices: none -> 28.8 us  [the longest x1 16.3 us: shards(): w_other = lax.ppermute(w_local, 'zh', [(0, 1), (1, 0)])]
    all_gather x1 -> x0, blocking collectives: 27 us -> none  [shards(): w_all = lax.all_gather(w_local, 'zh', axis=0, tiled=True)]
    all_to_all x1, waiting for transfers between devices: 43.8 us -> 20.6 us  [shards(): lax.all_to_all(pair_sum, 'zl', split_axis=0, concat_axis=0, tiled=True)]
    ppermute x0 -> x2, waiting for transfers between devices: none -> 13.5 us  [the longest x1 12 us: shards(): w_other = lax.ppermute(w_local, 'zh', [(0, 1), (1, 0)])]
    ppermute x5, waiting for transfers between devices: 74.3 us -> 66.7 us  [gather_by_doubling(): other = lax.ppermute(cur, CTX, [(i, i ^ bit) for i in range(n)])]
    all_to_all x1, starting transfers between devices: 19.6 us -> 15.7 us  [shards(): lax.all_to_all(pair_sum, 'zl', split_axis=0, concat_axis=0, tiled=True)]
  transfers between devices with their start and end apart: 8 -> 10, of which waited for: 7 -> 9; matrix products, arithmetic and copies ran while one was open for 4% -> 4% of each run, Pallas kernels for 0% -> 0%
where the time goes in v2:
time: 302 us; the launch traced here: 298 us
  waiting for transfers between devices  115 us (38%)
  starting transfers between devices  78.8 us (26%)
  blocking collectives  62.5 us (21%)
  between operations  14.5 us (5%)
  matrix products  11 us (4%)
  other arithmetic  9.39 us (3%)
  local copies, waits for them, and re-layouts  6.77 us (2%)
    ppermute x5, waiting for transfers between devices, gather_by_doubling(): other = lax.ppermute(cur, CTX, [(i, i ^ bit) for i in range(n)])  66.7 us
    all_to_all x1, blocking collectives, shards(): lax.all_to_all(outgoing, EXP, split_axis=0, concat_axis=0, tiled=True)  62.5 us
    ppermute x5, starting transfers between devices, gather_by_doubling(): other = lax.ppermute(cur, CTX, [(i, i ^ bit) for i in range(n)])  28.2 us
    all_to_all x1, waiting for transfers between devices, shards(): lax.all_to_all(pair_sum, 'zl', split_axis=0, concat_axis=0, tiled=True)  20.6 us
    ppermute x1, starting transfers between devices, shards(): w_other = lax.ppermute(w_local, 'zh', [(0, 1), (1, 0)])  16.3 us
    all_to_all x1, starting transfers between devices, shards(): lax.all_to_all(pair_sum, 'zl', split_axis=0, concat_axis=0, tiled=True)  15.7 us
    all_to_all x1, waiting for transfers between devices, shards(): lax.all_to_all(hidden.astype(jnp.bfloat16), EXP, split_axis=0, concat_axi...  14.6 us
    ppermute x1, starting transfers between devices, shards(): got = lax.ppermute(give, 'c', [(0, 1), (1, 0)])  12.5 us
  transfers between devices with their start and end apart: 10, of which 9 were waited for; matrix products, arithmetic and copies ran while one was open for 4% of the time, Pallas kernels for 0%

profile of v2, /device:TPU:1, one launch (start us, length us, event | category | flops | bytes accessed | tf_op | source)
XLA Modules:
  0.0 298.4 jit_solution(11673458810543237108)
XLA Ops:
  8.4 16.3 %collective-permute-start.6 = (bf16[48,4096]{1,0:T(8,128)(2,1)S(1)}, bf16[48,4096]{1,0:T(8,128)(2,1)S(1)}, u32[]{:S(2)}, u32[]{:S(2)}) collective-permute-start(bf16[48,4096]{1,0:T(8,128)(2,1)S(1)} %pad_maximum_fusion), channel_id=1, source_target_pairs={{0,256},{256,0},{1,257},{257,1},{2,258},{258,2},{3,259},{259,3},{4... | collective-permute-start | bytes 1179656 | tf_op jit(solution)/shard_map/ppermute | solution.py:77
  24.8 12.0 %collective-permute-done.6 = bf16[48,4096]{1,0:T(8,128)(2,1)S(1)} collective-permute-done((bf16[48,4096]{1,0:T(8,128)(2,1)S(1)}, bf16[48,4096]{1,0:T(8,128)(2,1)S(1)}, u32[]{:S(2)}, u32[]{:S(2)}) %collective-permute-start.6) | collective-permute-done | bytes 393248 | tf_op jit(solution)/shard_map/ppermute | solution.py:77
  36.8 2.3 maximum_select_fusion.2
  39.2 13.0 %collective-permute-start = (bf16[128,256]{1,0:T(8,128)(2,1)S(1)}, bf16[128,256]{1,0:T(8,128)(2,1)S(1)}, u32[]{:S(2)}, u32[]{:S(2)}) collective-permute-start(bf16[128,256]{1,0:T(8,128)(2,1)S(1)} %pad_maximum_fusion.1), channel_id=1, source_target_pairs={{0,256},{16,272},{32,288},{48,304},{64,320},{80,336},{96,352},{112... | collective-permute-start | bytes 196616 | tf_op jit(solution)/shard_map/ppermute | solution.py:44
  52.2 14.8 %collective-permute-done = bf16[128,256]{1,0:T(8,128)(2,1)S(1)} collective-permute-done((bf16[128,256]{1,0:T(8,128)(2,1)S(1)}, bf16[128,256]{1,0:T(8,128)(2,1)S(1)}, u32[]{:S(2)}, u32[]{:S(2)}) %collective-permute-start) | collective-permute-done | bytes 65568 | tf_op jit(solution)/shard_map/ppermute | solution.py:44
  67.1 4.7 %collective-permute-start.1 = (bf16[256,256]{1,0:T(8,128)(2,1)S(1)}, bf16[256,256]{1,0:T(8,128)(2,1)S(1)}, u32[]{:S(2)}, u32[]{:S(2)}) collective-permute-start(bf16[256,256]{1,0:T(8,128)(2,1)S(1)} %maximum_select_fusion.5), channel_id=1, source_target_pairs={{0,128},{16,144},{32,160},{48,176},{64,192},{80,208},{96,224},{112... | collective-permute-start | bytes 393224 | tf_op jit(solution)/shard_map/ppermute | solution.py:44
  71.7 3.2 %collective-permute-done.1 = bf16[256,256]{1,0:T(8,128)(2,1)S(1)} collective-permute-done((bf16[256,256]{1,0:T(8,128)(2,1)S(1)}, bf16[256,256]{1,0:T(8,128)(2,1)S(1)}, u32[]{:S(2)}, u32[]{:S(2)}) %collective-permute-start.1) | collective-permute-done | bytes 131104 | tf_op jit(solution)/shard_map/ppermute | solution.py:44
  75.0 3.1 %collective-permute-start.2 = (bf16[512,256]{1,0:T(8,128)(2,1)S(1)}, bf16[512,256]{1,0:T(8,128)(2,1)S(1)}, u32[]{:S(2)}, u32[]{:S(2)}) collective-permute-start(bf16[512,256]{1,0:T(8,128)(2,1)S(1)} %maximum_select_fusion.4), channel_id=1, source_target_pairs={{0,64},{16,80},{32,96},{48,112},{64,0},{80,16},{96,32},{112,48},{1... | collective-permute-start | bytes 786440 | tf_op jit(solution)/shard_map/ppermute | solution.py:44
  78.1 5.1 %collective-permute-done.2 = bf16[512,256]{1,0:T(8,128)(2,1)S(1)} collective-permute-done((bf16[512,256]{1,0:T(8,128)(2,1)S(1)}, bf16[512,256]{1,0:T(8,128)(2,1)S(1)}, u32[]{:S(2)}, u32[]{:S(2)}) %collective-permute-start.2) | collective-permute-done | bytes 262176 | tf_op jit(solution)/shard_map/ppermute | solution.py:44
  83.4 4.8 %collective-permute-start.3 = (bf16[1024,256]{1,0:T(8,128)(2,1)S(1)}, bf16[1024,256]{1,0:T(8,128)(2,1)S(1)}, u32[]{:S(2)}, u32[]{:S(2)}) collective-permute-start(bf16[1024,256]{1,0:T(8,128)(2,1)S(1)} %maximum_select_fusion.3), channel_id=1, source_target_pairs={{0,32},{16,48},{32,0},{48,16},{64,96},{80,112},{96,64},{112,80},{1... | collective-permute-start | bytes 1572872 | tf_op jit(solution)/shard_map/ppermute | solution.py:44
  88.5 18.3 %collective-permute-done.3 = bf16[1024,256]{1,0:T(8,128)(2,1)S(1)} collective-permute-done((bf16[1024,256]{1,0:T(8,128)(2,1)S(1)}, bf16[1024,256]{1,0:T(8,128)(2,1)S(1)}, u32[]{:S(2)}, u32[]{:S(2)}) %collective-permute-start.3) | collective-permute-done | bytes 524320 | tf_op jit(solution)/shard_map/ppermute | solution.py:44
  107.0 2.6 collective-permute-start.4
  110.8 25.3 %collective-permute-done.4 = bf16[2048,256]{1,0:T(8,128)(2,1)S(1)} collective-permute-done((bf16[2048,256]{1,0:T(8,128)(2,1)S(1)}, bf16[2048,256]{1,0:T(8,128)(2,1)S(1)}, u32[]{:S(2)}, u32[]{:S(2)}) %collective-permute-start.4) | collective-permute-done | bytes 1048608 | tf_op jit(solution)/shard_map/ppermute | solution.py:44
  141.0 12.5 %collective-permute-start.5 = (bf16[8,8,4096]{2,1,0:T(8,128)(2,1)S(1)}, bf16[8,8,4096]{2,1,0:T(8,128)(2,1)S(1)}, u32[]{:S(2)}, u32[]{:S(2)}) collective-permute-start(bf16[8,8,4096]{2,1,0:T(8,128)(2,1)S(1)} %fusion.28), channel_id=1, source_target_pairs={{0,1},{1,0},{2,3},{3,2},{4,5},{5,4},{6,7},{7,6},{8,9},{9,8},{10,11... | collective-permute-start | bytes 1572872 | tf_op jit(solution)/shard_map/ppermute | solution.py:146
  153.5 1.5 collective-permute-done.5
  156.0 15.7 %all-to-all-start = ((bf16[8,8,4096]{2,1,0:T(8,128)(2,1)}), bf16[8,8,4096]{2,1,0:T(8,128)(2,1)S(1)}, u32[]{:S(2)}, u32[]{:S(2)}) async-start(bf16[8,8,4096]{2,1,0:T(8,128)(2,1)} %fusion.13), calls=%async_computation | async-start | bytes 1048576 | tf_op jit(solution)/shard_map/all_to_all | solution.py:148
  172.4 20.6 %all-to-all-done = bf16[8,8,4096]{2,1,0:T(8,128)(2,1)S(1)} async-done(((bf16[8,8,4096]{2,1,0:T(8,128)(2,1)}), bf16[8,8,4096]{2,1,0:T(8,128)(2,1)S(1)}, u32[]{:S(2)}, u32[]{:S(2)}) %all-to-all-start) | async-done | bytes 524320 | tf_op jit(solution)/shard_map/all_to_all | solution.py:148
  194.6 1.4 reshape.367
  196.0 62.5 %all_to_all.15 = bf16[16,6,4096]{2,1,0:T(8,128)(2,1)} all-to-all(bf16[16,6,4096]{2,1,0:T(8,128)(2,1)S(1)} %reshape.367), channel_id=1, replica_groups=mesh['zh'=2,'x'=4,'y'=4,'zl'=8,'c'=2] {'zl','c'}, dimensions={0} | all-to-all | bytes 1572864 | tf_op jit(solution)/shard_map/all_to_all | solution.py:169
  258.4 1.4 reshape.390
  259.9 6.4 %fusion.22 = f32[96,16,2,2,24]{0,4,3,2,1:T(8,128)S(1)} fusion(bf16[16,2,2,24,4096]{4,3,2,1,0:T(8,128)(2,1)} %bitcast.316, bf16[96,4096,1,1,1]{1,0,2,3,4:T(8,128)(2,1)S(1)} %reshape.390), kind=kOutput, calls=%fused_computation.47 | convolution fusion | flops 1207959552 | bytes 13959168 | tf_op jit(solution)/shard_map/sd,fd->sf/dot_general | solution.py:172
  267.6 1.8 convert_element_type.92
  269.3 6.1 %all-to-all-start.2 = ((bf16[16,6,768]{2,1,0:T(8,128)(2,1)}), bf16[16,6,768]{2,1,0:T(8,128)(2,1)S(1)}, u32[]{:S(2)}, u32[]{:S(2)}) async-start(bf16[16,6,768]{2,1,0:T(8,128)(2,1)} %convert_element_type.92), calls=%async_computation.2 | async-start | bytes 393216 | tf_op jit(solution)/shard_map/all_to_all | solution.py:177
  275.5 14.6 %all-to-all-done.2 = bf16[16,6,768]{2,1,0:T(8,128)(2,1)S(1)} async-done(((bf16[16,6,768]{2,1,0:T(8,128)(2,1)}), bf16[16,6,768]{2,1,0:T(8,128)(2,1)S(1)}, u32[]{:S(2)}, u32[]{:S(2)}) %all-to-all-start.2) | async-done | bytes 147488 | tf_op jit(solution)/shard_map/all_to_all | solution.py:177
  (77 shorter events, 14.0 us)
Async XLA Ops:
  7.2 133.2 %copy-start = (bf16[256,4096]{1,0:T(8,128)(2,1)S(1)}, bf16[256,4096]{1,0:T(8,128)(2,1)}, u32[]{:S(2)}) copy-start(bf16[256,4096]{1,0:T(8,128)(2,1)} %param.17) | copy-start | bytes 6291460
  7.2 31.9 %copy-start.5 = (bf16[128,256]{1,0:T(8,128)(2,1)S(1)}, bf16[128,256]{1,0:T(8,128)(2,1)}, u32[]{:S(2)}) copy-start(bf16[128,256]{1,0:T(8,128)(2,1)} %param.15) | copy-start | bytes 196612
  7.2 31.9 %copy-start.6 = (bf16[128,256]{1,0:T(8,128)(2,1)S(1)}, bf16[128,256]{1,0:T(8,128)(2,1)}, u32[]{:S(2)}) copy-start(bf16[128,256]{1,0:T(8,128)(2,1)} %param.14) | copy-start | bytes 196612
  7.2 252.7 %all-gather.2.cloned.1.call-start = ((), (), s32[]{:S(2)}) async-start(), calls=%async_computation.3 | async-start | bytes 13369344 | tf_op jit(solution)/shard_map/all_gather | solution.py:83
  8.4 28.3 %collective-permute-start.6 = (bf16[48,4096]{1,0:T(8,128)(2,1)S(1)}, bf16[48,4096]{1,0:T(8,128)(2,1)S(1)}, u32[]{:S(2)}, u32[]{:S(2)}) collective-permute-start(bf16[48,4096]{1,0:T(8,128)(2,1)S(1)} %pad_maximum_fusion), channel_id=1, source_target_pairs={{0,256},{256,0},{1,257},{257,1},{2,258},{258,2},{3,259},{259,3},{4... | collective-permute-start | bytes 1179656 | tf_op jit(solution)/shard_map/ppermute | solution.py:77
  24.7 63.6 %copy-start.8 = (s32[64]{0:T(128)S(1)}, s32[64]{0:T(128)}, u32[]{:S(2)}) copy-start(s32[64]{0:T(128)} %param.16) | copy-start | bytes 772
  24.7 63.7 %copy-start.9 = (s32[32]{0:T(128)S(1)}, s32[32]{0:T(128)}, u32[]{:S(2)}) copy-start(s32[32]{0:T(128)} %constant.180) | copy-start | bytes 388
  39.2 27.8 %collective-permute-start = (bf16[128,256]{1,0:T(8,128)(2,1)S(1)}, bf16[128,256]{1,0:T(8,128)(2,1)S(1)}, u32[]{:S(2)}, u32[]{:S(2)}) collective-permute-start(bf16[128,256]{1,0:T(8,128)(2,1)S(1)} %pad_maximum_fusion.1), channel_id=1, source_target_pairs={{0,256},{16,272},{32,288},{48,304},{64,320},{80,336},{96,352},{112... | collective-permute-start | bytes 196616 | tf_op jit(solution)/shard_map/ppermute | solution.py:44
  67.1 7.8 %collective-permute-start.1 = (bf16[256,256]{1,0:T(8,128)(2,1)S(1)}, bf16[256,256]{1,0:T(8,128)(2,1)S(1)}, u32[]{:S(2)}, u32[]{:S(2)}) collective-permute-start(bf16[256,256]{1,0:T(8,128)(2,1)S(1)} %maximum_select_fusion.5), channel_id=1, source_target_pairs={{0,128},{16,144},{32,160},{48,176},{64,192},{80,208},{96,224},{112... | collective-permute-start | bytes 393224 | tf_op jit(solution)/shard_map/ppermute | solution.py:44
  75.0 8.2 %collective-permute-start.2 = (bf16[512,256]{1,0:T(8,128)(2,1)S(1)}, bf16[512,256]{1,0:T(8,128)(2,1)S(1)}, u32[]{:S(2)}, u32[]{:S(2)}) collective-permute-start(bf16[512,256]{1,0:T(8,128)(2,1)S(1)} %maximum_select_fusion.4), channel_id=1, source_target_pairs={{0,64},{16,80},{32,96},{48,112},{64,0},{80,16},{96,32},{112,48},{1... | collective-permute-start | bytes 786440 | tf_op jit(solution)/shard_map/ppermute | solution.py:44
  83.4 23.3 %collective-permute-start.3 = (bf16[1024,256]{1,0:T(8,128)(2,1)S(1)}, bf16[1024,256]{1,0:T(8,128)(2,1)S(1)}, u32[]{:S(2)}, u32[]{:S(2)}) collective-permute-start(bf16[1024,256]{1,0:T(8,128)(2,1)S(1)} %maximum_select_fusion.3), channel_id=1, source_target_pairs={{0,32},{16,48},{32,0},{48,16},{64,96},{80,112},{96,64},{112,80},{1... | collective-permute-start | bytes 1572872 | tf_op jit(solution)/shard_map/ppermute | solution.py:44
  107.0 29.1 %collective-permute-start.4 = (bf16[2048,256]{1,0:T(8,128)(2,1)S(1)}, bf16[2048,256]{1,0:T(8,128)(2,1)S(1)}, u32[]{:S(2)}, u32[]{:S(2)}) collective-permute-start(bf16[2048,256]{1,0:T(8,128)(2,1)S(1)} %maximum_select_fusion.1), channel_id=1, source_target_pairs={{0,16},{16,0},{32,48},{48,32},{64,80},{80,64},{96,112},{112,96},{1... | collective-permute-start | bytes 3145736 | tf_op jit(solution)/shard_map/ppermute | solution.py:44
  110.8 25.8 %copy-start.10 = (bf16[128,256]{1,0:T(8,128)(2,1)S(1)}, bf16[128,256]{1,0:T(8,128)(2,1)}, u32[]{:S(2)}) copy-start(bf16[128,256]{1,0:T(8,128)(2,1)} %param.13) | copy-start | bytes 196612
  140.9 30.9 %copy-start.3 = (s32[8,8]{1,0:T(8,128)S(1)}, s32[8,8]{1,0:T(8,128)}, u32[]{:S(2)}) copy-start(s32[8,8]{1,0:T(8,128)} %param.21) | copy-start | bytes 772
  140.9 52.1 %copy-start.2 = (bf16[8,4096]{1,0:T(8,128)(2,1)S(1)}, bf16[8,4096]{1,0:T(8,128)(2,1)}, u32[]{:S(2)}) copy-start(bf16[8,4096]{1,0:T(8,128)(2,1)} %param.12) | copy-start | bytes 196612
  141.0 52.3 %copy-start.4 = (f32[4096]{0:T(1024)S(1)}, f32[4096]{0:T(1024)}, u32[]{:S(2)}) copy-start(f32[4096]{0:T(1024)} %param.18) | copy-start | bytes 49156
  141.0 14.0 %collective-permute-start.5 = (bf16[8,8,4096]{2,1,0:T(8,128)(2,1)S(1)}, bf16[8,8,4096]{2,1,0:T(8,128)(2,1)S(1)}, u32[]{:S(2)}, u32[]{:S(2)}) collective-permute-start(bf16[8,8,4096]{2,1,0:T(8,128)(2,1)S(1)} %fusion.28), channel_id=1, source_target_pairs={{0,1},{1,0},{2,3},{3,2},{4,5},{5,4},{6,7},{7,6},{8,9},{9,8},{10,11... | collective-permute-start | bytes 1572872 | tf_op jit(solution)/shard_map/ppermute | solution.py:146
  156.0 37.0 %all-to-all-start = ((bf16[8,8,4096]{2,1,0:T(8,128)(2,1)}), bf16[8,8,4096]{2,1,0:T(8,128)(2,1)S(1)}, u32[]{:S(2)}, u32[]{:S(2)}) async-start(bf16[8,8,4096]{2,1,0:T(8,128)(2,1)} %fusion.13), calls=%async_computation | async-start | bytes 1048576 | tf_op jit(solution)/shard_map/all_to_all | solution.py:148
  193.2 65.2 %copy-start.1 = (bf16[8,4096]{1,0:T(8,128)(2,1)}, bf16[8,4096]{1,0:T(8,128)(2,1)S(1)}, u32[]{:S(2)}) copy-start(bf16[8,4096]{1,0:T(8,128)(2,1)S(1)} %get-tuple-element.9) | copy-start | bytes 196612
  266.4 24.4 %copy-start.7 = (f32[8,8]{1,0:T(8,128)S(1)}, f32[8,8]{1,0:T(8,128)}, u32[]{:S(2)}) copy-start(f32[8,8]{1,0:T(8,128)} %param.22) | copy-start | bytes 772
  269.3 20.7 %all-to-all-start.2 = ((bf16[16,6,768]{2,1,0:T(8,128)(2,1)}), bf16[16,6,768]{2,1,0:T(8,128)(2,1)S(1)}, u32[]{:S(2)}, u32[]{:S(2)}) async-start(bf16[16,6,768]{2,1,0:T(8,128)(2,1)} %convert_element_type.92), calls=%async_computation.2 | async-start | bytes 393216 | tf_op jit(solution)/shard_map/all_to_all | solution.py:177
Sparse Core Ops, SparseCore 0:
  39.2 145.8 all-gather.1

commit v3 on v2

--- a/solution.py
+++ b/solution.py
@@ -74,7 +74,20 @@
     fe_dev = expert_gate.shape[2]
     w_local = jnp.concatenate([expert_gate[0].T, expert_up[0].T], axis=0)
     zh_index = lax.axis_index("zh")
-    w_other = lax.ppermute(w_local, "zh", [(0, 1), (1, 0)])
+    core_index = lax.axis_index("c")
+
+    kv_head = exp_index * per_device // group
+    own_keys = lax.dynamic_slice_in_dim(keys, kv_head * HD, HD, 1)
+    own_values = lax.dynamic_slice_in_dim(values, kv_head * HD, HD, 1)
+    kv_local = jnp.where(core_index == 0, own_keys, own_values)
+
+    bits = doubling_bits(n_ctx)
+    first = bits[0]
+    n_w = w_local.size
+    joint = jnp.concatenate([w_local.reshape(-1), kv_local.reshape(-1)])
+    joint = lax.ppermute(joint, CTX, [(i, i ^ first) for i in range(n_ctx)])
+    w_other = joint[:n_w].reshape(w_local.shape)
+    kv_other = joint[n_w:].reshape(kv_local.shape)
     w_pair = jnp.where(
         zh_index == 0,
         jnp.concatenate([w_local, w_other]),
@@ -82,13 +95,19 @@
     )
     w_all = lax.all_gather(w_pair, ("x", "y"), axis=0, tiled=True)
 
-    kv_head = exp_index * per_device // group
-    own_keys = lax.dynamic_slice_in_dim(keys, kv_head * HD, HD, 1)
-    own_values = lax.dynamic_slice_in_dim(values, kv_head * HD, HD, 1)
-    kv_local = jnp.concatenate([own_keys, own_values], axis=1)
-    kv_all, order = gather_by_doubling(kv_local, n_ctx)
-    key_piece = kv_all[:, :HD]
-    value_piece = kv_all[:, HD:]
+    low = (ctx_index & first) == 0
+    cur = jnp.where(
+        low, jnp.concatenate([kv_local, kv_other]), jnp.concatenate([kv_other, kv_local])
+    )
+    order = [0, first]
+    for bit in bits[1:]:
+        other = lax.ppermute(cur, CTX, [(i, i ^ bit) for i in range(n_ctx)])
+        low = (ctx_index & bit) == 0
+        cur = jnp.where(low, jnp.concatenate([cur, other]), jnp.concatenate([other, cur]))
+        order = order + [o + bit for o in order]
+    partner = lax.ppermute(cur, "c", [(0, 1), (1, 0)])
+    key_piece = jnp.where(core_index == 0, cur, partner)
+    value_piece = jnp.where(core_index == 0, partner, cur)
     length = key_piece.shape[0]
     block_ctx = jnp.asarray(np.array(order, np.int32))
     key_rows_all = (
@@ -139,7 +158,6 @@
     tok_dev = residual.shape[0]
 
     share = jnp.dot(attn, out_proj, preferred_element_type=jnp.float32).astype(jnp.bfloat16)
-    core_index = lax.axis_index("c")
     by_core = jnp.transpose(share.reshape(n_exp // 2, 2, tok_dev, D), (1, 0, 2, 3))
     keep = jnp.where(core_index == 0, by_core[0], by_core[1])
     give = jnp.where(core_index == 0, by_core[1], by_core[0])

time: 302 us -> 265 us (0.88)
  waiting for transfers between devices: 115 us -> 65.9 us
  starting transfers between devices: 78.8 us -> 92.1 us
    ppermute x6, waiting for transfers between devices: 78.7 us -> 29.2 us  [the longest x4 15 us: shards(): other = lax.ppermute(cur, CTX, [(i, i ^ bit) for i in range(n_ctx)])]
    all_to_all x1, starting transfers between devices: 15.7 us -> 42.4 us  [shards(): lax.all_to_all(pair_sum, 'zl', split_axis=0, concat_axis=0, tiled=True)]
    ppermute x1, starting transfers between devices: 12.5 us -> 2.43 us  [shards(): got = lax.ppermute(give, 'c', [(0, 1), (1, 0)])]
    ppermute x6, starting transfers between devices: 44.5 us -> 41.2 us  [the longest x4 17.3 us: shards(): other = lax.ppermute(cur, CTX, [(i, i ^ bit) for i in range(n_ctx)])]
  transfers between devices with their start and end apart: 10 -> 10, of which waited for: 9 -> 9; matrix products, arithmetic and copies ran while one was open for 4% -> 5% of each run, Pallas kernels for 0% -> 0%
where the time goes in v3:
time: 265 us; the launch traced here: 264 us
  starting transfers between devices  92.1 us (35%)
  waiting for transfers between devices  65.9 us (25%)
  blocking collectives  62.4 us (24%)
  between operations  14.6 us (6%)
  matrix products  11 us (4%)
  other arithmetic  9.3 us (4%)
  local copies, waits for them, and re-layouts  8.79 us (3%)
    all_to_all x1, blocking collectives, shards(): lax.all_to_all(outgoing, EXP, split_axis=0, concat_axis=0, tiled=True)  62.4 us
    all_to_all x1, starting transfers between devices, shards(): lax.all_to_all(pair_sum, 'zl', split_axis=0, concat_axis=0, tiled=True)  42.4 us
    all_to_all x1, waiting for transfers between devices, shards(): lax.all_to_all(pair_sum, 'zl', split_axis=0, concat_axis=0, tiled=True)  20.6 us
    ppermute x4, starting transfers between devices, shards(): other = lax.ppermute(cur, CTX, [(i, i ^ bit) for i in range(n_ctx)])  17.3 us
    ppermute x1, starting transfers between devices, shards(): joint = lax.ppermute(joint, CTX, [(i, i ^ first) for i in range(n_ctx)])  16.3 us
    ppermute x4, waiting for transfers between devices, shards(): other = lax.ppermute(cur, CTX, [(i, i ^ bit) for i in range(n_ctx)])  15 us
    all_to_all x1, waiting for transfers between devices, shards(): lax.all_to_all(hidden.astype(jnp.bfloat16), EXP, split_axis=0, concat_axi...  14.6 us
    ppermute x1, waiting for transfers between devices, shards(): joint = lax.ppermute(joint, CTX, [(i, i ^ first) for i in range(n_ctx)])  13.1 us
  transfers between devices with their start and end apart: 10, of which 9 were waited for; matrix products, arithmetic and copies ran while one was open for 5% of the time, Pallas kernels for 0%

profile of v3, /device:TPU:1, one launch (start us, length us, event | category | flops | bytes accessed | tf_op | source)
XLA Modules:
  0.0 264.1 jit_solution(16931087806240228455)
XLA Ops:
  7.3 1.2 maximum_bitcast_fusion
  10.1 16.3 %collective-permute-start = (bf16[212992]{0:T(1024)(128)(2,1)}, bf16[212992]{0:T(1024)(128)(2,1)}, u32[]{:S(2)}, u32[]{:S(2)}) collective-permute-start(bf16[212992]{0:T(1024)(128)(2,1)} %pad_maximum_fusion), channel_id=1, source_target_pairs={{0,256},{16,272},{32,288},{48,304},{64,320},{80,336},{96,352},{112... | collective-permute-start | bytes 1277960 | tf_op jit(solution)/shard_map/ppermute | solution.py:88
  26.4 13.1 %collective-permute-done = bf16[212992]{0:T(1024)(128)(2,1)} collective-permute-done((bf16[212992]{0:T(1024)(128)(2,1)}, bf16[212992]{0:T(1024)(128)(2,1)}, u32[]{:S(2)}, u32[]{:S(2)}) %collective-permute-start) | collective-permute-done | bytes 426016 | tf_op jit(solution)/shard_map/ppermute | solution.py:88
  42.6 5.7 %collective-permute-start.1 = (bf16[256,128]{1,0:T(8,128)(2,1)S(1)}, bf16[256,128]{1,0:T(8,128)(2,1)S(1)}, u32[]{:S(2)}, u32[]{:S(2)}) collective-permute-start(bf16[256,128]{1,0:T(8,128)(2,1)S(1)} %maximum_select_fusion.5), channel_id=1, source_target_pairs={{0,128},{16,144},{32,160},{48,176},{64,192},{80,208},{96,224},{112... | collective-permute-start | bytes 196616 | tf_op jit(solution)/shard_map/ppermute | solution.py:104
  48.3 1.6 collective-permute-done.1
  49.9 3.3 %collective-permute-start.2 = (bf16[512,128]{1,0:T(8,128)(2,1)S(1)}, bf16[512,128]{1,0:T(8,128)(2,1)S(1)}, u32[]{:S(2)}, u32[]{:S(2)}) collective-permute-start(bf16[512,128]{1,0:T(8,128)(2,1)S(1)} %maximum_select_fusion.4), channel_id=1, source_target_pairs={{0,64},{16,80},{32,96},{48,112},{64,0},{80,16},{96,32},{112,48},{1... | collective-permute-start | bytes 393224 | tf_op jit(solution)/shard_map/ppermute | solution.py:104
  53.3 2.4 collective-permute-done.2
  55.7 5.0 %collective-permute-start.3 = (bf16[1024,128]{1,0:T(8,128)(2,1)S(1)}, bf16[1024,128]{1,0:T(8,128)(2,1)S(1)}, u32[]{:S(2)}, u32[]{:S(2)}) collective-permute-start(bf16[1024,128]{1,0:T(8,128)(2,1)S(1)} %maximum_select_fusion.3), channel_id=1, source_target_pairs={{0,32},{16,48},{32,0},{48,16},{64,96},{80,112},{96,64},{112,80},{1... | collective-permute-start | bytes 786440 | tf_op jit(solution)/shard_map/ppermute | solution.py:104
  60.8 3.7 %collective-permute-done.3 = bf16[1024,128]{1,0:T(8,128)(2,1)S(1)} collective-permute-done((bf16[1024,128]{1,0:T(8,128)(2,1)S(1)}, bf16[1024,128]{1,0:T(8,128)(2,1)S(1)}, u32[]{:S(2)}, u32[]{:S(2)}) %collective-permute-start.3) | collective-permute-done | bytes 262176 | tf_op jit(solution)/shard_map/ppermute | solution.py:104
  64.7 3.2 %collective-permute-start.4 = (bf16[2048,128]{1,0:T(8,128)(2,1)S(1)}, bf16[2048,128]{1,0:T(8,128)(2,1)S(1)}, u32[]{:S(2)}, u32[]{:S(2)}) collective-permute-start(bf16[2048,128]{1,0:T(8,128)(2,1)S(1)} %maximum_select_fusion.2), channel_id=1, source_target_pairs={{0,16},{16,0},{32,48},{48,32},{64,80},{80,64},{96,112},{112,96},{1... | collective-permute-start | bytes 1572872 | tf_op jit(solution)/shard_map/ppermute | solution.py:104
  68.1 7.3 %collective-permute-done.4 = bf16[2048,128]{1,0:T(8,128)(2,1)S(1)} collective-permute-done((bf16[2048,128]{1,0:T(8,128)(2,1)S(1)}, bf16[2048,128]{1,0:T(8,128)(2,1)S(1)}, u32[]{:S(2)}, u32[]{:S(2)}) %collective-permute-start.4) | collective-permute-done | bytes 524320 | tf_op jit(solution)/shard_map/ppermute | solution.py:104
  75.7 7.6 %collective-permute-start.5 = (bf16[4096,128]{1,0:T(8,128)(2,1)S(1)}, bf16[4096,128]{1,0:T(8,128)(2,1)S(1)}, u32[]{:S(2)}, u32[]{:S(2)}) collective-permute-start(bf16[4096,128]{1,0:T(8,128)(2,1)S(1)} %maximum_select_fusion), channel_id=1, source_target_pairs={{0,1},{1,0},{2,3},{3,2},{4,5},{5,4},{6,7},{7,6},{8,9},{9,8},{10,11... | collective-permute-start | bytes 3145736 | tf_op jit(solution)/shard_map/ppermute | solution.py:108
  90.1 2.4 collective-permute-start.6
  92.5 1.5 collective-permute-done.6
  95.1 42.4 %all-to-all-start = ((bf16[8,8,4096]{2,1,0:T(8,128)(2,1)}), bf16[8,8,4096]{2,1,0:T(8,128)(2,1)S(1)}, u32[]{:S(2)}, u32[]{:S(2)}) async-start(bf16[8,8,4096]{2,1,0:T(8,128)(2,1)} %fusion.13), calls=%async_computation | async-start | bytes 1048576 | tf_op jit(solution)/shard_map/all_to_all | solution.py:166
  138.1 20.6 %all-to-all-done = bf16[8,8,4096]{2,1,0:T(8,128)(2,1)S(1)} async-done(((bf16[8,8,4096]{2,1,0:T(8,128)(2,1)}), bf16[8,8,4096]{2,1,0:T(8,128)(2,1)S(1)}, u32[]{:S(2)}, u32[]{:S(2)}) %all-to-all-start) | async-done | bytes 524320 | tf_op jit(solution)/shard_map/all_to_all | solution.py:166
  159.0 1.3 convolution_convert_fusion.1
  160.3 1.4 reshape.393
  161.7 62.4 %all_to_all.15 = bf16[16,6,4096]{2,1,0:T(8,128)(2,1)} all-to-all(bf16[16,6,4096]{2,1,0:T(8,128)(2,1)S(1)} %reshape.393), channel_id=1, replica_groups=mesh['zh'=2,'x'=4,'y'=4,'zl'=8,'c'=2] {'zl','c'}, dimensions={0} | all-to-all | bytes 1572864 | tf_op jit(solution)/shard_map/all_to_all | solution.py:187
  224.1 1.4 reshape.416
  225.6 6.4 %fusion.22 = f32[96,16,2,2,24]{0,4,3,2,1:T(8,128)S(1)} fusion(bf16[16,2,2,24,4096]{4,3,2,1,0:T(8,128)(2,1)} %bitcast.322, bf16[96,4096,1,1,1]{1,0,2,3,4:T(8,128)(2,1)S(1)} %reshape.416), kind=kOutput, calls=%fused_computation.48 | convolution fusion | flops 1207959552 | bytes 13959168 | tf_op jit(solution)/shard_map/sd,fd->sf/dot_general | solution.py:190
  233.3 1.8 convert_element_type.92
  235.1 6.1 %all-to-all-start.2 = ((bf16[16,6,768]{2,1,0:T(8,128)(2,1)}), bf16[16,6,768]{2,1,0:T(8,128)(2,1)S(1)}, u32[]{:S(2)}, u32[]{:S(2)}) async-start(bf16[16,6,768]{2,1,0:T(8,128)(2,1)} %convert_element_type.92), calls=%async_computation.2 | async-start | bytes 393216 | tf_op jit(solution)/shard_map/all_to_all | solution.py:195
  241.2 14.6 %all-to-all-done.2 = bf16[16,6,768]{2,1,0:T(8,128)(2,1)S(1)} async-done(((bf16[16,6,768]{2,1,0:T(8,128)(2,1)}), bf16[16,6,768]{2,1,0:T(8,128)(2,1)S(1)}, u32[]{:S(2)}, u32[]{:S(2)}) %all-to-all-start.2) | async-done | bytes 147488 | tf_op jit(solution)/shard_map/all_to_all | solution.py:195
  (81 shorter events, 16.7 us)
Async XLA Ops:
  7.2 82.3 %copy-start = (bf16[256,4096]{1,0:T(8,128)(2,1)S(1)}, bf16[256,4096]{1,0:T(8,128)(2,1)}, u32[]{:S(2)}) copy-start(bf16[256,4096]{1,0:T(8,128)(2,1)} %param.17) | copy-start | bytes 6291460
  7.2 33.5 %copy-start.2 = (bf16[1,4096,24]{1,2,0:T(8,128)(2,1)S(1)}, bf16[1,4096,24]{1,2,0:T(8,128)(2,1)}, u32[]{:S(2)}) copy-start(bf16[1,4096,24]{1,2,0:T(8,128)(2,1)} %param.19) | copy-start | bytes 589828
  7.2 33.5 %copy-start.1 = (bf16[1,4096,24]{1,2,0:T(8,128)(2,1)S(1)}, bf16[1,4096,24]{1,2,0:T(8,128)(2,1)}, u32[]{:S(2)}) copy-start(bf16[1,4096,24]{1,2,0:T(8,128)(2,1)} %param.20) | copy-start | bytes 589828
  7.2 218.4 %all-gather.2.cloned.1.call-start = ((), (), s32[]{:S(2)}) async-start(), calls=%async_computation.3 | async-start | bytes 13369344 | tf_op jit(solution)/shard_map/all_gather | solution.py:96
  10.1 29.3 %collective-permute-start = (bf16[212992]{0:T(1024)(128)(2,1)}, bf16[212992]{0:T(1024)(128)(2,1)}, u32[]{:S(2)}, u32[]{:S(2)}) collective-permute-start(bf16[212992]{0:T(1024)(128)(2,1)} %pad_maximum_fusion), channel_id=1, source_target_pairs={{0,256},{16,272},{32,288},{48,304},{64,320},{80,336},{96,352},{112... | collective-permute-start | bytes 1277960 | tf_op jit(solution)/shard_map/ppermute | solution.py:88
  40.7 27.3 %copy-start.8 = (s32[64]{0:T(128)S(1)}, s32[64]{0:T(128)}, u32[]{:S(2)}) copy-start(s32[64]{0:T(128)} %param.16) | copy-start | bytes 772
  40.7 27.3 %copy-start.9 = (s32[32]{0:T(128)S(1)}, s32[32]{0:T(128)}, u32[]{:S(2)}) copy-start(s32[32]{0:T(128)} %constant.180) | copy-start | bytes 388
  42.6 7.3 %collective-permute-start.1 = (bf16[256,128]{1,0:T(8,128)(2,1)S(1)}, bf16[256,128]{1,0:T(8,128)(2,1)S(1)}, u32[]{:S(2)}, u32[]{:S(2)}) collective-permute-start(bf16[256,128]{1,0:T(8,128)(2,1)S(1)} %maximum_select_fusion.5), channel_id=1, source_target_pairs={{0,128},{16,144},{32,160},{48,176},{64,192},{80,208},{96,224},{112... | collective-permute-start | bytes 196616 | tf_op jit(solution)/shard_map/ppermute | solution.py:104
  49.9 5.7 %collective-permute-start.2 = (bf16[512,128]{1,0:T(8,128)(2,1)S(1)}, bf16[512,128]{1,0:T(8,128)(2,1)S(1)}, u32[]{:S(2)}, u32[]{:S(2)}) collective-permute-start(bf16[512,128]{1,0:T(8,128)(2,1)S(1)} %maximum_select_fusion.4), channel_id=1, source_target_pairs={{0,64},{16,80},{32,96},{48,112},{64,0},{80,16},{96,32},{112,48},{1... | collective-permute-start | bytes 393224 | tf_op jit(solution)/shard_map/ppermute | solution.py:104
  55.7 8.8 %collective-permute-start.3 = (bf16[1024,128]{1,0:T(8,128)(2,1)S(1)}, bf16[1024,128]{1,0:T(8,128)(2,1)S(1)}, u32[]{:S(2)}, u32[]{:S(2)}) collective-permute-start(bf16[1024,128]{1,0:T(8,128)(2,1)S(1)} %maximum_select_fusion.3), channel_id=1, source_target_pairs={{0,32},{16,48},{32,0},{48,16},{64,96},{80,112},{96,64},{112,80},{1... | collective-permute-start | bytes 786440 | tf_op jit(solution)/shard_map/ppermute | solution.py:104
  64.7 10.7 %collective-permute-start.4 = (bf16[2048,128]{1,0:T(8,128)(2,1)S(1)}, bf16[2048,128]{1,0:T(8,128)(2,1)S(1)}, u32[]{:S(2)}, u32[]{:S(2)}) collective-permute-start(bf16[2048,128]{1,0:T(8,128)(2,1)S(1)} %maximum_select_fusion.2), channel_id=1, source_target_pairs={{0,16},{16,0},{32,48},{48,32},{64,80},{80,64},{96,112},{112,96},{1... | collective-permute-start | bytes 1572872 | tf_op jit(solution)/shard_map/ppermute | solution.py:104
  75.7 9.9 %collective-permute-start.5 = (bf16[4096,128]{1,0:T(8,128)(2,1)S(1)}, bf16[4096,128]{1,0:T(8,128)(2,1)S(1)}, u32[]{:S(2)}, u32[]{:S(2)}) collective-permute-start(bf16[4096,128]{1,0:T(8,128)(2,1)S(1)} %maximum_select_fusion), channel_id=1, source_target_pairs={{0,1},{1,0},{2,3},{3,2},{4,5},{5,4},{6,7},{7,6},{8,9},{9,8},{10,11... | collective-permute-start | bytes 3145736 | tf_op jit(solution)/shard_map/ppermute | solution.py:108
  84.4 1.3 copy-start.10
  90.0 47.5 %copy-start.5 = (s32[8,8]{1,0:T(8,128)S(1)}, s32[8,8]{1,0:T(8,128)}, u32[]{:S(2)}) copy-start(s32[8,8]{1,0:T(8,128)} %param.21) | copy-start | bytes 772
  90.1 68.7 %copy-start.4 = (bf16[8,4096]{1,0:T(8,128)(2,1)S(1)}, bf16[8,4096]{1,0:T(8,128)(2,1)}, u32[]{:S(2)}) copy-start(bf16[8,4096]{1,0:T(8,128)(2,1)} %param.12) | copy-start | bytes 196612
  90.1 68.9 %copy-start.6 = (f32[4096]{0:T(1024)S(1)}, f32[4096]{0:T(1024)}, u32[]{:S(2)}) copy-start(f32[4096]{0:T(1024)} %param.18) | copy-start | bytes 49156
  90.1 4.0 %collective-permute-start.6 = (bf16[8,8,4096]{2,1,0:T(8,128)(2,1)S(1)}, bf16[8,8,4096]{2,1,0:T(8,128)(2,1)S(1)}, u32[]{:S(2)}, u32[]{:S(2)}) collective-permute-start(bf16[8,8,4096]{2,1,0:T(8,128)(2,1)S(1)} %fusion.28), channel_id=1, source_target_pairs={{0,1},{1,0},{2,3},{3,2},{4,5},{5,4},{6,7},{7,6},{8,9},{9,8},{10,11... | collective-permute-start | bytes 1572872 | tf_op jit(solution)/shard_map/ppermute | solution.py:164
  95.1 63.6 %all-to-all-start = ((bf16[8,8,4096]{2,1,0:T(8,128)(2,1)}), bf16[8,8,4096]{2,1,0:T(8,128)(2,1)S(1)}, u32[]{:S(2)}, u32[]{:S(2)}) async-start(bf16[8,8,4096]{2,1,0:T(8,128)(2,1)} %fusion.13), calls=%async_computation | async-start | bytes 1048576 | tf_op jit(solution)/shard_map/all_to_all | solution.py:166
  158.9 65.2 %copy-start.3 = (bf16[8,4096]{1,0:T(8,128)(2,1)}, bf16[8,4096]{1,0:T(8,128)(2,1)S(1)}, u32[]{:S(2)}) copy-start(bf16[8,4096]{1,0:T(8,128)(2,1)S(1)} %get-tuple-element.9) | copy-start | bytes 196612
  232.2 24.4 %copy-start.7 = (f32[8,8]{1,0:T(8,128)S(1)}, f32[8,8]{1,0:T(8,128)}, u32[]{:S(2)}) copy-start(f32[8,8]{1,0:T(8,128)} %param.22) | copy-start | bytes 772
  235.1 20.7 %all-to-all-start.2 = ((bf16[16,6,768]{2,1,0:T(8,128)(2,1)}), bf16[16,6,768]{2,1,0:T(8,128)(2,1)S(1)}, u32[]{:S(2)}, u32[]{:S(2)}) async-start(bf16[16,6,768]{2,1,0:T(8,128)(2,1)} %convert_element_type.92), calls=%async_computation.2 | async-start | bytes 393216 | tf_op jit(solution)/shard_map/all_to_all | solution.py:195
Sparse Core Ops, SparseCore 0:
  41.9 138.5 all-gather.1

commit v4 on v3

--- a/solution.py
+++ b/solution.py
@@ -93,7 +93,6 @@
         jnp.concatenate([w_local, w_other]),
         jnp.concatenate([w_other, w_local]),
     )
-    w_all = lax.all_gather(w_pair, ("x", "y"), axis=0, tiled=True)
 
     low = (ctx_index & first) == 0
     cur = jnp.where(
@@ -108,6 +107,8 @@
     partner = lax.ppermute(cur, "c", [(0, 1), (1, 0)])
     key_piece = jnp.where(core_index == 0, cur, partner)
     value_piece = jnp.where(core_index == 0, partner, cur)
+    w_pair, key_piece, value_piece = lax.optimization_barrier((w_pair, key_piece, value_piece))
+    w_all = lax.all_gather(w_pair, ("x", "y"), axis=0, tiled=True)
     length = key_piece.shape[0]
     block_ctx = jnp.asarray(np.array(order, np.int32))
     key_rows_all = (

time: 265 us -> 259 us (0.977)
  starting transfers between devices: 92.1 us -> 82.2 us
  other arithmetic: 9.3 us -> 14.1 us
    all_to_all x1, starting transfers between devices: 42.4 us -> 30.4 us  [shards(): lax.all_to_all(pair_sum, 'zl', split_axis=0, concat_axis=0, tiled=True)]
  transfers between devices with their start and end apart: 10 -> 10, of which waited for: 9 -> 8; matrix products, arithmetic and copies ran while one was open for 5% -> 6% of each run, Pallas kernels for 0% -> 0%
where the time goes in v4:
time: 259 us; the launch traced here: 258 us
  starting transfers between devices  82.2 us (32%)
  waiting for transfers between devices  65.3 us (25%)
  blocking collectives  62.2 us (24%)
  between operations  14.5 us (6%)
  other arithmetic  14.1 us (5%)
  matrix products  12 us (5%)
  local copies, waits for them, and re-layouts  8.06 us (3%)
    all_to_all x1, blocking collectives, shards(): lax.all_to_all(outgoing, EXP, split_axis=0, concat_axis=0, tiled=True)  62.2 us
    all_to_all x1, starting transfers between devices, shards(): lax.all_to_all(pair_sum, 'zl', split_axis=0, concat_axis=0, tiled=True)  30.4 us
    all_to_all x1, waiting for transfers between devices, shards(): lax.all_to_all(pair_sum, 'zl', split_axis=0, concat_axis=0, tiled=True)  20.8 us
    ppermute x4, starting transfers between devices, shards(): other = lax.ppermute(cur, CTX, [(i, i ^ bit) for i in range(n_ctx)])  17.3 us
    ppermute x1, starting transfers between devices, shards(): joint = lax.ppermute(joint, CTX, [(i, i ^ first) for i in range(n_ctx)])  16.3 us
    ppermute x4, waiting for transfers between devices, shards(): other = lax.ppermute(cur, CTX, [(i, i ^ bit) for i in range(n_ctx)])  15.3 us
    all_to_all x1, waiting for transfers between devices, shards(): lax.all_to_all(hidden.astype(jnp.bfloat16), EXP, split_axis=0, concat_axi...  14.6 us
    ppermute x1, waiting for transfers between devices, shards(): joint = lax.ppermute(joint, CTX, [(i, i ^ first) for i in range(n_ctx)])  12.7 us
  transfers between devices with their start and end apart: 10, of which 8 were waited for; matrix products, arithmetic and copies ran while one was open for 6% of the time, Pallas kernels for 0%

profile of v4, /device:TPU:1, one launch (start us, length us, event | category | flops | bytes accessed | tf_op | source)
XLA Modules:
  0.0 258.4 jit_solution(16790787754023791733)
XLA Ops:
  9.3 16.3 %collective-permute-start = (bf16[212992]{0:T(1024)(128)(2,1)S(1)}, bf16[212992]{0:T(1024)(128)(2,1)S(1)}, u32[]{:S(2)}, u32[]{:S(2)}) collective-permute-start(bf16[212992]{0:T(1024)(128)(2,1)S(1)} %pad_maximum_fusion), channel_id=1, source_target_pairs={{0,256},{16,272},{32,288},{48,304},{64,320},{80,336},{96,352},{112... | collective-permute-start | bytes 1277960 | tf_op jit(solution)/shard_map/ppermute | solution.py:88
  25.6 12.7 %collective-permute-done = bf16[212992]{0:T(1024)(128)(2,1)S(1)} collective-permute-done((bf16[212992]{0:T(1024)(128)(2,1)S(1)}, bf16[212992]{0:T(1024)(128)(2,1)S(1)}, u32[]{:S(2)}, u32[]{:S(2)}) %collective-permute-start) | collective-permute-done | bytes 426016 | tf_op jit(solution)/shard_map/ppermute | solution.py:88
  38.4 5.7 %collective-permute-start.1 = (bf16[256,128]{1,0:T(8,128)(2,1)S(1)}, bf16[256,128]{1,0:T(8,128)(2,1)S(1)}, u32[]{:S(2)}, u32[]{:S(2)}) collective-permute-start(bf16[256,128]{1,0:T(8,128)(2,1)S(1)} %maximum_select_fusion.5), channel_id=1, source_target_pairs={{0,128},{16,144},{32,160},{48,176},{64,192},{80,208},{96,224},{112... | collective-permute-start | bytes 196616 | tf_op jit(solution)/shard_map/ppermute | solution.py:103
  44.1 1.6 collective-permute-done.1
  45.8 3.3 %collective-permute-start.2 = (bf16[512,128]{1,0:T(8,128)(2,1)S(1)}, bf16[512,128]{1,0:T(8,128)(2,1)S(1)}, u32[]{:S(2)}, u32[]{:S(2)}) collective-permute-start(bf16[512,128]{1,0:T(8,128)(2,1)S(1)} %maximum_select_fusion.4), channel_id=1, source_target_pairs={{0,64},{16,80},{32,96},{48,112},{64,0},{80,16},{96,32},{112,48},{1... | collective-permute-start | bytes 393224 | tf_op jit(solution)/shard_map/ppermute | solution.py:103
  49.1 2.4 collective-permute-done.2
  51.6 5.0 %collective-permute-start.3 = (bf16[1024,128]{1,0:T(8,128)(2,1)S(1)}, bf16[1024,128]{1,0:T(8,128)(2,1)S(1)}, u32[]{:S(2)}, u32[]{:S(2)}) collective-permute-start(bf16[1024,128]{1,0:T(8,128)(2,1)S(1)} %maximum_select_fusion.3), channel_id=1, source_target_pairs={{0,32},{16,48},{32,0},{48,16},{64,96},{80,112},{96,64},{112,80},{1... | collective-permute-start | bytes 786440 | tf_op jit(solution)/shard_map/ppermute | solution.py:103
  56.6 3.7 %collective-permute-done.3 = bf16[1024,128]{1,0:T(8,128)(2,1)S(1)} collective-permute-done((bf16[1024,128]{1,0:T(8,128)(2,1)S(1)}, bf16[1024,128]{1,0:T(8,128)(2,1)S(1)}, u32[]{:S(2)}, u32[]{:S(2)}) %collective-permute-start.3) | collective-permute-done | bytes 262176 | tf_op jit(solution)/shard_map/ppermute | solution.py:103
  60.5 3.2 %collective-permute-start.4 = (bf16[2048,128]{1,0:T(8,128)(2,1)S(1)}, bf16[2048,128]{1,0:T(8,128)(2,1)}, u32[]{:S(2)}, u32[]{:S(2)}) collective-permute-start(bf16[2048,128]{1,0:T(8,128)(2,1)S(1)} %maximum_select_fusion.2), channel_id=1, source_target_pairs={{0,16},{16,0},{32,48},{48,32},{64,80},{80,64},{96,112},{112,96},{1... | collective-permute-start | bytes 1572872 | tf_op jit(solution)/shard_map/ppermute | solution.py:103
  63.8 7.5 %collective-permute-done.4 = bf16[2048,128]{1,0:T(8,128)(2,1)} collective-permute-done((bf16[2048,128]{1,0:T(8,128)(2,1)S(1)}, bf16[2048,128]{1,0:T(8,128)(2,1)}, u32[]{:S(2)}, u32[]{:S(2)}) %collective-permute-start.4) | collective-permute-done | bytes 524320 | tf_op jit(solution)/shard_map/ppermute | solution.py:103
  71.3 1.8 maximum_select_fusion
  73.1 7.6 %collective-permute-start.5 = (bf16[4096,128]{1,0:T(8,128)(2,1)S(1)}, bf16[4096,128]{1,0:T(8,128)(2,1)}, u32[]{:S(2)}, u32[]{:S(2)}) collective-permute-start(bf16[4096,128]{1,0:T(8,128)(2,1)S(1)} %maximum_select_fusion), channel_id=1, source_target_pairs={{0,1},{1,0},{2,3},{3,2},{4,5},{5,4},{6,7},{7,6},{8,9},{9,8},{10,11... | collective-permute-start | bytes 3145736 | tf_op jit(solution)/shard_map/ppermute | solution.py:107
  81.7 2.5 maximum_select_fusion.1
  84.2 2.8 %broadcast_select_fusion = (bf16[4096,128]{1,0:T(8,128)(2,1)}, bf16[4096,128]{1,0:T(8,128)(2,1)}) fusion(bf16[4096,128]{1,0:T(8,128)(2,1)} %collective-permute-done.5, bf16[4096,128]{1,0:T(8,128)(2,1)S(1)} %maximum_select_fusion, pred[]{:T(512)S(6)} %eq.124), kind=kLoop, calls=%fused_computation.37 | loop fusion | flops 1048576 | bytes 4194305 | tf_op jit(solution)/shard_map/jit(_where)/select_n | solution.py:109
  94.0 2.1 collective-permute-start.6
  96.1 1.9 collective-permute-done.6
  98.9 30.4 %all-to-all-start = ((bf16[8,8,4096]{2,1,0:T(8,128)(2,1)}), bf16[8,8,4096]{2,1,0:T(8,128)(2,1)S(1)}, u32[]{:S(2)}, u32[]{:S(2)}) async-start(bf16[8,8,4096]{2,1,0:T(8,128)(2,1)} %fusion.13), calls=%async_computation | async-start | bytes 1048576 | tf_op jit(solution)/shard_map/all_to_all | solution.py:167
  129.9 20.8 %all-to-all-done = bf16[8,8,4096]{2,1,0:T(8,128)(2,1)S(1)} async-done(((bf16[8,8,4096]{2,1,0:T(8,128)(2,1)}), bf16[8,8,4096]{2,1,0:T(8,128)(2,1)S(1)}, u32[]{:S(2)}, u32[]{:S(2)}) %all-to-all-start) | async-done | bytes 524320 | tf_op jit(solution)/shard_map/all_to_all | solution.py:167
  153.8 62.2 %all_to_all.15 = bf16[16,6,4096]{2,1,0:T(8,128)(2,1)} all-to-all(bf16[16,6,4096]{2,1,0:T(8,128)(2,1)S(1)} %reshape.393), channel_id=1, replica_groups=mesh['zh'=2,'x'=4,'y'=4,'zl'=8,'c'=2] {'zl','c'}, dimensions={0} | all-to-all | bytes 1572864 | tf_op jit(solution)/shard_map/all_to_all | solution.py:188
  216.0 1.4 reshape.416
  217.5 6.4 %fusion.22 = f32[96,16,2,2,24]{0,4,3,2,1:T(8,128)S(1)} fusion(bf16[16,2,2,24,4096]{4,3,2,1,0:T(8,128)(2,1)} %bitcast.322, bf16[96,4096,1,1,1]{1,0,2,3,4:T(8,128)(2,1)S(1)} %reshape.416), kind=kOutput, calls=%fused_computation.48 | convolution fusion | flops 1207959552 | bytes 13959168 | tf_op jit(solution)/shard_map/sd,fd->sf/dot_general | solution.py:191
  225.1 1.8 convert_element_type.92
  226.9 8.5 %all-to-all-start.2 = ((bf16[16,6,768]{2,1,0:T(8,128)(2,1)}), bf16[16,6,768]{2,1,0:T(8,128)(2,1)S(1)}, u32[]{:S(2)}, u32[]{:S(2)}) async-start(bf16[16,6,768]{2,1,0:T(8,128)(2,1)} %convert_element_type.92), calls=%async_computation.2 | async-start | bytes 393216 | tf_op jit(solution)/shard_map/all_to_all | solution.py:196
  235.5 14.6 %all-to-all-done.2 = bf16[16,6,768]{2,1,0:T(8,128)(2,1)S(1)} async-done(((bf16[16,6,768]{2,1,0:T(8,128)(2,1)}), bf16[16,6,768]{2,1,0:T(8,128)(2,1)S(1)}, u32[]{:S(2)}, u32[]{:S(2)}) %all-to-all-start.2) | async-done | bytes 147488 | tf_op jit(solution)/shard_map/all_to_all | solution.py:196
  (86 shorter events, 17.5 us)
Async XLA Ops:
  7.2 86.2 %copy-start = (bf16[256,4096]{1,0:T(8,128)(2,1)S(1)}, bf16[256,4096]{1,0:T(8,128)(2,1)}, u32[]{:S(2)}) copy-start(bf16[256,4096]{1,0:T(8,128)(2,1)} %param.17) | copy-start | bytes 6291460
  7.2 210.3 %all-gather.2.cloned.1.call-start = ((), (), s32[]{:S(2)}) async-start(), calls=%async_computation.3 | async-start | bytes 13369344 | tf_op jit(solution)/shard_map/all_gather | solution.py:111
  9.3 29.0 %collective-permute-start = (bf16[212992]{0:T(1024)(128)(2,1)S(1)}, bf16[212992]{0:T(1024)(128)(2,1)S(1)}, u32[]{:S(2)}, u32[]{:S(2)}) collective-permute-start(bf16[212992]{0:T(1024)(128)(2,1)S(1)} %pad_maximum_fusion), channel_id=1, source_target_pairs={{0,256},{16,272},{32,288},{48,304},{64,320},{80,336},{96,352},{112... | collective-permute-start | bytes 1277960 | tf_op jit(solution)/shard_map/ppermute | solution.py:88
  38.4 18.2 %copy-start.2 = (bf16[212992]{0:T(1024)(128)(2,1)}, bf16[212992]{0:T(1024)(128)(2,1)S(1)}, u32[]{:S(2)}) copy-start(bf16[212992]{0:T(1024)(128)(2,1)S(1)} %collective-permute-done) | copy-start | bytes 1277956
  38.4 7.3 %collective-permute-start.1 = (bf16[256,128]{1,0:T(8,128)(2,1)S(1)}, bf16[256,128]{1,0:T(8,128)(2,1)S(1)}, u32[]{:S(2)}, u32[]{:S(2)}) collective-permute-start(bf16[256,128]{1,0:T(8,128)(2,1)S(1)} %maximum_select_fusion.5), channel_id=1, source_target_pairs={{0,128},{16,144},{32,160},{48,176},{64,192},{80,208},{96,224},{112... | collective-permute-start | bytes 196616 | tf_op jit(solution)/shard_map/ppermute | solution.py:103
  45.8 5.7 %collective-permute-start.2 = (bf16[512,128]{1,0:T(8,128)(2,1)S(1)}, bf16[512,128]{1,0:T(8,128)(2,1)S(1)}, u32[]{:S(2)}, u32[]{:S(2)}) collective-permute-start(bf16[512,128]{1,0:T(8,128)(2,1)S(1)} %maximum_select_fusion.4), channel_id=1, source_target_pairs={{0,64},{16,80},{32,96},{48,112},{64,0},{80,16},{96,32},{112,48},{1... | collective-permute-start | bytes 393224 | tf_op jit(solution)/shard_map/ppermute | solution.py:103
  51.6 8.8 %collective-permute-start.3 = (bf16[1024,128]{1,0:T(8,128)(2,1)S(1)}, bf16[1024,128]{1,0:T(8,128)(2,1)S(1)}, u32[]{:S(2)}, u32[]{:S(2)}) collective-permute-start(bf16[1024,128]{1,0:T(8,128)(2,1)S(1)} %maximum_select_fusion.3), channel_id=1, source_target_pairs={{0,32},{16,48},{32,0},{48,16},{64,96},{80,112},{96,64},{112,80},{1... | collective-permute-start | bytes 786440 | tf_op jit(solution)/shard_map/ppermute | solution.py:103
  60.4 20.4 %slice-start = ((bf16[212992]{0:T(1024)(128)(2,1)}), bf16[196608]{0:T(1024)(128)(2,1)S(1)}, s32[]{:S(2)}) async-start(bf16[212992]{0:T(1024)(128)(2,1)} %copy-done.2), calls=%async_computation.4 | async-start | bytes 786432 | tf_op jit(solution)/shard_map/slice | solution.py:89
  60.5 3.3 %copy-start.1 = (bf16[2048,128]{1,0:T(8,128)(2,1)}, bf16[2048,128]{1,0:T(8,128)(2,1)S(1)}, u32[]{:S(2)}) copy-start(bf16[2048,128]{1,0:T(8,128)(2,1)S(1)} %maximum_select_fusion.2) | copy-start | bytes 1572868
  60.5 10.8 %collective-permute-start.4 = (bf16[2048,128]{1,0:T(8,128)(2,1)S(1)}, bf16[2048,128]{1,0:T(8,128)(2,1)}, u32[]{:S(2)}, u32[]{:S(2)}) collective-permute-start(bf16[2048,128]{1,0:T(8,128)(2,1)S(1)} %maximum_select_fusion.2), channel_id=1, source_target_pairs={{0,16},{16,0},{32,48},{48,32},{64,80},{80,64},{96,112},{112,96},{1... | collective-permute-start | bytes 1572872 | tf_op jit(solution)/shard_map/ppermute | solution.py:103
  73.1 11.1 %collective-permute-start.5 = (bf16[4096,128]{1,0:T(8,128)(2,1)S(1)}, bf16[4096,128]{1,0:T(8,128)(2,1)}, u32[]{:S(2)}, u32[]{:S(2)}) collective-permute-start(bf16[4096,128]{1,0:T(8,128)(2,1)S(1)} %maximum_select_fusion), channel_id=1, source_target_pairs={{0,1},{1,0},{2,3},{3,2},{4,5},{5,4},{6,7},{7,6},{8,9},{9,8},{10,11... | collective-permute-start | bytes 3145736 | tf_op jit(solution)/shard_map/ppermute | solution.py:107
  84.2 2.8 %copy-start.10 = (s32[64]{0:T(128)S(1)}, s32[64]{0:T(128)}, u32[]{:S(2)}) copy-start(s32[64]{0:T(128)} %param.16) | copy-start | bytes 772
  84.2 2.9 %copy-start.11 = (s32[32]{0:T(128)S(1)}, s32[32]{0:T(128)}, u32[]{:S(2)}) copy-start(s32[32]{0:T(128)} %constant.180) | copy-start | bytes 388
  84.2 4.1 %copy-start.12 = (bf16[128,256]{1,0:T(8,128)(2,1)S(1)}, bf16[128,256]{1,0:T(8,128)(2,1)}, u32[]{:S(2)}) copy-start(bf16[128,256]{1,0:T(8,128)(2,1)} %param.13) | copy-start | bytes 196612
  87.0 2.7 %copy-start.4 = (bf16[4096,128]{1,0:T(8,128)(2,1)S(1)}, bf16[4096,128]{1,0:T(8,128)(2,1)}, u32[]{:S(2)}) copy-start(bf16[4096,128]{1,0:T(8,128)(2,1)} %get-tuple-element.5) | copy-start | bytes 3145732
  90.7 1.2 copy-start.3
  93.9 35.4 %copy-start.7 = (s32[8,8]{1,0:T(8,128)S(1)}, s32[8,8]{1,0:T(8,128)}, u32[]{:S(2)}) copy-start(s32[8,8]{1,0:T(8,128)} %param.21) | copy-start | bytes 772
  93.9 56.9 %copy-start.6 = (bf16[8,4096]{1,0:T(8,128)(2,1)S(1)}, bf16[8,4096]{1,0:T(8,128)(2,1)}, u32[]{:S(2)}) copy-start(bf16[8,4096]{1,0:T(8,128)(2,1)} %param.12) | copy-start | bytes 196612
  94.0 57.1 %copy-start.8 = (f32[4096]{0:T(1024)S(1)}, f32[4096]{0:T(1024)}, u32[]{:S(2)}) copy-start(f32[4096]{0:T(1024)} %param.18) | copy-start | bytes 49156
  94.0 3.9 %collective-permute-start.6 = (bf16[8,8,4096]{2,1,0:T(8,128)(2,1)S(1)}, bf16[8,8,4096]{2,1,0:T(8,128)(2,1)S(1)}, u32[]{:S(2)}, u32[]{:S(2)}) collective-permute-start(bf16[8,8,4096]{2,1,0:T(8,128)(2,1)S(1)} %fusion.28), channel_id=1, source_target_pairs={{0,1},{1,0},{2,3},{3,2},{4,5},{5,4},{6,7},{7,6},{8,9},{9,8},{10,11... | collective-permute-start | bytes 1572872 | tf_op jit(solution)/shard_map/ppermute | solution.py:165
  98.9 51.9 %all-to-all-start = ((bf16[8,8,4096]{2,1,0:T(8,128)(2,1)}), bf16[8,8,4096]{2,1,0:T(8,128)(2,1)S(1)}, u32[]{:S(2)}, u32[]{:S(2)}) async-start(bf16[8,8,4096]{2,1,0:T(8,128)(2,1)} %fusion.13), calls=%async_computation | async-start | bytes 1048576 | tf_op jit(solution)/shard_map/all_to_all | solution.py:167
  151.0 65.0 %copy-start.5 = (bf16[8,4096]{1,0:T(8,128)(2,1)}, bf16[8,4096]{1,0:T(8,128)(2,1)S(1)}, u32[]{:S(2)}) copy-start(bf16[8,4096]{1,0:T(8,128)(2,1)S(1)} %get-tuple-element.15) | copy-start | bytes 196612
  224.0 26.8 %copy-start.9 = (f32[8,8]{1,0:T(8,128)S(1)}, f32[8,8]{1,0:T(8,128)}, u32[]{:S(2)}) copy-start(f32[8,8]{1,0:T(8,128)} %param.22) | copy-start | bytes 772
  226.9 23.2 %all-to-all-start.2 = ((bf16[16,6,768]{2,1,0:T(8,128)(2,1)}), bf16[16,6,768]{2,1,0:T(8,128)(2,1)S(1)}, u32[]{:S(2)}, u32[]{:S(2)}) async-start(bf16[16,6,768]{2,1,0:T(8,128)(2,1)} %convert_element_type.92), calls=%async_computation.2 | async-start | bytes 393216 | tf_op jit(solution)/shard_map/all_to_all | solution.py:196
Sparse Core Ops, SparseCore 0:
  87.1 128.1 all-gather.1

commit v5 on v3

--- a/solution.py
+++ b/solution.py
@@ -158,34 +158,69 @@
     tok_dev = residual.shape[0]
 
     share = jnp.dot(attn, out_proj, preferred_element_type=jnp.float32).astype(jnp.bfloat16)
-    by_core = jnp.transpose(share.reshape(n_exp // 2, 2, tok_dev, D), (1, 0, 2, 3))
+    zl_index = lax.axis_index("zl")
+    n_zl = n_exp // 2
+    by_core = jnp.transpose(share.reshape(n_zl, 2, tok_dev, D), (1, 0, 2, 3))
     keep = jnp.where(core_index == 0, by_core[0], by_core[1])
     give = jnp.where(core_index == 0, by_core[1], by_core[0])
     got = lax.ppermute(give, "c", [(0, 1), (1, 0)])
-    pair_sum = (keep.astype(jnp.float32) + got.astype(jnp.float32)).astype(jnp.bfloat16)
-    shares = lax.all_to_all(pair_sum, "zl", split_axis=0, concat_axis=0, tiled=True)
-    head_total = jnp.sum(shares.astype(jnp.float32), axis=0)
+    part = keep.astype(jnp.float32) + got.astype(jnp.float32)
+    zl_bits = doubling_bits(n_zl)[::-1]
+    part = part.reshape((2,) * len(zl_bits) + (tok_dev, D))
+    for step, bit in enumerate(zl_bits):
+        axis = len(zl_bits) - 1 - step
+        mine = (zl_index & bit) == 0
+        lo = lax.index_in_dim(part, 0, axis, keepdims=False)
+        hi = lax.index_in_dim(part, 1, axis, keepdims=False)
+        stay = jnp.where(mine, lo, hi)
+        send = jnp.where(mine, hi, lo)
+        part = stay + lax.ppermute(send, "zl", [(i, i ^ bit) for i in range(n_zl)])
+    head_total = part
     mixed = (residual.astype(jnp.float32) + head_total).astype(jnp.bfloat16)
     mixed_f = mixed.astype(jnp.float32)
     square = jnp.mean(mixed_f * mixed_f, axis=1, keepdims=True)
     normed = (mixed_f * lax.rsqrt(square + 1e-06) * norm_gain[None, :]).astype(jnp.bfloat16)
 
+    ids_pad = jnp.zeros((tok_dev, 128), jnp.bfloat16).at[:, :TOPK].set(
+        expert_ids.astype(jnp.bfloat16)
+    )
+    cur = jnp.concatenate([normed, ids_pad], axis=1)
+    order = [0]
+    for bit in doubling_bits(n_zl):
+        other = lax.ppermute(cur, "zl", [(i, i ^ bit) for i in range(n_zl)])
+        low = (zl_index & bit) == 0
+        cur = jnp.where(low, jnp.concatenate([cur, other]), jnp.concatenate([other, cur]))
+        order = order + [o + bit for o in order]
+    partner = lax.ppermute(cur, "c", [(0, 1), (1, 0)])
+    both = jnp.where(
+        core_index == 0, jnp.concatenate([cur, partner]), jnp.concatenate([partner, cur])
+    )
+    blocks = []
+    for src in range(n_exp):
+        q = (src % 2) * n_zl + order.index(src // 2)
+        blocks.append(both[q * tok_dev : (q + 1) * tok_dev])
+    gathered = jnp.concatenate(blocks)
+    normed_all = gathered[:, :D]
+    ids_all = gathered[:, D : D + TOPK].astype(jnp.int32)
+
     most_slots = 3 * tok_dev // 4
+    chosen = jnp.any(ids_all == exp_index, axis=1).astype(jnp.int32).reshape(n_exp, tok_dev)
+    rank = jnp.cumsum(chosen, axis=1) - chosen
+    dest = jnp.where(
+        chosen == 1, jnp.arange(n_exp, dtype=jnp.int32)[:, None] * most_slots + rank, -1
+    ).reshape(-1)
+    placing = (
+        jnp.arange(n_exp * most_slots, dtype=jnp.int32)[:, None] == dest[None, :]
+    ).astype(jnp.bfloat16)
+    received = jnp.dot(placing, normed_all, preferred_element_type=jnp.float32).astype(
+        jnp.bfloat16
+    )
+
     ids_flat = expert_ids.reshape(-1)
     onehot = (ids_flat[:, None] == jnp.arange(EXPERTS, dtype=jnp.int32)[None, :]).astype(jnp.int32)
     earlier = jnp.cumsum(onehot, axis=0) - onehot
     slot = jnp.sum(earlier * onehot, axis=1)
     target = ids_flat * most_slots + slot
-    placing = (
-        target[:, None] == jnp.arange(EXPERTS * most_slots, dtype=jnp.int32)[None, :]
-    ).astype(jnp.bfloat16)
-    placing = jnp.sum(placing.reshape(tok_dev, TOPK, EXPERTS * most_slots), axis=1)
-    outgoing = jnp.einsum("ts,td->sd", placing, normed, preferred_element_type=jnp.float32).astype(
-        jnp.bfloat16
-    )
-    outgoing = outgoing.reshape(EXPERTS, most_slots, D)
-    received = lax.all_to_all(outgoing, EXP, split_axis=0, concat_axis=0, tiled=True)
-    received = received.reshape(EXPERTS * most_slots, D)
 
     proj = jnp.einsum("sd,fd->sf", received, w_all, preferred_element_type=jnp.float32)
     proj = proj.reshape(EXPERTS * most_slots, n_xy, n_zh, 2, fe_dev)

time: 265 us -> 287 us (1.083)
  waiting for transfers between devices: 65.9 us -> 142 us
  blocking collectives: 62.4 us -> 0 us
  starting transfers between devices: 92.1 us -> 99.4 us
  other arithmetic: 9.3 us -> 12.2 us
    all_to_all x1 -> x0, blocking collectives: 62.4 us -> none  [shards(): lax.all_to_all(outgoing, EXP, split_axis=0, concat_axis=0, tiled=True)]
    ppermute x0 -> x6, waiting for transfers between devices: none -> 54.5 us  [the longest x3 33.9 us: shards(): part = stay + lax.ppermute(send, 'zl', [(i, i ^ bit) for i in range(n_zl)])]
    all_to_all x1 -> x0, starting transfers between devices: 42.4 us -> none  [shards(): lax.all_to_all(pair_sum, 'zl', split_axis=0, concat_axis=0, tiled=True)]
    all_gather x1, waiting for transfers between devices: 0.02 us -> 41.2 us  [shards(): w_all = lax.all_gather(w_pair, ('x', 'y'), axis=0, tiled=True)]
    ppermute x0 -> x6, starting transfers between devices: none -> 40.6 us  [the longest x3 34.8 us: shards(): part = stay + lax.ppermute(send, 'zl', [(i, i ^ bit) for i in range(n_zl)])]
    all_to_all x1 -> x0, waiting for transfers between devices: 20.6 us -> none  [shards(): lax.all_to_all(pair_sum, 'zl', split_axis=0, concat_axis=0, tiled=True)]
    all_to_all x1, starting transfers between devices: 6.05 us -> 10.7 us  [shards(): lax.all_to_all(hidden.astype(jnp.bfloat16), EXP, split_axis=0, concat_axi...]
    ppermute x1 -> x2, starting transfers between devices: 7.63 us -> 12.2 us  [shards(): partner = lax.ppermute(cur, 'c', [(0, 1), (1, 0)])]
  transfers between devices with their start and end apart: 10 -> 16, of which waited for: 9 -> 16; matrix products, arithmetic and copies ran while one was open for 5% -> 2% of each run, Pallas kernels for 0% -> 0%
where the time goes in v5:
time: 287 us
  waiting for transfers between devices  142 us (49%)
  starting transfers between devices  99.4 us (35%)
  between operations  14.8 us (5%)
  other arithmetic  12.2 us (4%)
  matrix products  10.4 us (4%)
  local copies, waits for them, and re-layouts  8.41 us (3%)
    all_gather x1, waiting for transfers between devices, shards(): w_all = lax.all_gather(w_pair, ('x', 'y'), axis=0, tiled=True)  41.2 us
    ppermute x3, starting transfers between devices, shards(): part = stay + lax.ppermute(send, 'zl', [(i, i ^ bit) for i in range(n_zl)])  34.8 us
    ppermute x3, waiting for transfers between devices, shards(): part = stay + lax.ppermute(send, 'zl', [(i, i ^ bit) for i in range(n_zl)])  33.9 us
    ppermute x3, waiting for transfers between devices, shards(): other = lax.ppermute(cur, 'zl', [(i, i ^ bit) for i in range(n_zl)])  20.6 us
    ppermute x4, starting transfers between devices, shards(): other = lax.ppermute(cur, CTX, [(i, i ^ bit) for i in range(n_ctx)])  17.3 us
    ppermute x1, starting transfers between devices, shards(): joint = lax.ppermute(joint, CTX, [(i, i ^ first) for i in range(n_ctx)])  16.3 us
    ppermute x4, waiting for transfers between devices, shards(): other = lax.ppermute(cur, CTX, [(i, i ^ bit) for i in range(n_ctx)])  15 us
    all_to_all x1, waiting for transfers between devices, shards(): lax.all_to_all(hidden.astype(jnp.bfloat16), EXP, split_axis=0, concat_axi...  14.6 us
  transfers between devices with their start and end apart: 16, of which 16 were waited for; matrix products, arithmetic and copies ran while one was open for 2% of the time, Pallas kernels for 0%

profile of v5, /device:TPU:1, one launch (start us, length us, event | category | flops | bytes accessed | tf_op | source)
XLA Modules:
  0.0 286.8 jit_solution(9249243995834748690)
XLA Ops:
  8.6 16.3 %collective-permute-start = (bf16[212992]{0:T(1024)(128)(2,1)S(1)}, bf16[212992]{0:T(1024)(128)(2,1)S(1)}, u32[]{:S(2)}, u32[]{:S(2)}) collective-permute-start(bf16[212992]{0:T(1024)(128)(2,1)S(1)} %pad_maximum_fusion), channel_id=1, source_target_pairs={{0,256},{16,272},{32,288},{48,304},{64,320},{80,336},{96,352},{112... | collective-permute-start | bytes 1277960 | tf_op jit(solution)/shard_map/ppermute | solution.py:88
  24.9 12.7 %collective-permute-done = bf16[212992]{0:T(1024)(128)(2,1)S(1)} collective-permute-done((bf16[212992]{0:T(1024)(128)(2,1)S(1)}, bf16[212992]{0:T(1024)(128)(2,1)S(1)}, u32[]{:S(2)}, u32[]{:S(2)}) %collective-permute-start) | collective-permute-done | bytes 426016 | tf_op jit(solution)/shard_map/ppermute | solution.py:88
  37.7 5.7 %collective-permute-start.1 = (bf16[256,128]{1,0:T(8,128)(2,1)S(1)}, bf16[256,128]{1,0:T(8,128)(2,1)S(1)}, u32[]{:S(2)}, u32[]{:S(2)}) collective-permute-start(bf16[256,128]{1,0:T(8,128)(2,1)S(1)} %maximum_select_fusion.9), channel_id=1, source_target_pairs={{0,128},{16,144},{32,160},{48,176},{64,192},{80,208},{96,224},{112... | collective-permute-start | bytes 196616 | tf_op jit(solution)/shard_map/ppermute | solution.py:104
  45.1 3.3 %collective-permute-start.2 = (bf16[512,128]{1,0:T(8,128)(2,1)S(1)}, bf16[512,128]{1,0:T(8,128)(2,1)S(1)}, u32[]{:S(2)}, u32[]{:S(2)}) collective-permute-start(bf16[512,128]{1,0:T(8,128)(2,1)S(1)} %maximum_select_fusion.8), channel_id=1, source_target_pairs={{0,64},{16,80},{32,96},{48,112},{64,0},{80,16},{96,32},{112,48},{1... | collective-permute-start | bytes 393224 | tf_op jit(solution)/shard_map/ppermute | solution.py:104
  48.4 2.4 collective-permute-done.2
  50.9 5.0 %collective-permute-start.3 = (bf16[1024,128]{1,0:T(8,128)(2,1)S(1)}, bf16[1024,128]{1,0:T(8,128)(2,1)S(1)}, u32[]{:S(2)}, u32[]{:S(2)}) collective-permute-start(bf16[1024,128]{1,0:T(8,128)(2,1)S(1)} %maximum_select_fusion.6), channel_id=1, source_target_pairs={{0,32},{16,48},{32,0},{48,16},{64,96},{80,112},{96,64},{112,80},{1... | collective-permute-start | bytes 786440 | tf_op jit(solution)/shard_map/ppermute | solution.py:104
  55.9 3.7 %collective-permute-done.3 = bf16[1024,128]{1,0:T(8,128)(2,1)S(1)} collective-permute-done((bf16[1024,128]{1,0:T(8,128)(2,1)S(1)}, bf16[1024,128]{1,0:T(8,128)(2,1)S(1)}, u32[]{:S(2)}, u32[]{:S(2)}) %collective-permute-start.3) | collective-permute-done | bytes 262176 | tf_op jit(solution)/shard_map/ppermute | solution.py:104
  59.8 3.2 %collective-permute-start.4 = (bf16[2048,128]{1,0:T(8,128)(2,1)S(1)}, bf16[2048,128]{1,0:T(8,128)(2,1)S(1)}, u32[]{:S(2)}, u32[]{:S(2)}) collective-permute-start(bf16[2048,128]{1,0:T(8,128)(2,1)S(1)} %maximum_select_fusion.4), channel_id=1, source_target_pairs={{0,16},{16,0},{32,48},{48,32},{64,80},{80,64},{96,112},{112,96},{1... | collective-permute-start | bytes 1572872 | tf_op jit(solution)/shard_map/ppermute | solution.py:104
  63.3 7.3 %collective-permute-done.4 = bf16[2048,128]{1,0:T(8,128)(2,1)S(1)} collective-permute-done((bf16[2048,128]{1,0:T(8,128)(2,1)S(1)}, bf16[2048,128]{1,0:T(8,128)(2,1)S(1)}, u32[]{:S(2)}, u32[]{:S(2)}) %collective-permute-start.4) | collective-permute-done | bytes 524320 | tf_op jit(solution)/shard_map/ppermute | solution.py:104
  70.8 7.6 %collective-permute-start.5 = (bf16[4096,128]{1,0:T(8,128)(2,1)S(1)}, bf16[4096,128]{1,0:T(8,128)(2,1)S(1)}, u32[]{:S(2)}, u32[]{:S(2)}) collective-permute-start(bf16[4096,128]{1,0:T(8,128)(2,1)S(1)} %maximum_select_fusion.1), channel_id=1, source_target_pairs={{0,1},{1,0},{2,3},{3,2},{4,5},{5,4},{6,7},{7,6},{8,9},{9,8},{10,11... | collective-permute-start | bytes 3145736 | tf_op jit(solution)/shard_map/ppermute | solution.py:108
  86.3 2.3 collective-permute-start.6
  92.6 25.7 %collective-permute-start.7 = (f32[2,2,8,4096]{3,2,1,0:T(8,128)}, f32[2,2,8,4096]{3,2,1,0:T(8,128)}, u32[]{:S(2)}, u32[]{:S(2)}) collective-permute-start(f32[2,2,8,4096]{3,2,1,0:T(8,128)} %select_bitcast_fusion), channel_id=1, source_target_pairs={{0,2},{2,0},{4,6},{6,4},{8,10},{10,8},{12,14},{14,12},{1,3},{3,1},... | collective-permute-start | bytes 1572872 | tf_op jit(solution)/shard_map/ppermute | solution.py:177
  119.9 10.7 %collective-permute-done.7 = f32[2,2,8,4096]{3,2,1,0:T(8,128)} collective-permute-done((f32[2,2,8,4096]{3,2,1,0:T(8,128)}, f32[2,2,8,4096]{3,2,1,0:T(8,128)}, u32[]{:S(2)}, u32[]{:S(2)}) %collective-permute-start.7) | collective-permute-done | bytes 524320 | tf_op jit(solution)/shard_map/ppermute | solution.py:177
  135.8 12.7 %collective-permute-done.8 = f32[2,8,4096]{2,1,0:T(8,128)S(1)} collective-permute-done((f32[2,8,4096]{2,1,0:T(8,128)S(1)}, f32[2,8,4096]{2,1,0:T(8,128)S(1)}, u32[]{:S(2)}, u32[]{:S(2)}) %collective-permute-start.8) | collective-permute-done | bytes 262176 | tf_op jit(solution)/shard_map/ppermute | solution.py:177
  148.5 7.1 %collective-permute-start.9 = (f32[8,4096]{1,0:T(8,128)S(1)}, f32[8,4096]{1,0:T(8,128)S(1)}, u32[]{:S(2)}, u32[]{:S(2)}) collective-permute-start(f32[8,4096]{1,0:T(8,128)S(1)} %select_bitcast_fusion.3), channel_id=1, source_target_pairs={{0,8},{2,10},{4,12},{6,14},{8,0},{10,2},{12,4},{14,6},{1,9},{3,11}... | collective-permute-start | bytes 393224 | tf_op jit(solution)/shard_map/ppermute | solution.py:177
  156.3 10.5 %collective-permute-done.9 = f32[8,4096]{1,0:T(8,128)S(1)} collective-permute-done((f32[8,4096]{1,0:T(8,128)S(1)}, f32[8,4096]{1,0:T(8,128)S(1)}, u32[]{:S(2)}, u32[]{:S(2)}) %collective-permute-start.9) | collective-permute-done | bytes 131104 | tf_op jit(solution)/shard_map/ppermute | solution.py:177
  169.0 7.0 %collective-permute-done.10 = bf16[8,4224]{1,0:T(8,128)(2,1)S(1)} collective-permute-done((bf16[8,4224]{1,0:T(8,128)(2,1)S(1)}, bf16[8,4224]{1,0:T(8,128)(2,1)S(1)}, u32[]{:S(2)}, u32[]{:S(2)}) %collective-permute-start.10) | collective-permute-done | bytes 67616 | tf_op jit(solution)/shard_map/ppermute | solution.py:190
  178.0 7.5 %collective-permute-done.11 = bf16[16,4224]{1,0:T(8,128)(2,1)S(1)} collective-permute-done((bf16[16,4224]{1,0:T(8,128)(2,1)S(1)}, bf16[16,4224]{1,0:T(8,128)(2,1)S(1)}, u32[]{:S(2)}, u32[]{:S(2)}) %collective-permute-start.11) | collective-permute-done | bytes 135200 | tf_op jit(solution)/shard_map/ppermute | solution.py:190
  187.7 6.1 %collective-permute-done.12 = bf16[32,4224]{1,0:T(8,128)(2,1)S(1)} collective-permute-done((bf16[32,4224]{1,0:T(8,128)(2,1)S(1)}, bf16[32,4224]{1,0:T(8,128)(2,1)S(1)}, u32[]{:S(2)}, u32[]{:S(2)}) %collective-permute-start.12) | collective-permute-done | bytes 270368 | tf_op jit(solution)/shard_map/ppermute | solution.py:190
  193.9 4.6 %collective-permute-start.13 = (bf16[64,4224]{1,0:T(8,128)(2,1)S(1)}, bf16[64,4224]{1,0:T(8,128)(2,1)S(1)}, u32[]{:S(2)}, u32[]{:S(2)}) collective-permute-start(bf16[64,4224]{1,0:T(8,128)(2,1)S(1)} %maximum_select_fusion.3), channel_id=1, source_target_pairs={{0,1},{1,0},{2,3},{3,2},{4,5},{5,4},{6,7},{7,6},{8,9},{9,8},{10,11... | collective-permute-start | bytes 1622024 | tf_op jit(solution)/shard_map/ppermute | solution.py:194
  201.8 41.2 %all-gather.2.cloned.1.call-done = bf16[1536,4096]{1,0:T(8,128)(2,1)} async-done(((bf16[96,4096]{1,0:T(8,128)(2,1)}), bf16[1536,4096]{1,0:T(8,128)(2,1)}) %all-gather.2.cloned.1.call-update) | async-done | bytes 12582928 | tf_op jit(solution)/shard_map/all_gather | solution.py:96
  243.0 7.1 %fusion.4 = f32[96,1536]{0,1:T(8,128)S(1)} fusion(bf16[1536,4096]{1,0:T(8,128)(2,1)} %all-gather.2.cloned.1.call-done, bf16[128,4224]{1,0:T(8,128)(2,1)} %copy-done.6, s32[128]{0:T(128)S(1)} %compare_select_fusion.2), kind=kOutput, calls=%fused_computation.11 | convolution fusion | flops 1309028352 | bytes 14221824 | tf_op jit(solution)/shard_map/sd,fd->sf/dot_general | solution.py:225
  253.1 10.7 %all-to-all-start = ((bf16[16,6,768]{2,1,0:T(8,128)(2,1)}), bf16[16,6,768]{2,1,0:T(8,128)(2,1)S(1)}, u32[]{:S(2)}, u32[]{:S(2)}) async-start(bf16[16,6,768]{2,1,0:T(8,128)(2,1)} %convert_element_type.102), calls=%async_computation | async-start | bytes 393216 | tf_op jit(solution)/shard_map/all_to_all | solution.py:230
  263.9 14.6 %all-to-all-done = bf16[16,6,768]{2,1,0:T(8,128)(2,1)S(1)} async-done(((bf16[16,6,768]{2,1,0:T(8,128)(2,1)}), bf16[16,6,768]{2,1,0:T(8,128)(2,1)S(1)}, u32[]{:S(2)}, u32[]{:S(2)}) %all-to-all-start) | async-done | bytes 147488 | tf_op jit(solution)/shard_map/all_to_all | solution.py:230
  (144 shorter events, 37.0 us)
Async XLA Ops:
  7.2 77.5 %copy-start = (bf16[256,4096]{1,0:T(8,128)(2,1)S(1)}, bf16[256,4096]{1,0:T(8,128)(2,1)}, u32[]{:S(2)}) copy-start(bf16[256,4096]{1,0:T(8,128)(2,1)} %param.19) | copy-start | bytes 6291460
  7.2 235.8 %all-gather.2.cloned.1.call-start = ((), (), s32[]{:S(2)}) async-start(), calls=%async_computation.1 | async-start | bytes 13369344 | tf_op jit(solution)/shard_map/all_gather | solution.py:96
  8.6 54.5 %copy-start.16 = (s32[64]{0:T(128)S(1)}, s32[64]{0:T(128)}, u32[]{:S(2)}) copy-start(s32[64]{0:T(128)} %param.18) | copy-start | bytes 772
  8.6 54.6 %copy-start.17 = (s32[32]{0:T(128)S(1)}, s32[32]{0:T(128)}, u32[]{:S(2)}) copy-start(s32[32]{0:T(128)} %constant.218) | copy-start | bytes 388
  8.6 29.0 %collective-permute-start = (bf16[212992]{0:T(1024)(128)(2,1)S(1)}, bf16[212992]{0:T(1024)(128)(2,1)S(1)}, u32[]{:S(2)}, u32[]{:S(2)}) collective-permute-start(bf16[212992]{0:T(1024)(128)(2,1)S(1)} %pad_maximum_fusion), channel_id=1, source_target_pairs={{0,256},{16,272},{32,288},{48,304},{64,320},{80,336},{96,352},{112... | collective-permute-start | bytes 1277960 | tf_op jit(solution)/shard_map/ppermute | solution.py:88
  37.7 7.3 %collective-permute-start.1 = (bf16[256,128]{1,0:T(8,128)(2,1)S(1)}, bf16[256,128]{1,0:T(8,128)(2,1)S(1)}, u32[]{:S(2)}, u32[]{:S(2)}) collective-permute-start(bf16[256,128]{1,0:T(8,128)(2,1)S(1)} %maximum_select_fusion.9), channel_id=1, source_target_pairs={{0,128},{16,144},{32,160},{48,176},{64,192},{80,208},{96,224},{112... | collective-permute-start | bytes 196616 | tf_op jit(solution)/shard_map/ppermute | solution.py:104
  45.1 5.7 %collective-permute-start.2 = (bf16[512,128]{1,0:T(8,128)(2,1)S(1)}, bf16[512,128]{1,0:T(8,128)(2,1)S(1)}, u32[]{:S(2)}, u32[]{:S(2)}) collective-permute-start(bf16[512,128]{1,0:T(8,128)(2,1)S(1)} %maximum_select_fusion.8), channel_id=1, source_target_pairs={{0,64},{16,80},{32,96},{48,112},{64,0},{80,16},{96,32},{112,48},{1... | collective-permute-start | bytes 393224 | tf_op jit(solution)/shard_map/ppermute | solution.py:104
  50.9 8.8 %collective-permute-start.3 = (bf16[1024,128]{1,0:T(8,128)(2,1)S(1)}, bf16[1024,128]{1,0:T(8,128)(2,1)S(1)}, u32[]{:S(2)}, u32[]{:S(2)}) collective-permute-start(bf16[1024,128]{1,0:T(8,128)(2,1)S(1)} %maximum_select_fusion.6), channel_id=1, source_target_pairs={{0,32},{16,48},{32,0},{48,16},{64,96},{80,112},{96,64},{112,80},{1... | collective-permute-start | bytes 786440 | tf_op jit(solution)/shard_map/ppermute | solution.py:104
  59.8 10.7 %collective-permute-start.4 = (bf16[2048,128]{1,0:T(8,128)(2,1)S(1)}, bf16[2048,128]{1,0:T(8,128)(2,1)S(1)}, u32[]{:S(2)}, u32[]{:S(2)}) collective-permute-start(bf16[2048,128]{1,0:T(8,128)(2,1)S(1)} %maximum_select_fusion.4), channel_id=1, source_target_pairs={{0,16},{16,0},{32,48},{48,32},{64,80},{80,64},{96,112},{112,96},{1... | collective-permute-start | bytes 1572872 | tf_op jit(solution)/shard_map/ppermute | solution.py:104
  70.8 9.9 %collective-permute-start.5 = (bf16[4096,128]{1,0:T(8,128)(2,1)S(1)}, bf16[4096,128]{1,0:T(8,128)(2,1)S(1)}, u32[]{:S(2)}, u32[]{:S(2)}) collective-permute-start(bf16[4096,128]{1,0:T(8,128)(2,1)S(1)} %maximum_select_fusion.1), channel_id=1, source_target_pairs={{0,1},{1,0},{2,3},{3,2},{4,5},{5,4},{6,7},{7,6},{8,9},{9,8},{10,11... | collective-permute-start | bytes 3145736 | tf_op jit(solution)/shard_map/ppermute | solution.py:108
  86.3 3.9 %collective-permute-start.6 = (bf16[8,8,4096]{2,1,0:T(8,128)(2,1)S(1)}, bf16[8,8,4096]{2,1,0:T(8,128)(2,1)}, u32[]{:S(2)}, u32[]{:S(2)}) collective-permute-start(bf16[8,8,4096]{2,1,0:T(8,128)(2,1)S(1)} %select_bitcast_fusion.1), channel_id=1, source_target_pairs={{0,1},{1,0},{2,3},{3,2},{4,5},{5,4},{6,7},{7,6},{8,9},{9,8},{10,11... | collective-permute-start | bytes 1572872 | tf_op jit(solution)/shard_map/ppermute | solution.py:166
  91.7 27.2 %slice-start = ((bf16[212992]{0:T(1024)(128)(2,1)}), bf16[196608]{0:T(1024)(128)(2,1)S(1)}, s32[]{:S(2)}) async-start(bf16[212992]{0:T(1024)(128)(2,1)} %copy-done.4), calls=%async_computation.2 | async-start | bytes 786432 | tf_op jit(solution)/shard_map/slice | solution.py:89
  92.6 38.0 %collective-permute-start.7 = (f32[2,2,8,4096]{3,2,1,0:T(8,128)}, f32[2,2,8,4096]{3,2,1,0:T(8,128)}, u32[]{:S(2)}, u32[]{:S(2)}) collective-permute-start(f32[2,2,8,4096]{3,2,1,0:T(8,128)} %select_bitcast_fusion), channel_id=1, source_target_pairs={{0,2},{2,0},{4,6},{6,4},{8,10},{10,8},{12,14},{14,12},{1,3},{3,1},... | collective-permute-start | bytes 1572872 | tf_op jit(solution)/shard_map/ppermute | solution.py:177
  132.6 15.9 %collective-permute-start.8 = (f32[2,8,4096]{2,1,0:T(8,128)S(1)}, f32[2,8,4096]{2,1,0:T(8,128)S(1)}, u32[]{:S(2)}, u32[]{:S(2)}) collective-permute-start(f32[2,8,4096]{2,1,0:T(8,128)S(1)} %select_bitcast_fusion.2), channel_id=1, source_target_pairs={{0,4},{2,6},{4,0},{6,2},{8,12},{10,14},{12,8},{14,10},{1,5},{3,7},... | collective-permute-start | bytes 786440 | tf_op jit(solution)/shard_map/ppermute | solution.py:177
  135.7 19.9 %copy-start.10 = (s32[8,8]{1,0:T(8,128)S(1)}, s32[8,8]{1,0:T(8,128)}, u32[]{:S(2)}) copy-start(s32[8,8]{1,0:T(8,128)} %param.23) | copy-start | bytes 772
  135.7 31.1 %copy-start.11 = (bf16[8,4096]{1,0:T(8,128)(2,1)S(1)}, bf16[8,4096]{1,0:T(8,128)(2,1)}, u32[]{:S(2)}) copy-start(bf16[8,4096]{1,0:T(8,128)(2,1)} %param.14) | copy-start | bytes 196612
  135.7 31.2 %copy-start.14 = (f32[4096]{0:T(1024)S(1)}, f32[4096]{0:T(1024)}, u32[]{:S(2)}) copy-start(f32[4096]{0:T(1024)} %param.20) | copy-start | bytes 49156
  148.5 18.3 %collective-permute-start.9 = (f32[8,4096]{1,0:T(8,128)S(1)}, f32[8,4096]{1,0:T(8,128)S(1)}, u32[]{:S(2)}, u32[]{:S(2)}) collective-permute-start(f32[8,4096]{1,0:T(8,128)S(1)} %select_bitcast_fusion.3), channel_id=1, source_target_pairs={{0,8},{2,10},{4,12},{6,14},{8,0},{10,2},{12,4},{14,6},{1,9},{3,11}... | collective-permute-start | bytes 393224 | tf_op jit(solution)/shard_map/ppermute | solution.py:177
  166.9 26.9 %copy-start.9 = (bf16[8,4096]{1,0:T(8,128)(2,1)}, bf16[8,4096]{1,0:T(8,128)(2,1)S(1)}, u32[]{:S(2)}) copy-start(bf16[8,4096]{1,0:T(8,128)(2,1)S(1)} %get-tuple-element.19) | copy-start | bytes 196612
  167.1 8.9 %collective-permute-start.10 = (bf16[8,4224]{1,0:T(8,128)(2,1)S(1)}, bf16[8,4224]{1,0:T(8,128)(2,1)S(1)}, u32[]{:S(2)}, u32[]{:S(2)}) collective-permute-start(bf16[8,4224]{1,0:T(8,128)(2,1)S(1)} %pad_maximum_fusion.1), channel_id=1, source_target_pairs={{0,8},{2,10},{4,12},{6,14},{8,0},{10,2},{12,4},{14,6},{1,9},{3,11}... | collective-permute-start | bytes 202760 | tf_op jit(solution)/shard_map/ppermute | solution.py:190
  176.0 9.4 %collective-permute-start.11 = (bf16[16,4224]{1,0:T(8,128)(2,1)S(1)}, bf16[16,4224]{1,0:T(8,128)(2,1)S(1)}, u32[]{:S(2)}, u32[]{:S(2)}) collective-permute-start(bf16[16,4224]{1,0:T(8,128)(2,1)S(1)} %maximum_select_fusion.7), channel_id=1, source_target_pairs={{0,4},{2,6},{4,0},{6,2},{8,12},{10,14},{12,8},{14,10},{1,5},{3,7},... | collective-permute-start | bytes 405512 | tf_op jit(solution)/shard_map/ppermute | solution.py:190
  185.5 8.3 %collective-permute-start.12 = (bf16[32,4224]{1,0:T(8,128)(2,1)S(1)}, bf16[32,4224]{1,0:T(8,128)(2,1)S(1)}, u32[]{:S(2)}, u32[]{:S(2)}) collective-permute-start(bf16[32,4224]{1,0:T(8,128)(2,1)S(1)} %maximum_select_fusion.5), channel_id=1, source_target_pairs={{0,2},{2,0},{4,6},{6,4},{8,10},{10,8},{12,14},{14,12},{1,3},{3,1},... | collective-permute-start | bytes 811016 | tf_op jit(solution)/shard_map/ppermute | solution.py:190
  193.9 6.0 %collective-permute-start.13 = (bf16[64,4224]{1,0:T(8,128)(2,1)S(1)}, bf16[64,4224]{1,0:T(8,128)(2,1)S(1)}, u32[]{:S(2)}, u32[]{:S(2)}) collective-permute-start(bf16[64,4224]{1,0:T(8,128)(2,1)S(1)} %maximum_select_fusion.3), channel_id=1, source_target_pairs={{0,1},{1,0},{2,3},{3,2},{4,5},{5,4},{6,7},{7,6},{8,9},{9,8},{10,11... | collective-permute-start | bytes 1622024 | tf_op jit(solution)/shard_map/ppermute | solution.py:194
  253.1 25.3 %all-to-all-start = ((bf16[16,6,768]{2,1,0:T(8,128)(2,1)}), bf16[16,6,768]{2,1,0:T(8,128)(2,1)S(1)}, u32[]{:S(2)}, u32[]{:S(2)}) async-start(bf16[16,6,768]{2,1,0:T(8,128)(2,1)} %convert_element_type.102), calls=%async_computation | async-start | bytes 393216 | tf_op jit(solution)/shard_map/all_to_all | solution.py:230
  (12 other events, 100.7 us)
Sparse Core Ops, SparseCore 0:
  135.9 107.0 all-gather.1

commit v6 on v5

--- a/solution.py
+++ b/solution.py
@@ -165,26 +165,22 @@
     give = jnp.where(core_index == 0, by_core[1], by_core[0])
     got = lax.ppermute(give, "c", [(0, 1), (1, 0)])
     part = keep.astype(jnp.float32) + got.astype(jnp.float32)
-    zl_bits = doubling_bits(n_zl)[::-1]
-    part = part.reshape((2,) * len(zl_bits) + (tok_dev, D))
-    for step, bit in enumerate(zl_bits):
-        axis = len(zl_bits) - 1 - step
-        mine = (zl_index & bit) == 0
-        lo = lax.index_in_dim(part, 0, axis, keepdims=False)
-        hi = lax.index_in_dim(part, 1, axis, keepdims=False)
-        stay = jnp.where(mine, lo, hi)
-        send = jnp.where(mine, hi, lo)
-        part = stay + lax.ppermute(send, "zl", [(i, i ^ bit) for i in range(n_zl)])
-    head_total = part
+    pair_sum = part.astype(jnp.bfloat16)
+    shares = lax.all_to_all(pair_sum, "zl", split_axis=0, concat_axis=0, tiled=True)
+    head_total = jnp.sum(shares.astype(jnp.float32), axis=0)
     mixed = (residual.astype(jnp.float32) + head_total).astype(jnp.bfloat16)
     mixed_f = mixed.astype(jnp.float32)
     square = jnp.mean(mixed_f * mixed_f, axis=1, keepdims=True)
     normed = (mixed_f * lax.rsqrt(square + 1e-06) * norm_gain[None, :]).astype(jnp.bfloat16)
 
-    ids_pad = jnp.zeros((tok_dev, 128), jnp.bfloat16).at[:, :TOPK].set(
-        expert_ids.astype(jnp.bfloat16)
-    )
-    cur = jnp.concatenate([normed, ids_pad], axis=1)
+    ids_all = lax.all_to_all(
+        jnp.broadcast_to(expert_ids[None], (n_exp,) + expert_ids.shape),
+        EXP,
+        split_axis=0,
+        concat_axis=0,
+        tiled=True,
+    ).reshape(n_exp * tok_dev, TOPK)
+    cur = normed
     order = [0]
     for bit in doubling_bits(n_zl):
         other = lax.ppermute(cur, "zl", [(i, i ^ bit) for i in range(n_zl)])
@@ -200,8 +196,7 @@
         q = (src % 2) * n_zl + order.index(src // 2)
         blocks.append(both[q * tok_dev : (q + 1) * tok_dev])
     gathered = jnp.concatenate(blocks)
-    normed_all = gathered[:, :D]
-    ids_all = gathered[:, D : D + TOPK].astype(jnp.int32)
+    normed_all = gathered
 
     most_slots = 3 * tok_dev // 4
     chosen = jnp.any(ids_all == exp_index, axis=1).astype(jnp.int32).reshape(n_exp, tok_dev)

time: 287 us -> 259 us (0.902)
  waiting for transfers between devices: 142 us -> 69.8 us
  blocking collectives: 0 us -> 55.7 us
  starting transfers between devices: 99.4 us -> 78.6 us
  local copies, waits for them, and re-layouts: 8.41 us -> 15.9 us
    all_to_all x0 -> x1, blocking collectives: none -> 55.7 us  [shards(): lax.all_to_all(pair_sum, 'zl', split_axis=0, concat_axis=0, tiled=True)]
    ppermute x3 -> x0, starting transfers between devices: 34.8 us -> none  [shards(): part = stay + lax.ppermute(send, 'zl', [(i, i ^ bit) for i in range(n_zl)])]
    ppermute x3 -> x0, waiting for transfers between devices: 33.9 us -> none  [shards(): part = stay + lax.ppermute(send, 'zl', [(i, i ^ bit) for i in range(n_zl)])]
    all_gather x1, waiting for transfers between devices: 41.2 us -> 13.3 us  [shards(): w_all = lax.all_gather(w_pair, ('x', 'y'), axis=0, tiled=True)]
    all_to_all x0 -> x1, starting transfers between devices: none -> 10.2 us  [shards(): lax.all_to_all(jnp.broadcast_to(expert_ids[None], (n_exp,) + expert_ids.s...]
    ppermute x3, waiting for transfers between devices: 20.6 us -> 11.6 us  [shards(): other = lax.ppermute(cur, 'zl', [(i, i ^ bit) for i in range(n_zl)])]
    unnamed x54 -> x46, local copies, waits for them, and re-layouts: 3.18 us -> 9.62 us
    ppermute x3, starting transfers between devices: 5.76 us -> 11.6 us  [shards(): other = lax.ppermute(cur, 'zl', [(i, i ^ bit) for i in range(n_zl)])]
  transfers between devices with their start and end apart: 16 -> 14, of which waited for: 16 -> 11; matrix products, arithmetic and copies ran while one was open for 2% -> 9% of each run, Pallas kernels for 0% -> 0%
where the time goes in v6:
time: 259 us
  starting transfers between devices  78.6 us (30%)
  waiting for transfers between devices  69.8 us (27%)
  blocking collectives  55.7 us (22%)
  local copies, waits for them, and re-layouts  15.9 us (6%)
  between operations  14.7 us (6%)
  other arithmetic  13.5 us (5%)
  matrix products  10.4 us (4%)
    all_to_all x1, blocking collectives, shards(): lax.all_to_all(pair_sum, 'zl', split_axis=0, concat_axis=0, tiled=True)  55.7 us
    ppermute x4, starting transfers between devices, shards(): other = lax.ppermute(cur, CTX, [(i, i ^ bit) for i in range(n_ctx)])  17.3 us
    ppermute x1, starting transfers between devices, shards(): joint = lax.ppermute(joint, CTX, [(i, i ^ first) for i in range(n_ctx)])  16.3 us
    ppermute x4, waiting for transfers between devices, shards(): other = lax.ppermute(cur, CTX, [(i, i ^ bit) for i in range(n_ctx)])  15 us
    all_to_all x1, waiting for transfers between devices, shards(): lax.all_to_all(hidden.astype(jnp.bfloat16), EXP, split_axis=0, concat_axi...  14.6 us
    all_gather x1, waiting for transfers between devices, shards(): w_all = lax.all_gather(w_pair, ('x', 'y'), axis=0, tiled=True)  13.3 us
    ppermute x1, waiting for transfers between devices, shards(): joint = lax.ppermute(joint, CTX, [(i, i ^ first) for i in range(n_ctx)])  12.7 us
    ppermute x3, starting transfers between devices, shards(): other = lax.ppermute(cur, 'zl', [(i, i ^ bit) for i in range(n_zl)])  11.6 us
  transfers between devices with their start and end apart: 14, of which 11 were waited for; matrix products, arithmetic and copies ran while one was open for 9% of the time, Pallas kernels for 0%

profile of v6, /device:TPU:1, one launch (start us, length us, event | category | flops | bytes accessed | tf_op | source)
XLA Modules:
  0.0 258.6 jit_solution(12962198220362588948)
XLA Ops:
  9.4 16.3 %collective-permute-start = (bf16[212992]{0:T(1024)(128)(2,1)S(1)}, bf16[212992]{0:T(1024)(128)(2,1)S(1)}, u32[]{:S(2)}, u32[]{:S(2)}) collective-permute-start(bf16[212992]{0:T(1024)(128)(2,1)S(1)} %pad_maximum_fusion), channel_id=1, source_target_pairs={{0,256},{16,272},{32,288},{48,304},{64,320},{80,336},{96,352},{112... | collective-permute-start | bytes 1277960 | tf_op jit(solution)/shard_map/ppermute | solution.py:88
  25.7 12.7 %collective-permute-done = bf16[212992]{0:T(1024)(128)(2,1)S(1)} collective-permute-done((bf16[212992]{0:T(1024)(128)(2,1)S(1)}, bf16[212992]{0:T(1024)(128)(2,1)S(1)}, u32[]{:S(2)}, u32[]{:S(2)}) %collective-permute-start) | collective-permute-done | bytes 426016 | tf_op jit(solution)/shard_map/ppermute | solution.py:88
  38.4 5.7 %collective-permute-start.1 = (bf16[256,128]{1,0:T(8,128)(2,1)S(1)}, bf16[256,128]{1,0:T(8,128)(2,1)S(1)}, u32[]{:S(2)}, u32[]{:S(2)}) collective-permute-start(bf16[256,128]{1,0:T(8,128)(2,1)S(1)} %maximum_select_fusion.9), channel_id=1, source_target_pairs={{0,128},{16,144},{32,160},{48,176},{64,192},{80,208},{96,224},{112... | collective-permute-start | bytes 196616 | tf_op jit(solution)/shard_map/ppermute | solution.py:104
  45.8 3.3 %collective-permute-start.2 = (bf16[512,128]{1,0:T(8,128)(2,1)S(1)}, bf16[512,128]{1,0:T(8,128)(2,1)S(1)}, u32[]{:S(2)}, u32[]{:S(2)}) collective-permute-start(bf16[512,128]{1,0:T(8,128)(2,1)S(1)} %maximum_select_fusion.7), channel_id=1, source_target_pairs={{0,64},{16,80},{32,96},{48,112},{64,0},{80,16},{96,32},{112,48},{1... | collective-permute-start | bytes 393224 | tf_op jit(solution)/shard_map/ppermute | solution.py:104
  49.1 2.4 collective-permute-done.2
  51.6 5.0 %collective-permute-start.3 = (bf16[1024,128]{1,0:T(8,128)(2,1)S(1)}, bf16[1024,128]{1,0:T(8,128)(2,1)S(1)}, u32[]{:S(2)}, u32[]{:S(2)}) collective-permute-start(bf16[1024,128]{1,0:T(8,128)(2,1)S(1)} %maximum_select_fusion.5), channel_id=1, source_target_pairs={{0,32},{16,48},{32,0},{48,16},{64,96},{80,112},{96,64},{112,80},{1... | collective-permute-start | bytes 786440 | tf_op jit(solution)/shard_map/ppermute | solution.py:104
  56.8 3.6 %collective-permute-done.3 = bf16[1024,128]{1,0:T(8,128)(2,1)S(1)} collective-permute-done((bf16[1024,128]{1,0:T(8,128)(2,1)S(1)}, bf16[1024,128]{1,0:T(8,128)(2,1)S(1)}, u32[]{:S(2)}, u32[]{:S(2)}) %collective-permute-start.3) | collective-permute-done | bytes 262176 | tf_op jit(solution)/shard_map/ppermute | solution.py:104
  60.5 3.2 %collective-permute-start.4 = (bf16[2048,128]{1,0:T(8,128)(2,1)S(1)}, bf16[2048,128]{1,0:T(8,128)(2,1)}, u32[]{:S(2)}, u32[]{:S(2)}) collective-permute-start(bf16[2048,128]{1,0:T(8,128)(2,1)S(1)} %maximum_select_fusion.3), channel_id=1, source_target_pairs={{0,16},{16,0},{32,48},{48,32},{64,80},{80,64},{96,112},{112,96},{1... | collective-permute-start | bytes 1572872 | tf_op jit(solution)/shard_map/ppermute | solution.py:104
  63.9 7.4 %collective-permute-done.4 = bf16[2048,128]{1,0:T(8,128)(2,1)} collective-permute-done((bf16[2048,128]{1,0:T(8,128)(2,1)S(1)}, bf16[2048,128]{1,0:T(8,128)(2,1)}, u32[]{:S(2)}, u32[]{:S(2)}) %collective-permute-start.4) | collective-permute-done | bytes 524320 | tf_op jit(solution)/shard_map/ppermute | solution.py:104
  73.1 7.6 %collective-permute-start.5 = (bf16[4096,128]{1,0:T(8,128)(2,1)S(1)}, bf16[4096,128]{1,0:T(8,128)(2,1)}, u32[]{:S(2)}, u32[]{:S(2)}) collective-permute-start(bf16[4096,128]{1,0:T(8,128)(2,1)S(1)} %maximum_select_fusion), channel_id=1, source_target_pairs={{0,1},{1,0},{2,3},{3,2},{4,5},{5,4},{6,7},{7,6},{8,9},{9,8},{10,11... | collective-permute-start | bytes 3145736 | tf_op jit(solution)/shard_map/ppermute | solution.py:108
  83.9 2.5 maximum_select_fusion.2
  92.5 2.1 collective-permute-start.6
  96.6 55.7 %all_to_all.15 = bf16[8,8,4096]{2,1,0:T(8,128)(2,1)S(1)} all-to-all(bf16[8,8,4096]{2,1,0:T(8,128)(2,1)S(1)} %fusion.14), channel_id=1, replica_groups=mesh['zh'=2,'x'=4,'y'=4,'zl'=8,'c'=2] {'zl'}, dimensions={0} | all-to-all | bytes 1048576 | tf_op jit(solution)/shard_map/all_to_all | solution.py:169
  152.6 4.7 %collective-permute-start.7 = (bf16[8,4096]{1,0:T(8,128)(2,1)S(1)}, bf16[8,4096]{1,0:T(8,128)(2,1)S(1)}, u32[]{:S(2)}, u32[]{:S(2)}) collective-permute-start(bf16[8,4096]{1,0:T(8,128)(2,1)S(1)} %fusion.48), channel_id=1, source_target_pairs={{0,8},{2,10},{4,12},{6,14},{8,0},{10,2},{12,4},{14,6},{1,9},{3,11}... | collective-permute-start | bytes 196616 | tf_op jit(solution)/shard_map/ppermute | solution.py:186
  157.3 4.2 %collective-permute-done.7 = bf16[8,4096]{1,0:T(8,128)(2,1)S(1)} collective-permute-done((bf16[8,4096]{1,0:T(8,128)(2,1)S(1)}, bf16[8,4096]{1,0:T(8,128)(2,1)S(1)}, u32[]{:S(2)}, u32[]{:S(2)}) %collective-permute-start.7) | collective-permute-done | bytes 65568 | tf_op jit(solution)/shard_map/ppermute | solution.py:186
  161.6 3.7 %collective-permute-start.8 = (bf16[16,4096]{1,0:T(8,128)(2,1)S(1)}, bf16[16,4096]{1,0:T(8,128)(2,1)S(1)}, u32[]{:S(2)}, u32[]{:S(2)}) collective-permute-start(bf16[16,4096]{1,0:T(8,128)(2,1)S(1)} %maximum_select_fusion.8), channel_id=1, source_target_pairs={{0,4},{2,6},{4,0},{6,2},{8,12},{10,14},{12,8},{14,10},{1,5},{3,7},... | collective-permute-start | bytes 393224 | tf_op jit(solution)/shard_map/ppermute | solution.py:186
  165.9 10.2 %all-to-all-start.1 = ((s32[16,8,8]{2,1,0:T(8,128)}), s32[16,8,8]{2,1,0:T(8,128)S(1)}, u32[]{:S(2)}, u32[]{:S(2)}) async-start(s32[16,8,8]{2,1,0:T(8,128)} %broadcast_in_dim.166), calls=%async_computation.1 | async-start | bytes 131072 | tf_op jit(solution)/shard_map/all_to_all | solution.py:176
  176.3 3.3 %collective-permute-start.9 = (bf16[32,4096]{1,0:T(8,128)(2,1)S(1)}, bf16[32,4096]{1,0:T(8,128)(2,1)S(1)}, u32[]{:S(2)}, u32[]{:S(2)}) collective-permute-start(bf16[32,4096]{1,0:T(8,128)(2,1)S(1)} %maximum_select_fusion.6), channel_id=1, source_target_pairs={{0,2},{2,0},{4,6},{6,4},{8,10},{10,8},{12,14},{14,12},{1,3},{3,1},... | collective-permute-start | bytes 786440 | tf_op jit(solution)/shard_map/ppermute | solution.py:186
  179.8 7.3 %collective-permute-done.9 = bf16[32,4096]{1,0:T(8,128)(2,1)S(1)} collective-permute-done((bf16[32,4096]{1,0:T(8,128)(2,1)S(1)}, bf16[32,4096]{1,0:T(8,128)(2,1)S(1)}, u32[]{:S(2)}, u32[]{:S(2)}) %collective-permute-start.9) | collective-permute-done | bytes 262176 | tf_op jit(solution)/shard_map/ppermute | solution.py:186
  187.2 2.8 %collective-permute-start.10 = (bf16[64,4096]{1,0:T(8,128)(2,1)S(1)}, bf16[64,4096]{1,0:T(8,128)(2,1)S(1)}, u32[]{:S(2)}, u32[]{:S(2)}) collective-permute-start(bf16[64,4096]{1,0:T(8,128)(2,1)S(1)} %maximum_select_fusion.4), channel_id=1, source_target_pairs={{0,1},{1,0},{2,3},{3,2},{4,5},{5,4},{6,7},{7,6},{8,9},{9,8},{10,11... | collective-permute-start | bytes 1572872 | tf_op jit(solution)/shard_map/ppermute | solution.py:190
  201.5 13.3 %all-gather.2.cloned.1.call-done = bf16[1536,4096]{1,0:T(8,128)(2,1)} async-done(((bf16[96,4096]{1,0:T(8,128)(2,1)}), bf16[1536,4096]{1,0:T(8,128)(2,1)}) %all-gather.2.cloned.1.call-update) | async-done | bytes 12582928 | tf_op jit(solution)/shard_map/all_gather | solution.py:96
  214.8 7.1 %fusion.4 = f32[96,1536]{0,1:T(8,128)S(1)} fusion(bf16[1536,4096]{1,0:T(8,128)(2,1)} %all-gather.2.cloned.1.call-done, bf16[128,4096]{1,0:T(8,128)(2,1)} %slice_dynamic-update-slice_fusion, s32[128]{0:T(128)S(1)} %select_n.295), kind=kOutput, calls=%fused_computation.11 | convolution fusion | flops 1309028352 | bytes 14221824 | tf_op jit(solution)/shard_map/sd,fd->sf/dot_general | solution.py:220
  224.9 10.7 %all-to-all-start.2 = ((bf16[16,6,768]{2,1,0:T(8,128)(2,1)}), bf16[16,6,768]{2,1,0:T(8,128)(2,1)S(1)}, u32[]{:S(2)}, u32[]{:S(2)}) async-start(bf16[16,6,768]{2,1,0:T(8,128)(2,1)} %convert_element_type.96), calls=%async_computation.2 | async-start | bytes 393216 | tf_op jit(solution)/shard_map/all_to_all | solution.py:225
  235.6 14.6 %all-to-all-done.2 = bf16[16,6,768]{2,1,0:T(8,128)(2,1)S(1)} async-done(((bf16[16,6,768]{2,1,0:T(8,128)(2,1)}), bf16[16,6,768]{2,1,0:T(8,128)(2,1)S(1)}, u32[]{:S(2)}, u32[]{:S(2)}) %all-to-all-start.2) | async-done | bytes 147488 | tf_op jit(solution)/shard_map/all_to_all | solution.py:225
  (124 shorter events, 34.4 us)
Async XLA Ops:
  7.2 84.7 %copy-start = (bf16[256,4096]{1,0:T(8,128)(2,1)S(1)}, bf16[256,4096]{1,0:T(8,128)(2,1)}, u32[]{:S(2)}) copy-start(bf16[256,4096]{1,0:T(8,128)(2,1)} %param.17) | copy-start | bytes 6291460
  7.2 49.5 %copy-start.12 = (s32[64]{0:T(128)S(1)}, s32[64]{0:T(128)}, u32[]{:S(2)}) copy-start(s32[64]{0:T(128)} %param.16) | copy-start | bytes 772
  7.2 207.6 %all-gather.2.cloned.1.call-start = ((), (), s32[]{:S(2)}) async-start(), calls=%async_computation.3 | async-start | bytes 13369344 | tf_op jit(solution)/shard_map/all_gather | solution.py:96
  8.4 55.4 %copy-start.13 = (s32[32]{0:T(128)S(1)}, s32[32]{0:T(128)}, u32[]{:S(2)}) copy-start(s32[32]{0:T(128)} %constant.186) | copy-start | bytes 388
  9.4 29.0 %collective-permute-start = (bf16[212992]{0:T(1024)(128)(2,1)S(1)}, bf16[212992]{0:T(1024)(128)(2,1)S(1)}, u32[]{:S(2)}, u32[]{:S(2)}) collective-permute-start(bf16[212992]{0:T(1024)(128)(2,1)S(1)} %pad_maximum_fusion), channel_id=1, source_target_pairs={{0,256},{16,272},{32,288},{48,304},{64,320},{80,336},{96,352},{112... | collective-permute-start | bytes 1277960 | tf_op jit(solution)/shard_map/ppermute | solution.py:88
  38.4 18.4 %copy-start.2 = (bf16[212992]{0:T(1024)(128)(2,1)}, bf16[212992]{0:T(1024)(128)(2,1)S(1)}, u32[]{:S(2)}) copy-start(bf16[212992]{0:T(1024)(128)(2,1)S(1)} %collective-permute-done) | copy-start | bytes 1277956
  38.4 7.3 %collective-permute-start.1 = (bf16[256,128]{1,0:T(8,128)(2,1)S(1)}, bf16[256,128]{1,0:T(8,128)(2,1)S(1)}, u32[]{:S(2)}, u32[]{:S(2)}) collective-permute-start(bf16[256,128]{1,0:T(8,128)(2,1)S(1)} %maximum_select_fusion.9), channel_id=1, source_target_pairs={{0,128},{16,144},{32,160},{48,176},{64,192},{80,208},{96,224},{112... | collective-permute-start | bytes 196616 | tf_op jit(solution)/shard_map/ppermute | solution.py:104
  45.8 5.7 %collective-permute-start.2 = (bf16[512,128]{1,0:T(8,128)(2,1)S(1)}, bf16[512,128]{1,0:T(8,128)(2,1)S(1)}, u32[]{:S(2)}, u32[]{:S(2)}) collective-permute-start(bf16[512,128]{1,0:T(8,128)(2,1)S(1)} %maximum_select_fusion.7), channel_id=1, source_target_pairs={{0,64},{16,80},{32,96},{48,112},{64,0},{80,16},{96,32},{112,48},{1... | collective-permute-start | bytes 393224 | tf_op jit(solution)/shard_map/ppermute | solution.py:104
  51.6 8.8 %collective-permute-start.3 = (bf16[1024,128]{1,0:T(8,128)(2,1)S(1)}, bf16[1024,128]{1,0:T(8,128)(2,1)S(1)}, u32[]{:S(2)}, u32[]{:S(2)}) collective-permute-start(bf16[1024,128]{1,0:T(8,128)(2,1)S(1)} %maximum_select_fusion.5), channel_id=1, source_target_pairs={{0,32},{16,48},{32,0},{48,16},{64,96},{80,112},{96,64},{112,80},{1... | collective-permute-start | bytes 786440 | tf_op jit(solution)/shard_map/ppermute | solution.py:104
  60.4 22.6 %slice-start = ((bf16[212992]{0:T(1024)(128)(2,1)}), bf16[196608]{0:T(1024)(128)(2,1)S(1)}, s32[]{:S(2)}) async-start(bf16[212992]{0:T(1024)(128)(2,1)} %copy-done.2), calls=%async_computation.4 | async-start | bytes 786432 | tf_op jit(solution)/shard_map/slice | solution.py:89
  60.5 10.8 %collective-permute-start.4 = (bf16[2048,128]{1,0:T(8,128)(2,1)S(1)}, bf16[2048,128]{1,0:T(8,128)(2,1)}, u32[]{:S(2)}, u32[]{:S(2)}) collective-permute-start(bf16[2048,128]{1,0:T(8,128)(2,1)S(1)} %maximum_select_fusion.3), channel_id=1, source_target_pairs={{0,16},{16,0},{32,48},{48,32},{64,80},{80,64},{96,112},{112,96},{1... | collective-permute-start | bytes 1572872 | tf_op jit(solution)/shard_map/ppermute | solution.py:104
  73.1 13.3 %collective-permute-start.5 = (bf16[4096,128]{1,0:T(8,128)(2,1)S(1)}, bf16[4096,128]{1,0:T(8,128)(2,1)}, u32[]{:S(2)}, u32[]{:S(2)}) collective-permute-start(bf16[4096,128]{1,0:T(8,128)(2,1)S(1)} %maximum_select_fusion), channel_id=1, source_target_pairs={{0,1},{1,0},{2,3},{3,2},{4,5},{5,4},{6,7},{7,6},{8,9},{9,8},{10,11... | collective-permute-start | bytes 3145736 | tf_op jit(solution)/shard_map/ppermute | solution.py:108
  92.5 59.9 %copy-start.9 = (bf16[8,4096]{1,0:T(8,128)(2,1)S(1)}, bf16[8,4096]{1,0:T(8,128)(2,1)}, u32[]{:S(2)}) copy-start(bf16[8,4096]{1,0:T(8,128)(2,1)} %param.12) | copy-start | bytes 196612
  92.5 60.1 %copy-start.10 = (f32[4096]{0:T(1024)S(1)}, f32[4096]{0:T(1024)}, u32[]{:S(2)}) copy-start(f32[4096]{0:T(1024)} %param.18) | copy-start | bytes 49156
  92.5 72.8 %copy-start.8 = (s32[8,8]{1,0:T(8,128)S(1)}, s32[8,8]{1,0:T(8,128)}, u32[]{:S(2)}) copy-start(s32[8,8]{1,0:T(8,128)} %param.21) | copy-start | bytes 772
  92.5 3.9 %collective-permute-start.6 = (bf16[8,8,4096]{2,1,0:T(8,128)(2,1)S(1)}, bf16[8,8,4096]{2,1,0:T(8,128)(2,1)S(1)}, u32[]{:S(2)}, u32[]{:S(2)}) collective-permute-start(bf16[8,8,4096]{2,1,0:T(8,128)(2,1)S(1)} %fusion.27), channel_id=1, source_target_pairs={{0,1},{1,0},{2,3},{3,2},{4,5},{5,4},{6,7},{7,6},{8,9},{9,8},{10,11... | collective-permute-start | bytes 1572872 | tf_op jit(solution)/shard_map/ppermute | solution.py:166
  152.5 39.0 %copy-start.7 = (bf16[8,4096]{1,0:T(8,128)(2,1)}, bf16[8,4096]{1,0:T(8,128)(2,1)S(1)}, u32[]{:S(2)}) copy-start(bf16[8,4096]{1,0:T(8,128)(2,1)S(1)} %get-tuple-element.7) | copy-start | bytes 196612
  152.6 8.9 %collective-permute-start.7 = (bf16[8,4096]{1,0:T(8,128)(2,1)S(1)}, bf16[8,4096]{1,0:T(8,128)(2,1)S(1)}, u32[]{:S(2)}, u32[]{:S(2)}) collective-permute-start(bf16[8,4096]{1,0:T(8,128)(2,1)S(1)} %fusion.48), channel_id=1, source_target_pairs={{0,8},{2,10},{4,12},{6,14},{8,0},{10,2},{12,4},{14,6},{1,9},{3,11}... | collective-permute-start | bytes 196616 | tf_op jit(solution)/shard_map/ppermute | solution.py:186
  161.6 14.7 %collective-permute-start.8 = (bf16[16,4096]{1,0:T(8,128)(2,1)S(1)}, bf16[16,4096]{1,0:T(8,128)(2,1)S(1)}, u32[]{:S(2)}, u32[]{:S(2)}) collective-permute-start(bf16[16,4096]{1,0:T(8,128)(2,1)S(1)} %maximum_select_fusion.8), channel_id=1, source_target_pairs={{0,4},{2,6},{4,0},{6,2},{8,12},{10,14},{12,8},{14,10},{1,5},{3,7},... | collective-permute-start | bytes 393224 | tf_op jit(solution)/shard_map/ppermute | solution.py:186
  165.9 24.4 %all-to-all-start.1 = ((s32[16,8,8]{2,1,0:T(8,128)}), s32[16,8,8]{2,1,0:T(8,128)S(1)}, u32[]{:S(2)}, u32[]{:S(2)}) async-start(s32[16,8,8]{2,1,0:T(8,128)} %broadcast_in_dim.166), calls=%async_computation.1 | async-start | bytes 131072 | tf_op jit(solution)/shard_map/all_to_all | solution.py:176
  176.3 10.8 %collective-permute-start.9 = (bf16[32,4096]{1,0:T(8,128)(2,1)S(1)}, bf16[32,4096]{1,0:T(8,128)(2,1)S(1)}, u32[]{:S(2)}, u32[]{:S(2)}) collective-permute-start(bf16[32,4096]{1,0:T(8,128)(2,1)S(1)} %maximum_select_fusion.6), channel_id=1, source_target_pairs={{0,2},{2,0},{4,6},{6,4},{8,10},{10,8},{12,14},{14,12},{1,3},{3,1},... | collective-permute-start | bytes 786440 | tf_op jit(solution)/shard_map/ppermute | solution.py:186
  187.2 4.1 %collective-permute-start.10 = (bf16[64,4096]{1,0:T(8,128)(2,1)S(1)}, bf16[64,4096]{1,0:T(8,128)(2,1)S(1)}, u32[]{:S(2)}, u32[]{:S(2)}) collective-permute-start(bf16[64,4096]{1,0:T(8,128)(2,1)S(1)} %maximum_select_fusion.4), channel_id=1, source_target_pairs={{0,1},{1,0},{2,3},{3,2},{4,5},{5,4},{6,7},{7,6},{8,9},{9,8},{10,11... | collective-permute-start | bytes 1572872 | tf_op jit(solution)/shard_map/ppermute | solution.py:190
  222.0 29.0 %copy-start.11 = (f32[8,8]{1,0:T(8,128)S(1)}, f32[8,8]{1,0:T(8,128)}, u32[]{:S(2)}) copy-start(f32[8,8]{1,0:T(8,128)} %param.22) | copy-start | bytes 772
  224.9 25.3 %all-to-all-start.2 = ((bf16[16,6,768]{2,1,0:T(8,128)(2,1)}), bf16[16,6,768]{2,1,0:T(8,128)(2,1)S(1)}, u32[]{:S(2)}, u32[]{:S(2)}) async-start(bf16[16,6,768]{2,1,0:T(8,128)(2,1)} %convert_element_type.96), calls=%async_computation.2 | async-start | bytes 393216 | tf_op jit(solution)/shard_map/all_to_all | solution.py:225
  (6 other events, 10.4 us)
Sparse Core Ops, SparseCore 0:
  86.6 128.1 all-gather.1

commit v7 on v6

--- a/solution.py
+++ b/solution.py
@@ -83,11 +83,8 @@
 
     bits = doubling_bits(n_ctx)
     first = bits[0]
-    n_w = w_local.size
-    joint = jnp.concatenate([w_local.reshape(-1), kv_local.reshape(-1)])
-    joint = lax.ppermute(joint, CTX, [(i, i ^ first) for i in range(n_ctx)])
-    w_other = joint[:n_w].reshape(w_local.shape)
-    kv_other = joint[n_w:].reshape(kv_local.shape)
+    kv_other = lax.ppermute(kv_local, CTX, [(i, i ^ first) for i in range(n_ctx)])
+    w_other = lax.ppermute(w_local, "zh", [(0, 1), (1, 0)])
     w_pair = jnp.where(
         zh_index == 0,
         jnp.concatenate([w_local, w_other]),

time: 259 us -> 243 us (0.938)
  blocking collectives: 55.7 us -> 34 us
  starting transfers between devices: 78.6 us -> 99 us
  waiting for transfers between devices: 69.8 us -> 54.6 us
    all_to_all x1, blocking collectives: 55.7 us -> 34 us  [shards(): lax.all_to_all(pair_sum, 'zl', split_axis=0, concat_axis=0, tiled=True)]
    ppermute x1 -> x2, starting transfers between devices: 16.3 us -> 28.8 us  [the longest x1 16.3 us: shards(): lax.ppermute(kv_local, CTX, [(i, i ^ first) for i in range(n_ctx)])]
    ppermute x1 -> x2, waiting for transfers between devices: 12.7 us -> 1.38 us  [the longest x1 1.38 us: shards(): lax.ppermute(kv_local, CTX, [(i, i ^ first) for i in range(n_ctx)])]
    ppermute x1, starting transfers between devices: 2.07 us -> 12.6 us  [shards(): got = lax.ppermute(give, 'c', [(0, 1), (1, 0)])]
    unnamed x46 -> x43, local copies, waits for them, and re-layouts: 9.62 us -> 9.58 us
  transfers between devices with their start and end apart: 14 -> 15, of which waited for: 11 -> 10; matrix products, arithmetic and copies ran while one was open for 9% -> 11% of each run, Pallas kernels for 0% -> 0%
where the time goes in v7:
time: 243 us; the launch traced here: 242 us
  starting transfers between devices  99 us (41%)
  waiting for transfers between devices  54.6 us (22%)
  blocking collectives  34 us (14%)
  local copies, waits for them, and re-layouts  15 us (6%)
  between operations  14.6 us (6%)
  other arithmetic  14.3 us (6%)
  matrix products  10.4 us (4%)
    all_to_all x1, blocking collectives, shards(): lax.all_to_all(pair_sum, 'zl', split_axis=0, concat_axis=0, tiled=True)  34 us
    ppermute x1, starting transfers between devices, shards(): lax.ppermute(kv_local, CTX, [(i, i ^ first) for i in range(n_ctx)])  16.3 us
    ppermute x4, starting transfers between devices, shards(): other = lax.ppermute(cur, CTX, [(i, i ^ bit) for i in range(n_ctx)])  14.9 us
    all_to_all x1, waiting for transfers between devices, shards(): lax.all_to_all(hidden.astype(jnp.bfloat16), EXP, split_axis=0, concat_axi...  14.6 us
    ppermute x4, waiting for transfers between devices, shards(): other = lax.ppermute(cur, CTX, [(i, i ^ bit) for i in range(n_ctx)])  12.8 us
    ppermute x1, starting transfers between devices, shards(): got = lax.ppermute(give, 'c', [(0, 1), (1, 0)])  12.6 us
    ppermute x1, starting transfers between devices, shards(): w_other = lax.ppermute(w_local, 'zh', [(0, 1), (1, 0)])  12.5 us
    all_gather x1, waiting for transfers between devices, shards(): w_all = lax.all_gather(w_pair, ('x', 'y'), axis=0, tiled=True)  12.1 us
  transfers between devices with their start and end apart: 15, of which 10 were waited for; matrix products, arithmetic and copies ran while one was open for 11% of the time, Pallas kernels for 0%

profile of v7, /device:TPU:1, one launch (start us, length us, event | category | flops | bytes accessed | tf_op | source)
XLA Modules:
  0.0 241.9 jit_solution(12140778651035676064)
XLA Ops:
  8.2 16.3 %collective-permute-start = (bf16[128,128]{1,0:T(8,128)(2,1)S(1)}, bf16[128,128]{1,0:T(8,128)(2,1)S(1)}, u32[]{:S(2)}, u32[]{:S(2)}) collective-permute-start(bf16[128,128]{1,0:T(8,128)(2,1)S(1)} %dynamic-slice_select_fusion), channel_id=1, source_target_pairs={{0,256},{16,272},{32,288},{48,304},{64,320},{80,336},{96,352},{112... | collective-permute-start | bytes 98312 | tf_op jit(solution)/shard_map/ppermute | solution.py:86
  25.9 4.7 %collective-permute-start.1 = (bf16[256,128]{1,0:T(8,128)(2,1)S(1)}, bf16[256,128]{1,0:T(8,128)(2,1)S(1)}, u32[]{:S(2)}, u32[]{:S(2)}) collective-permute-start(bf16[256,128]{1,0:T(8,128)(2,1)S(1)} %maximum_select_fusion.9), channel_id=1, source_target_pairs={{0,128},{16,144},{32,160},{48,176},{64,192},{80,208},{96,224},{112... | collective-permute-start | bytes 196616 | tf_op jit(solution)/shard_map/ppermute | solution.py:101
  32.4 3.1 %collective-permute-start.2 = (bf16[512,128]{1,0:T(8,128)(2,1)S(1)}, bf16[512,128]{1,0:T(8,128)(2,1)S(1)}, u32[]{:S(2)}, u32[]{:S(2)}) collective-permute-start(bf16[512,128]{1,0:T(8,128)(2,1)S(1)} %maximum_select_fusion.7), channel_id=1, source_target_pairs={{0,64},{16,80},{32,96},{48,112},{64,0},{80,16},{96,32},{112,48},{1... | collective-permute-start | bytes 393224 | tf_op jit(solution)/shard_map/ppermute | solution.py:101
  35.6 2.6 %collective-permute-done.2 = bf16[512,128]{1,0:T(8,128)(2,1)S(1)} collective-permute-done((bf16[512,128]{1,0:T(8,128)(2,1)S(1)}, bf16[512,128]{1,0:T(8,128)(2,1)S(1)}, u32[]{:S(2)}, u32[]{:S(2)}) %collective-permute-start.2) | collective-permute-done | bytes 131104 | tf_op jit(solution)/shard_map/ppermute | solution.py:101
  38.2 4.8 %collective-permute-start.3 = (bf16[1024,128]{1,0:T(8,128)(2,1)S(1)}, bf16[1024,128]{1,0:T(8,128)(2,1)S(1)}, u32[]{:S(2)}, u32[]{:S(2)}) collective-permute-start(bf16[1024,128]{1,0:T(8,128)(2,1)S(1)} %maximum_select_fusion.5), channel_id=1, source_target_pairs={{0,32},{16,48},{32,0},{48,16},{64,96},{80,112},{96,64},{112,80},{1... | collective-permute-start | bytes 786440 | tf_op jit(solution)/shard_map/ppermute | solution.py:101
  44.9 12.5 %collective-permute-start.11 = (bf16[48,4096]{1,0:T(8,128)(2,1)}, bf16[48,4096]{1,0:T(8,128)(2,1)}, u32[]{:S(2)}, u32[]{:S(2)}) collective-permute-start(bf16[48,4096]{1,0:T(8,128)(2,1)} %pad_maximum_fusion), channel_id=1, source_target_pairs={{0,256},{256,0},{1,257},{257,1},{2,258},{258,2},{3,259},{259,3},{4... | collective-permute-start | bytes 1179656 | tf_op jit(solution)/shard_map/ppermute | solution.py:87
  58.2 2.3 collective-permute-start.4
  60.9 8.4 %collective-permute-done.4 = bf16[2048,128]{1,0:T(8,128)(2,1)S(1)} collective-permute-done((bf16[2048,128]{1,0:T(8,128)(2,1)S(1)}, bf16[2048,128]{1,0:T(8,128)(2,1)S(1)}, u32[]{:S(2)}, u32[]{:S(2)}) %collective-permute-start.4) | collective-permute-done | bytes 524320 | tf_op jit(solution)/shard_map/ppermute | solution.py:101
  69.5 7.2 %collective-permute-start.5 = (bf16[4096,128]{1,0:T(8,128)(2,1)S(1)}, bf16[4096,128]{1,0:T(8,128)(2,1)}, u32[]{:S(2)}, u32[]{:S(2)}) collective-permute-start(bf16[4096,128]{1,0:T(8,128)(2,1)S(1)} %maximum_select_fusion), channel_id=1, source_target_pairs={{0,1},{1,0},{2,3},{3,2},{4,5},{5,4},{6,7},{7,6},{8,9},{9,8},{10,11... | collective-permute-start | bytes 3145736 | tf_op jit(solution)/shard_map/ppermute | solution.py:105
  78.0 1.9 broadcast_compare_fusion.1
  79.9 2.2 maximum_select_fusion.2
  88.3 12.6 %collective-permute-start.6 = (bf16[8,8,4096]{2,1,0:T(8,128)(2,1)S(1)}, bf16[8,8,4096]{2,1,0:T(8,128)(2,1)S(1)}, u32[]{:S(2)}, u32[]{:S(2)}) collective-permute-start(bf16[8,8,4096]{2,1,0:T(8,128)(2,1)S(1)} %fusion.27), channel_id=1, source_target_pairs={{0,1},{1,0},{2,3},{3,2},{4,5},{5,4},{6,7},{7,6},{8,9},{9,8},{10,11... | collective-permute-start | bytes 1572872 | tf_op jit(solution)/shard_map/ppermute | solution.py:163
  102.6 34.0 %all_to_all.15 = bf16[8,8,4096]{2,1,0:T(8,128)(2,1)S(1)} all-to-all(bf16[8,8,4096]{2,1,0:T(8,128)(2,1)S(1)} %fusion.14), channel_id=1, replica_groups=mesh['zh'=2,'x'=4,'y'=4,'zl'=8,'c'=2] {'zl'}, dimensions={0} | all-to-all | bytes 1048576 | tf_op jit(solution)/shard_map/all_to_all | solution.py:166
  137.0 4.6 %collective-permute-start.7 = (bf16[8,4096]{1,0:T(8,128)(2,1)S(1)}, bf16[8,4096]{1,0:T(8,128)(2,1)S(1)}, u32[]{:S(2)}, u32[]{:S(2)}) collective-permute-start(bf16[8,4096]{1,0:T(8,128)(2,1)S(1)} %fusion.48), channel_id=1, source_target_pairs={{0,8},{2,10},{4,12},{6,14},{8,0},{10,2},{12,4},{14,6},{1,9},{3,11}... | collective-permute-start | bytes 196616 | tf_op jit(solution)/shard_map/ppermute | solution.py:183
  141.6 4.3 %collective-permute-done.7 = bf16[8,4096]{1,0:T(8,128)(2,1)S(1)} collective-permute-done((bf16[8,4096]{1,0:T(8,128)(2,1)S(1)}, bf16[8,4096]{1,0:T(8,128)(2,1)S(1)}, u32[]{:S(2)}, u32[]{:S(2)}) %collective-permute-start.7) | collective-permute-done | bytes 65568 | tf_op jit(solution)/shard_map/ppermute | solution.py:183
  145.9 3.6 %collective-permute-start.8 = (bf16[16,4096]{1,0:T(8,128)(2,1)S(1)}, bf16[16,4096]{1,0:T(8,128)(2,1)S(1)}, u32[]{:S(2)}, u32[]{:S(2)}) collective-permute-start(bf16[16,4096]{1,0:T(8,128)(2,1)S(1)} %maximum_select_fusion.8), channel_id=1, source_target_pairs={{0,4},{2,6},{4,0},{6,2},{8,12},{10,14},{12,8},{14,10},{1,5},{3,7},... | collective-permute-start | bytes 393224 | tf_op jit(solution)/shard_map/ppermute | solution.py:183
  150.2 10.6 %all-to-all-start.1 = ((s32[16,8,8]{2,1,0:T(8,128)}), s32[16,8,8]{2,1,0:T(8,128)S(1)}, u32[]{:S(2)}, u32[]{:S(2)}) async-start(s32[16,8,8]{2,1,0:T(8,128)} %broadcast_in_dim.166), calls=%async_computation.1 | async-start | bytes 131072 | tf_op jit(solution)/shard_map/all_to_all | solution.py:173
  160.9 3.3 %collective-permute-start.9 = (bf16[32,4096]{1,0:T(8,128)(2,1)S(1)}, bf16[32,4096]{1,0:T(8,128)(2,1)S(1)}, u32[]{:S(2)}, u32[]{:S(2)}) collective-permute-start(bf16[32,4096]{1,0:T(8,128)(2,1)S(1)} %maximum_select_fusion.6), channel_id=1, source_target_pairs={{0,2},{2,0},{4,6},{6,4},{8,10},{10,8},{12,14},{14,12},{1,3},{3,1},... | collective-permute-start | bytes 786440 | tf_op jit(solution)/shard_map/ppermute | solution.py:183
  164.4 7.3 %collective-permute-done.9 = bf16[32,4096]{1,0:T(8,128)(2,1)S(1)} collective-permute-done((bf16[32,4096]{1,0:T(8,128)(2,1)S(1)}, bf16[32,4096]{1,0:T(8,128)(2,1)S(1)}, u32[]{:S(2)}, u32[]{:S(2)}) %collective-permute-start.9) | collective-permute-done | bytes 262176 | tf_op jit(solution)/shard_map/ppermute | solution.py:183
  171.7 2.8 %collective-permute-start.10 = (bf16[64,4096]{1,0:T(8,128)(2,1)S(1)}, bf16[64,4096]{1,0:T(8,128)(2,1)S(1)}, u32[]{:S(2)}, u32[]{:S(2)}) collective-permute-start(bf16[64,4096]{1,0:T(8,128)(2,1)S(1)} %maximum_select_fusion.4), channel_id=1, source_target_pairs={{0,1},{1,0},{2,3},{3,2},{4,5},{5,4},{6,7},{7,6},{8,9},{9,8},{10,11... | collective-permute-start | bytes 1572872 | tf_op jit(solution)/shard_map/ppermute | solution.py:187
  186.1 12.1 %all-gather.2.cloned.1.call-done = bf16[1536,4096]{1,0:T(8,128)(2,1)} async-done(((bf16[96,4096]{1,0:T(8,128)(2,1)}), bf16[1536,4096]{1,0:T(8,128)(2,1)}) %all-gather.2.cloned.1.call-update) | async-done | bytes 12582928 | tf_op jit(solution)/shard_map/all_gather | solution.py:93
  198.1 7.1 %fusion.4 = f32[96,1536]{0,1:T(8,128)S(1)} fusion(bf16[1536,4096]{1,0:T(8,128)(2,1)} %all-gather.2.cloned.1.call-done, bf16[128,4096]{1,0:T(8,128)(2,1)} %slice_dynamic-update-slice_fusion, s32[128]{0:T(128)S(1)} %select_n.295), kind=kOutput, calls=%fused_computation.11 | convolution fusion | flops 1309028352 | bytes 14221824 | tf_op jit(solution)/shard_map/sd,fd->sf/dot_general | solution.py:217
  208.3 10.7 %all-to-all-start.2 = ((bf16[16,6,768]{2,1,0:T(8,128)(2,1)}), bf16[16,6,768]{2,1,0:T(8,128)(2,1)S(1)}, u32[]{:S(2)}, u32[]{:S(2)}) async-start(bf16[16,6,768]{2,1,0:T(8,128)(2,1)} %convert_element_type.96), calls=%async_computation.2 | async-start | bytes 393216 | tf_op jit(solution)/shard_map/all_to_all | solution.py:222
  219.0 14.6 %all-to-all-done.2 = bf16[16,6,768]{2,1,0:T(8,128)(2,1)S(1)} async-done(((bf16[16,6,768]{2,1,0:T(8,128)(2,1)}), bf16[16,6,768]{2,1,0:T(8,128)(2,1)S(1)}, u32[]{:S(2)}, u32[]{:S(2)}) %all-to-all-start.2) | async-done | bytes 147488 | tf_op jit(solution)/shard_map/all_to_all | solution.py:222
  (118 shorter events, 33.9 us)
Async XLA Ops:
  7.2 80.6 %copy-start = (bf16[256,4096]{1,0:T(8,128)(2,1)S(1)}, bf16[256,4096]{1,0:T(8,128)(2,1)}, u32[]{:S(2)}) copy-start(bf16[256,4096]{1,0:T(8,128)(2,1)} %param.17) | copy-start | bytes 6291460
  7.2 53.4 %copy-start.12 = (s32[64]{0:T(128)S(1)}, s32[64]{0:T(128)}, u32[]{:S(2)}) copy-start(s32[64]{0:T(128)} %param.16) | copy-start | bytes 772
  7.2 190.9 %all-gather.2.cloned.1.call-start = ((), (), s32[]{:S(2)}) async-start(), calls=%async_computation.3 | async-start | bytes 13369344 | tf_op jit(solution)/shard_map/all_gather | solution.py:93
  8.2 17.7 %collective-permute-start = (bf16[128,128]{1,0:T(8,128)(2,1)S(1)}, bf16[128,128]{1,0:T(8,128)(2,1)S(1)}, u32[]{:S(2)}, u32[]{:S(2)}) collective-permute-start(bf16[128,128]{1,0:T(8,128)(2,1)S(1)} %dynamic-slice_select_fusion), channel_id=1, source_target_pairs={{0,256},{16,272},{32,288},{48,304},{64,320},{80,336},{96,352},{112... | collective-permute-start | bytes 98312 | tf_op jit(solution)/shard_map/ppermute | solution.py:86
  25.9 6.5 %collective-permute-start.1 = (bf16[256,128]{1,0:T(8,128)(2,1)S(1)}, bf16[256,128]{1,0:T(8,128)(2,1)S(1)}, u32[]{:S(2)}, u32[]{:S(2)}) collective-permute-start(bf16[256,128]{1,0:T(8,128)(2,1)S(1)} %maximum_select_fusion.9), channel_id=1, source_target_pairs={{0,128},{16,144},{32,160},{48,176},{64,192},{80,208},{96,224},{112... | collective-permute-start | bytes 196616 | tf_op jit(solution)/shard_map/ppermute | solution.py:101
  32.4 5.7 %collective-permute-start.2 = (bf16[512,128]{1,0:T(8,128)(2,1)S(1)}, bf16[512,128]{1,0:T(8,128)(2,1)S(1)}, u32[]{:S(2)}, u32[]{:S(2)}) collective-permute-start(bf16[512,128]{1,0:T(8,128)(2,1)S(1)} %maximum_select_fusion.7), channel_id=1, source_target_pairs={{0,64},{16,80},{32,96},{48,112},{64,0},{80,16},{96,32},{112,48},{1... | collective-permute-start | bytes 393224 | tf_op jit(solution)/shard_map/ppermute | solution.py:101
  38.2 19.9 %collective-permute-start.3 = (bf16[1024,128]{1,0:T(8,128)(2,1)S(1)}, bf16[1024,128]{1,0:T(8,128)(2,1)S(1)}, u32[]{:S(2)}, u32[]{:S(2)}) collective-permute-start(bf16[1024,128]{1,0:T(8,128)(2,1)S(1)} %maximum_select_fusion.5), channel_id=1, source_target_pairs={{0,32},{16,48},{32,0},{48,16},{64,96},{80,112},{96,64},{112,80},{1... | collective-permute-start | bytes 786440 | tf_op jit(solution)/shard_map/ppermute | solution.py:101
  44.9 35.0 %copy-start.1 = (bf16[1,4096,24]{1,2,0:T(8,128)(2,1)S(1)}, bf16[1,4096,24]{1,2,0:T(8,128)(2,1)}, u32[]{:S(2)}) copy-start(bf16[1,4096,24]{1,2,0:T(8,128)(2,1)} %param.20) | copy-start | bytes 589828
  44.9 35.0 %copy-start.2 = (bf16[1,4096,24]{1,2,0:T(8,128)(2,1)S(1)}, bf16[1,4096,24]{1,2,0:T(8,128)(2,1)}, u32[]{:S(2)}) copy-start(bf16[1,4096,24]{1,2,0:T(8,128)(2,1)} %param.19) | copy-start | bytes 589828
  44.9 35.0 %collective-permute-start.11 = (bf16[48,4096]{1,0:T(8,128)(2,1)}, bf16[48,4096]{1,0:T(8,128)(2,1)}, u32[]{:S(2)}, u32[]{:S(2)}) collective-permute-start(bf16[48,4096]{1,0:T(8,128)(2,1)} %pad_maximum_fusion), channel_id=1, source_target_pairs={{0,256},{256,0},{1,257},{257,1},{2,258},{258,2},{3,259},{259,3},{4... | collective-permute-start | bytes 1179656 | tf_op jit(solution)/shard_map/ppermute | solution.py:87
  58.2 11.0 %collective-permute-start.4 = (bf16[2048,128]{1,0:T(8,128)(2,1)S(1)}, bf16[2048,128]{1,0:T(8,128)(2,1)S(1)}, u32[]{:S(2)}, u32[]{:S(2)}) collective-permute-start(bf16[2048,128]{1,0:T(8,128)(2,1)S(1)} %maximum_select_fusion.3), channel_id=1, source_target_pairs={{0,16},{16,0},{32,48},{48,32},{64,80},{80,64},{96,112},{112,96},{1... | collective-permute-start | bytes 1572872 | tf_op jit(solution)/shard_map/ppermute | solution.py:101
  69.5 12.7 %collective-permute-start.5 = (bf16[4096,128]{1,0:T(8,128)(2,1)S(1)}, bf16[4096,128]{1,0:T(8,128)(2,1)}, u32[]{:S(2)}, u32[]{:S(2)}) collective-permute-start(bf16[4096,128]{1,0:T(8,128)(2,1)S(1)} %maximum_select_fusion), channel_id=1, source_target_pairs={{0,1},{1,0},{2,3},{3,2},{4,5},{5,4},{6,7},{7,6},{8,9},{9,8},{10,11... | collective-permute-start | bytes 3145736 | tf_op jit(solution)/shard_map/ppermute | solution.py:105
  88.3 48.5 %copy-start.9 = (bf16[8,4096]{1,0:T(8,128)(2,1)S(1)}, bf16[8,4096]{1,0:T(8,128)(2,1)}, u32[]{:S(2)}) copy-start(bf16[8,4096]{1,0:T(8,128)(2,1)} %param.12) | copy-start | bytes 196612
  88.3 48.6 %copy-start.10 = (f32[4096]{0:T(1024)S(1)}, f32[4096]{0:T(1024)}, u32[]{:S(2)}) copy-start(f32[4096]{0:T(1024)} %param.18) | copy-start | bytes 49156
  88.3 61.3 %copy-start.8 = (s32[8,8]{1,0:T(8,128)S(1)}, s32[8,8]{1,0:T(8,128)}, u32[]{:S(2)}) copy-start(s32[8,8]{1,0:T(8,128)} %param.21) | copy-start | bytes 772
  88.3 14.1 %collective-permute-start.6 = (bf16[8,8,4096]{2,1,0:T(8,128)(2,1)S(1)}, bf16[8,8,4096]{2,1,0:T(8,128)(2,1)S(1)}, u32[]{:S(2)}, u32[]{:S(2)}) collective-permute-start(bf16[8,8,4096]{2,1,0:T(8,128)(2,1)S(1)} %fusion.27), channel_id=1, source_target_pairs={{0,1},{1,0},{2,3},{3,2},{4,5},{5,4},{6,7},{7,6},{8,9},{9,8},{10,11... | collective-permute-start | bytes 1572872 | tf_op jit(solution)/shard_map/ppermute | solution.py:163
  136.9 39.2 %copy-start.7 = (bf16[8,4096]{1,0:T(8,128)(2,1)}, bf16[8,4096]{1,0:T(8,128)(2,1)S(1)}, u32[]{:S(2)}) copy-start(bf16[8,4096]{1,0:T(8,128)(2,1)S(1)} %get-tuple-element.7) | copy-start | bytes 196612
  137.0 8.9 %collective-permute-start.7 = (bf16[8,4096]{1,0:T(8,128)(2,1)S(1)}, bf16[8,4096]{1,0:T(8,128)(2,1)S(1)}, u32[]{:S(2)}, u32[]{:S(2)}) collective-permute-start(bf16[8,4096]{1,0:T(8,128)(2,1)S(1)} %fusion.48), channel_id=1, source_target_pairs={{0,8},{2,10},{4,12},{6,14},{8,0},{10,2},{12,4},{14,6},{1,9},{3,11}... | collective-permute-start | bytes 196616 | tf_op jit(solution)/shard_map/ppermute | solution.py:183
  145.9 14.9 %collective-permute-start.8 = (bf16[16,4096]{1,0:T(8,128)(2,1)S(1)}, bf16[16,4096]{1,0:T(8,128)(2,1)S(1)}, u32[]{:S(2)}, u32[]{:S(2)}) collective-permute-start(bf16[16,4096]{1,0:T(8,128)(2,1)S(1)} %maximum_select_fusion.8), channel_id=1, source_target_pairs={{0,4},{2,6},{4,0},{6,2},{8,12},{10,14},{12,8},{14,10},{1,5},{3,7},... | collective-permute-start | bytes 393224 | tf_op jit(solution)/shard_map/ppermute | solution.py:183
  150.2 24.7 %all-to-all-start.1 = ((s32[16,8,8]{2,1,0:T(8,128)}), s32[16,8,8]{2,1,0:T(8,128)S(1)}, u32[]{:S(2)}, u32[]{:S(2)}) async-start(s32[16,8,8]{2,1,0:T(8,128)} %broadcast_in_dim.166), calls=%async_computation.1 | async-start | bytes 131072 | tf_op jit(solution)/shard_map/all_to_all | solution.py:173
  160.9 10.7 %collective-permute-start.9 = (bf16[32,4096]{1,0:T(8,128)(2,1)S(1)}, bf16[32,4096]{1,0:T(8,128)(2,1)S(1)}, u32[]{:S(2)}, u32[]{:S(2)}) collective-permute-start(bf16[32,4096]{1,0:T(8,128)(2,1)S(1)} %maximum_select_fusion.6), channel_id=1, source_target_pairs={{0,2},{2,0},{4,6},{6,4},{8,10},{10,8},{12,14},{14,12},{1,3},{3,1},... | collective-permute-start | bytes 786440 | tf_op jit(solution)/shard_map/ppermute | solution.py:183
  171.7 4.1 %collective-permute-start.10 = (bf16[64,4096]{1,0:T(8,128)(2,1)S(1)}, bf16[64,4096]{1,0:T(8,128)(2,1)S(1)}, u32[]{:S(2)}, u32[]{:S(2)}) collective-permute-start(bf16[64,4096]{1,0:T(8,128)(2,1)S(1)} %maximum_select_fusion.4), channel_id=1, source_target_pairs={{0,1},{1,0},{2,3},{3,2},{4,5},{5,4},{6,7},{7,6},{8,9},{9,8},{10,11... | collective-permute-start | bytes 1572872 | tf_op jit(solution)/shard_map/ppermute | solution.py:187
  205.4 29.0 %copy-start.11 = (f32[8,8]{1,0:T(8,128)S(1)}, f32[8,8]{1,0:T(8,128)}, u32[]{:S(2)}) copy-start(f32[8,8]{1,0:T(8,128)} %param.22) | copy-start | bytes 772
  208.3 25.3 %all-to-all-start.2 = ((bf16[16,6,768]{2,1,0:T(8,128)(2,1)}), bf16[16,6,768]{2,1,0:T(8,128)(2,1)S(1)}, u32[]{:S(2)}, u32[]{:S(2)}) async-start(bf16[16,6,768]{2,1,0:T(8,128)(2,1)} %convert_element_type.96), calls=%async_computation.2 | async-start | bytes 393216 | tf_op jit(solution)/shard_map/all_to_all | solution.py:222
  (5 other events, 7.3 us)
Sparse Core Ops, SparseCore 0:
  82.2 115.8 all-gather.1

commit v8 on v7

--- a/solution.py
+++ b/solution.py
@@ -97,11 +97,13 @@
         low, jnp.concatenate([kv_local, kv_other]), jnp.concatenate([kv_other, kv_local])
     )
     order = [0, first]
-    for bit in bits[1:]:
+    for step, bit in enumerate(bits[1:]):
         other = lax.ppermute(cur, CTX, [(i, i ^ bit) for i in range(n_ctx)])
         low = (ctx_index & bit) == 0
         cur = jnp.where(low, jnp.concatenate([cur, other]), jnp.concatenate([other, cur]))
         order = order + [o + bit for o in order]
+        if step == 0:
+            w_pair, cur = lax.optimization_barrier((w_pair, cur))
     partner = lax.ppermute(cur, "c", [(0, 1), (1, 0)])
     key_piece = jnp.where(core_index == 0, cur, partner)
     value_piece = jnp.where(core_index == 0, partner, cur)

time: 243 us -> 257 us (1.058)
  blocking collectives: 34 us -> 54.1 us
  starting transfers between devices: 99 us -> 79.6 us
  waiting for transfers between devices: 54.6 us -> 69.9 us
    all_to_all x1, blocking collectives: 34 us -> 54.1 us  [shards(): lax.all_to_all(pair_sum, 'zl', split_axis=0, concat_axis=0, tiled=True)]
    ppermute x1, starting transfers between devices: 16.3 us -> 1.92 us  [shards(): lax.ppermute(kv_local, CTX, [(i, i ^ first) for i in range(n_ctx)])]
    ppermute x1, waiting for transfers between devices: 1.38 us -> 11.7 us  [shards(): lax.ppermute(kv_local, CTX, [(i, i ^ first) for i in range(n_ctx)])]
    ppermute x1, starting transfers between devices: 12.6 us -> 2.41 us  [shards(): got = lax.ppermute(give, 'c', [(0, 1), (1, 0)])]
    ppermute x1, starting transfers between devices: 12.5 us -> 16.3 us  [shards(): w_other = lax.ppermute(w_local, 'zh', [(0, 1), (1, 0)])]
    ppermute x4, waiting for transfers between devices: 12.8 us -> 16.2 us  [shards(): other = lax.ppermute(cur, CTX, [(i, i ^ bit) for i in range(n_ctx)])]
    unnamed x43 -> x37, local copies, waits for them, and re-layouts: 9.58 us -> 9.4 us
  transfers between devices with their start and end apart: 15 -> 15, of which waited for: 10 -> 12; matrix products, arithmetic and copies ran while one was open for 11% -> 8% of each run, Pallas kernels for 0% -> 0%
where the time goes in v8:
time: 257 us; the launch traced here: 256 us
  starting transfers between devices  79.6 us (31%)
  waiting for transfers between devices  69.9 us (27%)
  blocking collectives  54.1 us (21%)
  local copies, waits for them, and re-layouts  14.8 us (6%)
  between operations  14.6 us (6%)
  other arithmetic  13.1 us (5%)
  matrix products  10.4 us (4%)
    all_to_all x1, blocking collectives, shards(): lax.all_to_all(pair_sum, 'zl', split_axis=0, concat_axis=0, tiled=True)  54.1 us
    ppermute x1, starting transfers between devices, shards(): w_other = lax.ppermute(w_local, 'zh', [(0, 1), (1, 0)])  16.3 us
    ppermute x4, waiting for transfers between devices, shards(): other = lax.ppermute(cur, CTX, [(i, i ^ bit) for i in range(n_ctx)])  16.2 us
    ppermute x4, starting transfers between devices, shards(): other = lax.ppermute(cur, CTX, [(i, i ^ bit) for i in range(n_ctx)])  15.8 us
    all_to_all x1, waiting for transfers between devices, shards(): lax.all_to_all(hidden.astype(jnp.bfloat16), EXP, split_axis=0, concat_axi...  14.6 us
    all_gather x1, waiting for transfers between devices, shards(): w_all = lax.all_gather(w_pair, ('x', 'y'), axis=0, tiled=True)  13.4 us
    ppermute x1, waiting for transfers between devices, shards(): lax.ppermute(kv_local, CTX, [(i, i ^ first) for i in range(n_ctx)])  11.7 us
    ppermute x3, waiting for transfers between devices, shards(): other = lax.ppermute(cur, 'zl', [(i, i ^ bit) for i in range(n_zl)])  11.6 us
  transfers between devices with their start and end apart: 15, of which 12 were waited for; matrix products, arithmetic and copies ran while one was open for 8% of the time, Pallas kernels for 0%

profile of v8, /device:TPU:1, one launch (start us, length us, event | category | flops | bytes accessed | tf_op | source)
XLA Modules:
  0.0 256.4 jit_solution(2174602915216212224)
XLA Ops:
  8.4 16.3 %collective-permute-start = (bf16[48,4096]{1,0:T(8,128)(2,1)S(1)}, bf16[48,4096]{1,0:T(8,128)(2,1)S(1)}, u32[]{:S(2)}, u32[]{:S(2)}) collective-permute-start(bf16[48,4096]{1,0:T(8,128)(2,1)S(1)} %pad_maximum_fusion), channel_id=1, source_target_pairs={{0,256},{256,0},{1,257},{257,1},{2,258},{258,2},{3,259},{259,3},{4... | collective-permute-start | bytes 1179656 | tf_op jit(solution)/shard_map/ppermute | solution.py:87
  27.5 11.7 %collective-permute-done.1 = bf16[128,128]{1,0:T(8,128)(2,1)S(1)} collective-permute-done((bf16[128,128]{1,0:T(8,128)(2,1)S(1)}, bf16[128,128]{1,0:T(8,128)(2,1)S(1)}, u32[]{:S(2)}, u32[]{:S(2)}) %collective-permute-start.1) | collective-permute-done | bytes 32800 | tf_op jit(solution)/shard_map/ppermute | solution.py:86
  39.2 4.7 %collective-permute-start.2 = (bf16[256,128]{1,0:T(8,128)(2,1)S(1)}, bf16[256,128]{1,0:T(8,128)(2,1)S(1)}, u32[]{:S(2)}, u32[]{:S(2)}) collective-permute-start(bf16[256,128]{1,0:T(8,128)(2,1)S(1)} %maximum_select_fusion.9), channel_id=1, source_target_pairs={{0,128},{16,144},{32,160},{48,176},{64,192},{80,208},{96,224},{112... | collective-permute-start | bytes 196616 | tf_op jit(solution)/shard_map/ppermute | solution.py:101
  45.7 2.3 maximum_select_fusion.2
  48.0 3.1 %collective-permute-start.3 = (bf16[512,128]{1,0:T(8,128)(2,1)S(1)}, bf16[512,128]{1,0:T(8,128)(2,1)S(1)}, u32[]{:S(2)}, u32[]{:S(2)}) collective-permute-start(bf16[512,128]{1,0:T(8,128)(2,1)S(1)} %maximum_select_fusion.7), channel_id=1, source_target_pairs={{0,64},{16,80},{32,96},{48,112},{64,0},{80,16},{96,32},{112,48},{1... | collective-permute-start | bytes 393224 | tf_op jit(solution)/shard_map/ppermute | solution.py:101
  51.1 2.6 %collective-permute-done.3 = bf16[512,128]{1,0:T(8,128)(2,1)S(1)} collective-permute-done((bf16[512,128]{1,0:T(8,128)(2,1)S(1)}, bf16[512,128]{1,0:T(8,128)(2,1)S(1)}, u32[]{:S(2)}, u32[]{:S(2)}) %collective-permute-start.3) | collective-permute-done | bytes 131104 | tf_op jit(solution)/shard_map/ppermute | solution.py:101
  53.8 4.8 %collective-permute-start.4 = (bf16[1024,128]{1,0:T(8,128)(2,1)S(1)}, bf16[1024,128]{1,0:T(8,128)(2,1)S(1)}, u32[]{:S(2)}, u32[]{:S(2)}) collective-permute-start(bf16[1024,128]{1,0:T(8,128)(2,1)S(1)} %maximum_select_fusion.5), channel_id=1, source_target_pairs={{0,32},{16,48},{32,0},{48,16},{64,96},{80,112},{96,64},{112,80},{1... | collective-permute-start | bytes 786440 | tf_op jit(solution)/shard_map/ppermute | solution.py:101
  58.6 3.8 %collective-permute-done.4 = bf16[1024,128]{1,0:T(8,128)(2,1)S(1)} collective-permute-done((bf16[1024,128]{1,0:T(8,128)(2,1)S(1)}, bf16[1024,128]{1,0:T(8,128)(2,1)S(1)}, u32[]{:S(2)}, u32[]{:S(2)}) %collective-permute-start.4) | collective-permute-done | bytes 262176 | tf_op jit(solution)/shard_map/ppermute | solution.py:101
  62.6 3.2 %collective-permute-start.5 = (bf16[2048,128]{1,0:T(8,128)(2,1)S(1)}, bf16[2048,128]{1,0:T(8,128)(2,1)}, u32[]{:S(2)}, u32[]{:S(2)}) collective-permute-start(bf16[2048,128]{1,0:T(8,128)(2,1)S(1)} %maximum_select_fusion.3), channel_id=1, source_target_pairs={{0,16},{16,0},{32,48},{48,32},{64,80},{80,64},{96,112},{112,96},{1... | collective-permute-start | bytes 1572872 | tf_op jit(solution)/shard_map/ppermute | solution.py:101
  66.0 8.0 %collective-permute-done.5 = bf16[2048,128]{1,0:T(8,128)(2,1)} collective-permute-done((bf16[2048,128]{1,0:T(8,128)(2,1)S(1)}, bf16[2048,128]{1,0:T(8,128)(2,1)}, u32[]{:S(2)}, u32[]{:S(2)}) %collective-permute-start.5) | collective-permute-done | bytes 524320 | tf_op jit(solution)/shard_map/ppermute | solution.py:101
  75.8 7.6 %collective-permute-start.6 = (bf16[4096,128]{1,0:T(8,128)(2,1)S(1)}, bf16[4096,128]{1,0:T(8,128)(2,1)}, u32[]{:S(2)}, u32[]{:S(2)}) collective-permute-start(bf16[4096,128]{1,0:T(8,128)(2,1)S(1)} %maximum_select_fusion), channel_id=1, source_target_pairs={{0,1},{1,0},{2,3},{3,2},{4,5},{5,4},{6,7},{7,6},{8,9},{9,8},{10,11... | collective-permute-start | bytes 3145736 | tf_op jit(solution)/shard_map/ppermute | solution.py:107
  91.6 2.4 collective-permute-start.7
  95.8 54.1 %all_to_all.15 = bf16[8,8,4096]{2,1,0:T(8,128)(2,1)S(1)} all-to-all(bf16[8,8,4096]{2,1,0:T(8,128)(2,1)S(1)} %fusion.14), channel_id=1, replica_groups=mesh['zh'=2,'x'=4,'y'=4,'zl'=8,'c'=2] {'zl'}, dimensions={0} | all-to-all | bytes 1048576 | tf_op jit(solution)/shard_map/all_to_all | solution.py:168
  150.2 4.6 %collective-permute-start.8 = (bf16[8,4096]{1,0:T(8,128)(2,1)S(1)}, bf16[8,4096]{1,0:T(8,128)(2,1)S(1)}, u32[]{:S(2)}, u32[]{:S(2)}) collective-permute-start(bf16[8,4096]{1,0:T(8,128)(2,1)S(1)} %fusion.48), channel_id=1, source_target_pairs={{0,8},{2,10},{4,12},{6,14},{8,0},{10,2},{12,4},{14,6},{1,9},{3,11}... | collective-permute-start | bytes 196616 | tf_op jit(solution)/shard_map/ppermute | solution.py:185
  154.8 4.3 %collective-permute-done.8 = bf16[8,4096]{1,0:T(8,128)(2,1)S(1)} collective-permute-done((bf16[8,4096]{1,0:T(8,128)(2,1)S(1)}, bf16[8,4096]{1,0:T(8,128)(2,1)S(1)}, u32[]{:S(2)}, u32[]{:S(2)}) %collective-permute-start.8) | collective-permute-done | bytes 65568 | tf_op jit(solution)/shard_map/ppermute | solution.py:185
  159.1 3.6 %collective-permute-start.9 = (bf16[16,4096]{1,0:T(8,128)(2,1)S(1)}, bf16[16,4096]{1,0:T(8,128)(2,1)S(1)}, u32[]{:S(2)}, u32[]{:S(2)}) collective-permute-start(bf16[16,4096]{1,0:T(8,128)(2,1)S(1)} %maximum_select_fusion.8), channel_id=1, source_target_pairs={{0,4},{2,6},{4,0},{6,2},{8,12},{10,14},{12,8},{14,10},{1,5},{3,7},... | collective-permute-start | bytes 393224 | tf_op jit(solution)/shard_map/ppermute | solution.py:185
  163.4 10.6 %all-to-all-start.1 = ((s32[16,8,8]{2,1,0:T(8,128)}), s32[16,8,8]{2,1,0:T(8,128)S(1)}, u32[]{:S(2)}, u32[]{:S(2)}) async-start(s32[16,8,8]{2,1,0:T(8,128)} %broadcast_in_dim.166), calls=%async_computation.1 | async-start | bytes 131072 | tf_op jit(solution)/shard_map/all_to_all | solution.py:175
  174.1 3.3 %collective-permute-start.10 = (bf16[32,4096]{1,0:T(8,128)(2,1)S(1)}, bf16[32,4096]{1,0:T(8,128)(2,1)S(1)}, u32[]{:S(2)}, u32[]{:S(2)}) collective-permute-start(bf16[32,4096]{1,0:T(8,128)(2,1)S(1)} %maximum_select_fusion.6), channel_id=1, source_target_pairs={{0,2},{2,0},{4,6},{6,4},{8,10},{10,8},{12,14},{14,12},{1,3},{3,1},... | collective-permute-start | bytes 786440 | tf_op jit(solution)/shard_map/ppermute | solution.py:185
  177.6 7.3 %collective-permute-done.10 = bf16[32,4096]{1,0:T(8,128)(2,1)S(1)} collective-permute-done((bf16[32,4096]{1,0:T(8,128)(2,1)S(1)}, bf16[32,4096]{1,0:T(8,128)(2,1)S(1)}, u32[]{:S(2)}, u32[]{:S(2)}) %collective-permute-start.10) | collective-permute-done | bytes 262176 | tf_op jit(solution)/shard_map/ppermute | solution.py:185
  184.9 2.8 %collective-permute-start.11 = (bf16[64,4096]{1,0:T(8,128)(2,1)S(1)}, bf16[64,4096]{1,0:T(8,128)(2,1)S(1)}, u32[]{:S(2)}, u32[]{:S(2)}) collective-permute-start(bf16[64,4096]{1,0:T(8,128)(2,1)S(1)} %maximum_select_fusion.4), channel_id=1, source_target_pairs={{0,1},{1,0},{2,3},{3,2},{4,5},{5,4},{6,7},{7,6},{8,9},{9,8},{10,11... | collective-permute-start | bytes 1572872 | tf_op jit(solution)/shard_map/ppermute | solution.py:189
  199.3 13.4 %all-gather.2.cloned.1.call-done = bf16[1536,4096]{1,0:T(8,128)(2,1)} async-done(((bf16[96,4096]{1,0:T(8,128)(2,1)}), bf16[1536,4096]{1,0:T(8,128)(2,1)}) %all-gather.2.cloned.1.call-update) | async-done | bytes 12582928 | tf_op jit(solution)/shard_map/all_gather | solution.py:93
  212.6 7.1 %fusion.4 = f32[96,1536]{0,1:T(8,128)S(1)} fusion(bf16[1536,4096]{1,0:T(8,128)(2,1)} %all-gather.2.cloned.1.call-done, bf16[128,4096]{1,0:T(8,128)(2,1)} %slice_dynamic-update-slice_fusion, s32[128]{0:T(128)S(1)} %select_n.297), kind=kOutput, calls=%fused_computation.11 | convolution fusion | flops 1309028352 | bytes 14221824 | tf_op jit(solution)/shard_map/sd,fd->sf/dot_general | solution.py:219
  222.8 10.7 %all-to-all-start.2 = ((bf16[16,6,768]{2,1,0:T(8,128)(2,1)}), bf16[16,6,768]{2,1,0:T(8,128)(2,1)S(1)}, u32[]{:S(2)}, u32[]{:S(2)}) async-start(bf16[16,6,768]{2,1,0:T(8,128)(2,1)} %convert_element_type.96), calls=%async_computation.2 | async-start | bytes 393216 | tf_op jit(solution)/shard_map/all_to_all | solution.py:224
  233.5 14.6 %all-to-all-done.2 = bf16[16,6,768]{2,1,0:T(8,128)(2,1)S(1)} async-done(((bf16[16,6,768]{2,1,0:T(8,128)(2,1)}), bf16[16,6,768]{2,1,0:T(8,128)(2,1)S(1)}, u32[]{:S(2)}, u32[]{:S(2)}) %all-to-all-start.2) | async-done | bytes 147488 | tf_op jit(solution)/shard_map/all_to_all | solution.py:224
  (112 shorter events, 35.1 us)
Async XLA Ops:
  7.2 83.9 %copy-start = (bf16[256,4096]{1,0:T(8,128)(2,1)S(1)}, bf16[256,4096]{1,0:T(8,128)(2,1)}, u32[]{:S(2)}) copy-start(bf16[256,4096]{1,0:T(8,128)(2,1)} %param.17) | copy-start | bytes 6291460
  7.2 205.4 %all-gather.2.cloned.1.call-start = ((), (), s32[]{:S(2)}) async-start(), calls=%async_computation.3 | async-start | bytes 13369344 | tf_op jit(solution)/shard_map/all_gather | solution.py:93
  7.2 58.6 %copy-start.8 = (s32[64]{0:T(128)S(1)}, s32[64]{0:T(128)}, u32[]{:S(2)}) copy-start(s32[64]{0:T(128)} %param.16) | copy-start | bytes 772
  7.2 58.7 %copy-start.9 = (s32[32]{0:T(128)S(1)}, s32[32]{0:T(128)}, u32[]{:S(2)}) copy-start(s32[32]{0:T(128)} %constant.186) | copy-start | bytes 388
  8.4 37.3 %collective-permute-start = (bf16[48,4096]{1,0:T(8,128)(2,1)S(1)}, bf16[48,4096]{1,0:T(8,128)(2,1)S(1)}, u32[]{:S(2)}, u32[]{:S(2)}) collective-permute-start(bf16[48,4096]{1,0:T(8,128)(2,1)S(1)} %pad_maximum_fusion), channel_id=1, source_target_pairs={{0,256},{256,0},{1,257},{257,1},{2,258},{258,2},{3,259},{259,3},{4... | collective-permute-start | bytes 1179656 | tf_op jit(solution)/shard_map/ppermute | solution.py:87
  25.5 13.6 %collective-permute-start.1 = (bf16[128,128]{1,0:T(8,128)(2,1)S(1)}, bf16[128,128]{1,0:T(8,128)(2,1)S(1)}, u32[]{:S(2)}, u32[]{:S(2)}) collective-permute-start(bf16[128,128]{1,0:T(8,128)(2,1)S(1)} %dynamic-slice_select_fusion), channel_id=1, source_target_pairs={{0,256},{16,272},{32,288},{48,304},{64,320},{80,336},{96,352},{112... | collective-permute-start | bytes 98312 | tf_op jit(solution)/shard_map/ppermute | solution.py:86
  39.2 6.5 %collective-permute-start.2 = (bf16[256,128]{1,0:T(8,128)(2,1)S(1)}, bf16[256,128]{1,0:T(8,128)(2,1)S(1)}, u32[]{:S(2)}, u32[]{:S(2)}) collective-permute-start(bf16[256,128]{1,0:T(8,128)(2,1)S(1)} %maximum_select_fusion.9), channel_id=1, source_target_pairs={{0,128},{16,144},{32,160},{48,176},{64,192},{80,208},{96,224},{112... | collective-permute-start | bytes 196616 | tf_op jit(solution)/shard_map/ppermute | solution.py:101
  48.0 5.7 %collective-permute-start.3 = (bf16[512,128]{1,0:T(8,128)(2,1)S(1)}, bf16[512,128]{1,0:T(8,128)(2,1)S(1)}, u32[]{:S(2)}, u32[]{:S(2)}) collective-permute-start(bf16[512,128]{1,0:T(8,128)(2,1)S(1)} %maximum_select_fusion.7), channel_id=1, source_target_pairs={{0,64},{16,80},{32,96},{48,112},{64,0},{80,16},{96,32},{112,48},{1... | collective-permute-start | bytes 393224 | tf_op jit(solution)/shard_map/ppermute | solution.py:101
  53.8 8.6 %collective-permute-start.4 = (bf16[1024,128]{1,0:T(8,128)(2,1)S(1)}, bf16[1024,128]{1,0:T(8,128)(2,1)S(1)}, u32[]{:S(2)}, u32[]{:S(2)}) collective-permute-start(bf16[1024,128]{1,0:T(8,128)(2,1)S(1)} %maximum_select_fusion.5), channel_id=1, source_target_pairs={{0,32},{16,48},{32,0},{48,16},{64,96},{80,112},{96,64},{112,80},{1... | collective-permute-start | bytes 786440 | tf_op jit(solution)/shard_map/ppermute | solution.py:101
  62.6 3.4 %copy-start.1 = (bf16[2048,128]{1,0:T(8,128)(2,1)}, bf16[2048,128]{1,0:T(8,128)(2,1)S(1)}, u32[]{:S(2)}) copy-start(bf16[2048,128]{1,0:T(8,128)(2,1)S(1)} %maximum_select_fusion.3) | copy-start | bytes 1572868
  62.6 11.4 %collective-permute-start.5 = (bf16[2048,128]{1,0:T(8,128)(2,1)S(1)}, bf16[2048,128]{1,0:T(8,128)(2,1)}, u32[]{:S(2)}, u32[]{:S(2)}) collective-permute-start(bf16[2048,128]{1,0:T(8,128)(2,1)S(1)} %maximum_select_fusion.3), channel_id=1, source_target_pairs={{0,16},{16,0},{32,48},{48,32},{64,80},{80,64},{96,112},{112,96},{1... | collective-permute-start | bytes 1572872 | tf_op jit(solution)/shard_map/ppermute | solution.py:101
  75.8 10.0 %collective-permute-start.6 = (bf16[4096,128]{1,0:T(8,128)(2,1)S(1)}, bf16[4096,128]{1,0:T(8,128)(2,1)}, u32[]{:S(2)}, u32[]{:S(2)}) collective-permute-start(bf16[4096,128]{1,0:T(8,128)(2,1)S(1)} %maximum_select_fusion), channel_id=1, source_target_pairs={{0,1},{1,0},{2,3},{3,2},{4,5},{5,4},{6,7},{7,6},{8,9},{9,8},{10,11... | collective-permute-start | bytes 3145736 | tf_op jit(solution)/shard_map/ppermute | solution.py:107
  91.6 58.3 %copy-start.5 = (bf16[8,4096]{1,0:T(8,128)(2,1)S(1)}, bf16[8,4096]{1,0:T(8,128)(2,1)}, u32[]{:S(2)}) copy-start(bf16[8,4096]{1,0:T(8,128)(2,1)} %param.12) | copy-start | bytes 196612
  91.6 58.5 %copy-start.6 = (f32[4096]{0:T(1024)S(1)}, f32[4096]{0:T(1024)}, u32[]{:S(2)}) copy-start(f32[4096]{0:T(1024)} %param.18) | copy-start | bytes 49156
  91.6 71.1 %copy-start.4 = (s32[8,8]{1,0:T(8,128)S(1)}, s32[8,8]{1,0:T(8,128)}, u32[]{:S(2)}) copy-start(s32[8,8]{1,0:T(8,128)} %param.21) | copy-start | bytes 772
  91.6 3.9 %collective-permute-start.7 = (bf16[8,8,4096]{2,1,0:T(8,128)(2,1)S(1)}, bf16[8,8,4096]{2,1,0:T(8,128)(2,1)S(1)}, u32[]{:S(2)}, u32[]{:S(2)}) collective-permute-start(bf16[8,8,4096]{2,1,0:T(8,128)(2,1)S(1)} %fusion.27), channel_id=1, source_target_pairs={{0,1},{1,0},{2,3},{3,2},{4,5},{5,4},{6,7},{7,6},{8,9},{9,8},{10,11... | collective-permute-start | bytes 1572872 | tf_op jit(solution)/shard_map/ppermute | solution.py:165
  150.1 39.2 %copy-start.3 = (bf16[8,4096]{1,0:T(8,128)(2,1)}, bf16[8,4096]{1,0:T(8,128)(2,1)S(1)}, u32[]{:S(2)}) copy-start(bf16[8,4096]{1,0:T(8,128)(2,1)S(1)} %get-tuple-element.9) | copy-start | bytes 196612
  150.2 8.9 %collective-permute-start.8 = (bf16[8,4096]{1,0:T(8,128)(2,1)S(1)}, bf16[8,4096]{1,0:T(8,128)(2,1)S(1)}, u32[]{:S(2)}, u32[]{:S(2)}) collective-permute-start(bf16[8,4096]{1,0:T(8,128)(2,1)S(1)} %fusion.48), channel_id=1, source_target_pairs={{0,8},{2,10},{4,12},{6,14},{8,0},{10,2},{12,4},{14,6},{1,9},{3,11}... | collective-permute-start | bytes 196616 | tf_op jit(solution)/shard_map/ppermute | solution.py:185
  159.1 14.9 %collective-permute-start.9 = (bf16[16,4096]{1,0:T(8,128)(2,1)S(1)}, bf16[16,4096]{1,0:T(8,128)(2,1)S(1)}, u32[]{:S(2)}, u32[]{:S(2)}) collective-permute-start(bf16[16,4096]{1,0:T(8,128)(2,1)S(1)} %maximum_select_fusion.8), channel_id=1, source_target_pairs={{0,4},{2,6},{4,0},{6,2},{8,12},{10,14},{12,8},{14,10},{1,5},{3,7},... | collective-permute-start | bytes 393224 | tf_op jit(solution)/shard_map/ppermute | solution.py:185
  163.4 24.7 %all-to-all-start.1 = ((s32[16,8,8]{2,1,0:T(8,128)}), s32[16,8,8]{2,1,0:T(8,128)S(1)}, u32[]{:S(2)}, u32[]{:S(2)}) async-start(s32[16,8,8]{2,1,0:T(8,128)} %broadcast_in_dim.166), calls=%async_computation.1 | async-start | bytes 131072 | tf_op jit(solution)/shard_map/all_to_all | solution.py:175
  174.1 10.7 %collective-permute-start.10 = (bf16[32,4096]{1,0:T(8,128)(2,1)S(1)}, bf16[32,4096]{1,0:T(8,128)(2,1)S(1)}, u32[]{:S(2)}, u32[]{:S(2)}) collective-permute-start(bf16[32,4096]{1,0:T(8,128)(2,1)S(1)} %maximum_select_fusion.6), channel_id=1, source_target_pairs={{0,2},{2,0},{4,6},{6,4},{8,10},{10,8},{12,14},{14,12},{1,3},{3,1},... | collective-permute-start | bytes 786440 | tf_op jit(solution)/shard_map/ppermute | solution.py:185
  184.9 4.1 %collective-permute-start.11 = (bf16[64,4096]{1,0:T(8,128)(2,1)S(1)}, bf16[64,4096]{1,0:T(8,128)(2,1)S(1)}, u32[]{:S(2)}, u32[]{:S(2)}) collective-permute-start(bf16[64,4096]{1,0:T(8,128)(2,1)S(1)} %maximum_select_fusion.4), channel_id=1, source_target_pairs={{0,1},{1,0},{2,3},{3,2},{4,5},{5,4},{6,7},{7,6},{8,9},{9,8},{10,11... | collective-permute-start | bytes 1572872 | tf_op jit(solution)/shard_map/ppermute | solution.py:189
  219.9 29.0 %copy-start.7 = (f32[8,8]{1,0:T(8,128)S(1)}, f32[8,8]{1,0:T(8,128)}, u32[]{:S(2)}) copy-start(f32[8,8]{1,0:T(8,128)} %param.22) | copy-start | bytes 772
  222.8 25.3 %all-to-all-start.2 = ((bf16[16,6,768]{2,1,0:T(8,128)(2,1)}), bf16[16,6,768]{2,1,0:T(8,128)(2,1)S(1)}, u32[]{:S(2)}, u32[]{:S(2)}) async-start(bf16[16,6,768]{2,1,0:T(8,128)(2,1)} %convert_element_type.96), calls=%async_computation.2 | async-start | bytes 393216 | tf_op jit(solution)/shard_map/all_to_all | solution.py:224
  (2 other events, 2.7 us)
Sparse Core Ops, SparseCore 0:
  85.7 126.8 all-gather.1

commit v9 on v7

--- a/solution.py
+++ b/solution.py
@@ -195,7 +195,7 @@
     gathered = jnp.concatenate(blocks)
     normed_all = gathered
 
-    most_slots = 3 * tok_dev // 4
+    most_slots = tok_dev
     chosen = jnp.any(ids_all == exp_index, axis=1).astype(jnp.int32).reshape(n_exp, tok_dev)
     rank = jnp.cumsum(chosen, axis=1) - chosen
     dest = jnp.where(
@@ -214,12 +214,13 @@
     slot = jnp.sum(earlier * onehot, axis=1)
     target = ids_flat * most_slots + slot
 
-    proj = jnp.einsum("sd,fd->sf", received, w_all, preferred_element_type=jnp.float32)
-    proj = proj.reshape(EXPERTS * most_slots, n_xy, n_zh, 2, fe_dev)
-    hidden = jax.nn.silu(proj[:, :, :, 0]) * proj[:, :, :, 1]
-    hidden = jnp.transpose(hidden, (0, 2, 1, 3)).reshape(EXPERTS, most_slots, FE)
+    proj = jnp.einsum("fd,sd->fs", w_all, received, preferred_element_type=jnp.float32)
+    proj = proj.reshape(n_xy, n_zh, 2, fe_dev, EXPERTS * most_slots)
+    hidden = jax.nn.silu(proj[:, :, 0]) * proj[:, :, 1]
+    hidden = jnp.transpose(hidden, (1, 0, 2, 3)).reshape(FE, EXPERTS * most_slots)
+    hidden = hidden.astype(jnp.bfloat16).T.reshape(EXPERTS, most_slots, FE)
     returned = (
-        lax.all_to_all(hidden.astype(jnp.bfloat16), EXP, split_axis=0, concat_axis=0, tiled=True)
+        lax.all_to_all(hidden, EXP, split_axis=0, concat_axis=0, tiled=True)
         .astype(jnp.float32)
         .reshape(EXPERTS * most_slots, FE)
     )

time: 243 us -> 241 us (level)
    all_to_all x1, waiting for transfers between devices: 0.01 us -> 7.79 us  [shards(): lax.all_to_all(jnp.broadcast_to(expert_ids[None], (n_exp,) + expert_ids.s...]
    all_gather x1, waiting for transfers between devices: 12.1 us -> 7.19 us  [shards(): w_all = lax.all_gather(w_pair, ('x', 'y'), axis=0, tiled=True)]
    ppermute x3, waiting for transfers between devices: 11.6 us -> 8.26 us  [shards(): other = lax.ppermute(cur, 'zl', [(i, i ^ bit) for i in range(n_zl)])]
    convert_element_type x2 -> x0, local copies, waits for them, and re-layouts: 2.89 us -> none  [shards(): hidden.astype(jnp.bfloat16)]
where the time goes in v9:
time: 241 us; the launch traced here: 240 us
  starting transfers between devices  100 us (41%)
  waiting for transfers between devices  53.1 us (22%)
  blocking collectives  34 us (14%)
  between operations  14.6 us (6%)
  other arithmetic  14.4 us (6%)
  local copies, waits for them, and re-layouts  12.9 us (5%)
  matrix products  10.5 us (4%)
    all_to_all x1, blocking collectives, shards(): lax.all_to_all(pair_sum, 'zl', split_axis=0, concat_axis=0, tiled=True)  34 us
    ppermute x1, starting transfers between devices, shards(): lax.ppermute(kv_local, CTX, [(i, i ^ first) for i in range(n_ctx)])  16.3 us
    ppermute x4, starting transfers between devices, shards(): other = lax.ppermute(cur, CTX, [(i, i ^ bit) for i in range(n_ctx)])  14.9 us
    all_to_all x1, waiting for transfers between devices, shards(): lax.all_to_all(hidden, EXP, split_axis=0, concat_axis=0, tiled=True)  14.2 us
    ppermute x4, waiting for transfers between devices, shards(): other = lax.ppermute(cur, CTX, [(i, i ^ bit) for i in range(n_ctx)])  12.8 us
    ppermute x1, starting transfers between devices, shards(): got = lax.ppermute(give, 'c', [(0, 1), (1, 0)])  12.6 us
    ppermute x1, starting transfers between devices, shards(): w_other = lax.ppermute(w_local, 'zh', [(0, 1), (1, 0)])  12.5 us
    all_to_all x1, starting transfers between devices, shards(): lax.all_to_all(jnp.broadcast_to(expert_ids[None], (n_exp,) + expert_ids.s...  12.4 us
  transfers between devices with their start and end apart: 15, of which 10 were waited for; matrix products, arithmetic and copies ran while one was open for 11% of the time, Pallas kernels for 0%

profile of v9, /device:TPU:1, one launch (start us, length us, event | category | flops | bytes accessed | tf_op | source)
XLA Modules:
  0.0 240.0 jit_solution(1651839905963409402)
XLA Ops:
  8.2 16.3 %collective-permute-start = (bf16[128,128]{1,0:T(8,128)(2,1)S(1)}, bf16[128,128]{1,0:T(8,128)(2,1)S(1)}, u32[]{:S(2)}, u32[]{:S(2)}) collective-permute-start(bf16[128,128]{1,0:T(8,128)(2,1)S(1)} %dynamic-slice_select_fusion), channel_id=1, source_target_pairs={{0,256},{16,272},{32,288},{48,304},{64,320},{80,336},{96,352},{112... | collective-permute-start | bytes 98312 | tf_op jit(solution)/shard_map/ppermute | solution.py:86
  25.9 4.7 %collective-permute-start.1 = (bf16[256,128]{1,0:T(8,128)(2,1)S(1)}, bf16[256,128]{1,0:T(8,128)(2,1)S(1)}, u32[]{:S(2)}, u32[]{:S(2)}) collective-permute-start(bf16[256,128]{1,0:T(8,128)(2,1)S(1)} %maximum_select_fusion.9), channel_id=1, source_target_pairs={{0,128},{16,144},{32,160},{48,176},{64,192},{80,208},{96,224},{112... | collective-permute-start | bytes 196616 | tf_op jit(solution)/shard_map/ppermute | solution.py:101
  32.4 3.1 %collective-permute-start.2 = (bf16[512,128]{1,0:T(8,128)(2,1)S(1)}, bf16[512,128]{1,0:T(8,128)(2,1)S(1)}, u32[]{:S(2)}, u32[]{:S(2)}) collective-permute-start(bf16[512,128]{1,0:T(8,128)(2,1)S(1)} %maximum_select_fusion.7), channel_id=1, source_target_pairs={{0,64},{16,80},{32,96},{48,112},{64,0},{80,16},{96,32},{112,48},{1... | collective-permute-start | bytes 393224 | tf_op jit(solution)/shard_map/ppermute | solution.py:101
  35.6 2.6 %collective-permute-done.2 = bf16[512,128]{1,0:T(8,128)(2,1)S(1)} collective-permute-done((bf16[512,128]{1,0:T(8,128)(2,1)S(1)}, bf16[512,128]{1,0:T(8,128)(2,1)S(1)}, u32[]{:S(2)}, u32[]{:S(2)}) %collective-permute-start.2) | collective-permute-done | bytes 131104 | tf_op jit(solution)/shard_map/ppermute | solution.py:101
  38.2 4.8 %collective-permute-start.3 = (bf16[1024,128]{1,0:T(8,128)(2,1)S(1)}, bf16[1024,128]{1,0:T(8,128)(2,1)S(1)}, u32[]{:S(2)}, u32[]{:S(2)}) collective-permute-start(bf16[1024,128]{1,0:T(8,128)(2,1)S(1)} %maximum_select_fusion.5), channel_id=1, source_target_pairs={{0,32},{16,48},{32,0},{48,16},{64,96},{80,112},{96,64},{112,80},{1... | collective-permute-start | bytes 786440 | tf_op jit(solution)/shard_map/ppermute | solution.py:101
  44.9 12.5 %collective-permute-start.7 = (bf16[48,4096]{1,0:T(8,128)(2,1)}, bf16[48,4096]{1,0:T(8,128)(2,1)}, u32[]{:S(2)}, u32[]{:S(2)}) collective-permute-start(bf16[48,4096]{1,0:T(8,128)(2,1)} %pad_maximum_fusion), channel_id=1, source_target_pairs={{0,256},{256,0},{1,257},{257,1},{2,258},{258,2},{3,259},{259,3},{4... | collective-permute-start | bytes 1179656 | tf_op jit(solution)/shard_map/ppermute | solution.py:87
  58.2 2.3 collective-permute-start.4
  60.9 8.4 %collective-permute-done.4 = bf16[2048,128]{1,0:T(8,128)(2,1)S(1)} collective-permute-done((bf16[2048,128]{1,0:T(8,128)(2,1)S(1)}, bf16[2048,128]{1,0:T(8,128)(2,1)S(1)}, u32[]{:S(2)}, u32[]{:S(2)}) %collective-permute-start.4) | collective-permute-done | bytes 524320 | tf_op jit(solution)/shard_map/ppermute | solution.py:101
  69.5 7.2 %collective-permute-start.5 = (bf16[4096,128]{1,0:T(8,128)(2,1)S(1)}, bf16[4096,128]{1,0:T(8,128)(2,1)}, u32[]{:S(2)}, u32[]{:S(2)}) collective-permute-start(bf16[4096,128]{1,0:T(8,128)(2,1)S(1)} %maximum_select_fusion), channel_id=1, source_target_pairs={{0,1},{1,0},{2,3},{3,2},{4,5},{5,4},{6,7},{7,6},{8,9},{9,8},{10,11... | collective-permute-start | bytes 3145736 | tf_op jit(solution)/shard_map/ppermute | solution.py:105
  79.9 2.2 maximum_select_fusion.2
  88.3 12.6 %collective-permute-start.6 = (bf16[8,8,4096]{2,1,0:T(8,128)(2,1)S(1)}, bf16[8,8,4096]{2,1,0:T(8,128)(2,1)S(1)}, u32[]{:S(2)}, u32[]{:S(2)}) collective-permute-start(bf16[8,8,4096]{2,1,0:T(8,128)(2,1)S(1)} %fusion.27), channel_id=1, source_target_pairs={{0,1},{1,0},{2,3},{3,2},{4,5},{5,4},{6,7},{7,6},{8,9},{9,8},{10,11... | collective-permute-start | bytes 1572872 | tf_op jit(solution)/shard_map/ppermute | solution.py:163
  102.6 34.0 %all_to_all.15 = bf16[8,8,4096]{2,1,0:T(8,128)(2,1)S(1)} all-to-all(bf16[8,8,4096]{2,1,0:T(8,128)(2,1)S(1)} %fusion.14), channel_id=1, replica_groups=mesh['zh'=2,'x'=4,'y'=4,'zl'=8,'c'=2] {'zl'}, dimensions={0} | all-to-all | bytes 1048576 | tf_op jit(solution)/shard_map/all_to_all | solution.py:166
  137.0 4.6 %collective-permute-start.8 = (bf16[8,4096]{1,0:T(8,128)(2,1)S(1)}, bf16[8,4096]{1,0:T(8,128)(2,1)S(1)}, u32[]{:S(2)}, u32[]{:S(2)}) collective-permute-start(bf16[8,4096]{1,0:T(8,128)(2,1)S(1)} %fusion.47), channel_id=1, source_target_pairs={{0,8},{2,10},{4,12},{6,14},{8,0},{10,2},{12,4},{14,6},{1,9},{3,11}... | collective-permute-start | bytes 196616 | tf_op jit(solution)/shard_map/ppermute | solution.py:183
  141.6 4.3 %collective-permute-done.8 = bf16[8,4096]{1,0:T(8,128)(2,1)S(1)} collective-permute-done((bf16[8,4096]{1,0:T(8,128)(2,1)S(1)}, bf16[8,4096]{1,0:T(8,128)(2,1)S(1)}, u32[]{:S(2)}, u32[]{:S(2)}) %collective-permute-start.8) | collective-permute-done | bytes 65568 | tf_op jit(solution)/shard_map/ppermute | solution.py:183
  146.0 3.6 %collective-permute-start.9 = (bf16[16,4096]{1,0:T(8,128)(2,1)S(1)}, bf16[16,4096]{1,0:T(8,128)(2,1)S(1)}, u32[]{:S(2)}, u32[]{:S(2)}) collective-permute-start(bf16[16,4096]{1,0:T(8,128)(2,1)S(1)} %maximum_select_fusion.8), channel_id=1, source_target_pairs={{0,4},{2,6},{4,0},{6,2},{8,12},{10,14},{12,8},{14,10},{1,5},{3,7},... | collective-permute-start | bytes 393224 | tf_op jit(solution)/shard_map/ppermute | solution.py:183
  149.6 3.9 %collective-permute-done.9 = bf16[16,4096]{1,0:T(8,128)(2,1)S(1)} collective-permute-done((bf16[16,4096]{1,0:T(8,128)(2,1)S(1)}, bf16[16,4096]{1,0:T(8,128)(2,1)S(1)}, u32[]{:S(2)}, u32[]{:S(2)}) %collective-permute-start.9) | collective-permute-done | bytes 131104 | tf_op jit(solution)/shard_map/ppermute | solution.py:183
  153.6 3.8 %collective-permute-start.10 = (bf16[32,4096]{1,0:T(8,128)(2,1)S(1)}, bf16[32,4096]{1,0:T(8,128)(2,1)S(1)}, u32[]{:S(2)}, u32[]{:S(2)}) collective-permute-start(bf16[32,4096]{1,0:T(8,128)(2,1)S(1)} %maximum_select_fusion.6), channel_id=1, source_target_pairs={{0,2},{2,0},{4,6},{6,4},{8,10},{10,8},{12,14},{14,12},{1,3},{3,1},... | collective-permute-start | bytes 786440 | tf_op jit(solution)/shard_map/ppermute | solution.py:183
  158.0 12.4 %all-to-all-start.1 = ((s32[16,8,8]{2,1,0:T(8,128)}), s32[16,8,8]{2,1,0:T(8,128)S(1)}, u32[]{:S(2)}, u32[]{:S(2)}) async-start(s32[16,8,8]{2,1,0:T(8,128)} %broadcast_in_dim.166), calls=%async_computation.1 | async-start | bytes 131072 | tf_op jit(solution)/shard_map/all_to_all | solution.py:173
  170.5 2.0 collective-permute-start.11
  172.6 7.8 %all-to-all-done.1 = s32[16,8,8]{2,1,0:T(8,128)S(1)} async-done(((s32[16,8,8]{2,1,0:T(8,128)}), s32[16,8,8]{2,1,0:T(8,128)S(1)}, u32[]{:S(2)}, u32[]{:S(2)}) %all-to-all-start.1) | async-done | bytes 4128 | tf_op jit(solution)/shard_map/all_to_all | solution.py:173
  191.0 7.2 %all-gather.2.cloned.1.call-done = bf16[1536,4096]{1,0:T(8,128)(2,1)} async-done(((bf16[96,4096]{1,0:T(8,128)(2,1)}), bf16[1536,4096]{1,0:T(8,128)(2,1)}) %all-gather.2.cloned.1.call-update) | async-done | bytes 12582928 | tf_op jit(solution)/shard_map/all_gather | solution.py:93
  198.1 7.2 %fusion = f32[1536,128]{1,0:T(8,128)S(1)} fusion(bf16[1536,4096]{1,0:T(8,128)(2,1)} %all-gather.2.cloned.1.call-done, bf16[128,4096]{1,0:T(8,128)(2,1)} %slice_dynamic-update-slice_fusion, s32[128]{0:T(128)S(1)} %select_n.297), kind=kOutput, calls=%fused_computation.3 | convolution fusion | flops 1745371136 | bytes 14418432 | tf_op jit(solution)/shard_map/fd,sd->fs/dot_general | solution.py:217
  206.3 10.7 %all-to-all-start.2 = ((bf16[16,8,768]{2,1,0:T(8,128)(2,1)}), bf16[16,8,768]{2,1,0:T(8,128)(2,1)S(1)}, u32[]{:S(2)}, u32[]{:S(2)}) async-start(bf16[16,8,768]{2,1,0:T(8,128)(2,1)} %bitcast.49), calls=%async_computation.2 | async-start | bytes 393216 | tf_op jit(solution)/shard_map/all_to_all | solution.py:223
  217.5 14.2 %all-to-all-done.2 = bf16[16,8,768]{2,1,0:T(8,128)(2,1)S(1)} async-done(((bf16[16,8,768]{2,1,0:T(8,128)(2,1)}), bf16[16,8,768]{2,1,0:T(8,128)(2,1)S(1)}, u32[]{:S(2)}, u32[]{:S(2)}) %all-to-all-start.2) | async-done | bytes 196640 | tf_op jit(solution)/shard_map/all_to_all | solution.py:223
  (118 shorter events, 33.2 us)
Async XLA Ops:
  7.2 80.6 %copy-start = (bf16[256,4096]{1,0:T(8,128)(2,1)S(1)}, bf16[256,4096]{1,0:T(8,128)(2,1)}, u32[]{:S(2)}) copy-start(bf16[256,4096]{1,0:T(8,128)(2,1)} %param.17) | copy-start | bytes 6291460
  7.2 53.4 %copy-start.12 = (s32[64]{0:T(128)S(1)}, s32[64]{0:T(128)}, u32[]{:S(2)}) copy-start(s32[64]{0:T(128)} %param.16) | copy-start | bytes 772
  7.2 190.9 %all-gather.2.cloned.1.call-start = ((), (), s32[]{:S(2)}) async-start(), calls=%async_computation.3 | async-start | bytes 13369344 | tf_op jit(solution)/shard_map/all_gather | solution.py:93
  8.2 17.7 %collective-permute-start = (bf16[128,128]{1,0:T(8,128)(2,1)S(1)}, bf16[128,128]{1,0:T(8,128)(2,1)S(1)}, u32[]{:S(2)}, u32[]{:S(2)}) collective-permute-start(bf16[128,128]{1,0:T(8,128)(2,1)S(1)} %dynamic-slice_select_fusion), channel_id=1, source_target_pairs={{0,256},{16,272},{32,288},{48,304},{64,320},{80,336},{96,352},{112... | collective-permute-start | bytes 98312 | tf_op jit(solution)/shard_map/ppermute | solution.py:86
  25.9 6.5 %collective-permute-start.1 = (bf16[256,128]{1,0:T(8,128)(2,1)S(1)}, bf16[256,128]{1,0:T(8,128)(2,1)S(1)}, u32[]{:S(2)}, u32[]{:S(2)}) collective-permute-start(bf16[256,128]{1,0:T(8,128)(2,1)S(1)} %maximum_select_fusion.9), channel_id=1, source_target_pairs={{0,128},{16,144},{32,160},{48,176},{64,192},{80,208},{96,224},{112... | collective-permute-start | bytes 196616 | tf_op jit(solution)/shard_map/ppermute | solution.py:101
  32.4 5.7 %collective-permute-start.2 = (bf16[512,128]{1,0:T(8,128)(2,1)S(1)}, bf16[512,128]{1,0:T(8,128)(2,1)S(1)}, u32[]{:S(2)}, u32[]{:S(2)}) collective-permute-start(bf16[512,128]{1,0:T(8,128)(2,1)S(1)} %maximum_select_fusion.7), channel_id=1, source_target_pairs={{0,64},{16,80},{32,96},{48,112},{64,0},{80,16},{96,32},{112,48},{1... | collective-permute-start | bytes 393224 | tf_op jit(solution)/shard_map/ppermute | solution.py:101
  38.2 19.9 %collective-permute-start.3 = (bf16[1024,128]{1,0:T(8,128)(2,1)S(1)}, bf16[1024,128]{1,0:T(8,128)(2,1)S(1)}, u32[]{:S(2)}, u32[]{:S(2)}) collective-permute-start(bf16[1024,128]{1,0:T(8,128)(2,1)S(1)} %maximum_select_fusion.5), channel_id=1, source_target_pairs={{0,32},{16,48},{32,0},{48,16},{64,96},{80,112},{96,64},{112,80},{1... | collective-permute-start | bytes 786440 | tf_op jit(solution)/shard_map/ppermute | solution.py:101
  44.9 35.0 %copy-start.1 = (bf16[1,4096,24]{1,2,0:T(8,128)(2,1)S(1)}, bf16[1,4096,24]{1,2,0:T(8,128)(2,1)}, u32[]{:S(2)}) copy-start(bf16[1,4096,24]{1,2,0:T(8,128)(2,1)} %param.20) | copy-start | bytes 589828
  44.9 35.0 %copy-start.2 = (bf16[1,4096,24]{1,2,0:T(8,128)(2,1)S(1)}, bf16[1,4096,24]{1,2,0:T(8,128)(2,1)}, u32[]{:S(2)}) copy-start(bf16[1,4096,24]{1,2,0:T(8,128)(2,1)} %param.19) | copy-start | bytes 589828
  44.9 35.0 %collective-permute-start.7 = (bf16[48,4096]{1,0:T(8,128)(2,1)}, bf16[48,4096]{1,0:T(8,128)(2,1)}, u32[]{:S(2)}, u32[]{:S(2)}) collective-permute-start(bf16[48,4096]{1,0:T(8,128)(2,1)} %pad_maximum_fusion), channel_id=1, source_target_pairs={{0,256},{256,0},{1,257},{257,1},{2,258},{258,2},{3,259},{259,3},{4... | collective-permute-start | bytes 1179656 | tf_op jit(solution)/shard_map/ppermute | solution.py:87
  58.2 11.0 %collective-permute-start.4 = (bf16[2048,128]{1,0:T(8,128)(2,1)S(1)}, bf16[2048,128]{1,0:T(8,128)(2,1)S(1)}, u32[]{:S(2)}, u32[]{:S(2)}) collective-permute-start(bf16[2048,128]{1,0:T(8,128)(2,1)S(1)} %maximum_select_fusion.3), channel_id=1, source_target_pairs={{0,16},{16,0},{32,48},{48,32},{64,80},{80,64},{96,112},{112,96},{1... | collective-permute-start | bytes 1572872 | tf_op jit(solution)/shard_map/ppermute | solution.py:101
  69.5 12.7 %collective-permute-start.5 = (bf16[4096,128]{1,0:T(8,128)(2,1)S(1)}, bf16[4096,128]{1,0:T(8,128)(2,1)}, u32[]{:S(2)}, u32[]{:S(2)}) collective-permute-start(bf16[4096,128]{1,0:T(8,128)(2,1)S(1)} %maximum_select_fusion), channel_id=1, source_target_pairs={{0,1},{1,0},{2,3},{3,2},{4,5},{5,4},{6,7},{7,6},{8,9},{9,8},{10,11... | collective-permute-start | bytes 3145736 | tf_op jit(solution)/shard_map/ppermute | solution.py:105
  88.3 48.5 %copy-start.9 = (bf16[8,4096]{1,0:T(8,128)(2,1)S(1)}, bf16[8,4096]{1,0:T(8,128)(2,1)}, u32[]{:S(2)}) copy-start(bf16[8,4096]{1,0:T(8,128)(2,1)} %param.12) | copy-start | bytes 196612
  88.3 48.6 %copy-start.10 = (f32[4096]{0:T(1024)S(1)}, f32[4096]{0:T(1024)}, u32[]{:S(2)}) copy-start(f32[4096]{0:T(1024)} %param.18) | copy-start | bytes 49156
  88.3 69.0 %copy-start.8 = (s32[8,8]{1,0:T(8,128)S(1)}, s32[8,8]{1,0:T(8,128)}, u32[]{:S(2)}) copy-start(s32[8,8]{1,0:T(8,128)} %param.21) | copy-start | bytes 772
  88.3 14.1 %collective-permute-start.6 = (bf16[8,8,4096]{2,1,0:T(8,128)(2,1)S(1)}, bf16[8,8,4096]{2,1,0:T(8,128)(2,1)S(1)}, u32[]{:S(2)}, u32[]{:S(2)}) collective-permute-start(bf16[8,8,4096]{2,1,0:T(8,128)(2,1)S(1)} %fusion.27), channel_id=1, source_target_pairs={{0,1},{1,0},{2,3},{3,2},{4,5},{5,4},{6,7},{7,6},{8,9},{9,8},{10,11... | collective-permute-start | bytes 1572872 | tf_op jit(solution)/shard_map/ppermute | solution.py:163
  136.9 44.1 %copy-start.7 = (bf16[8,4096]{1,0:T(8,128)(2,1)}, bf16[8,4096]{1,0:T(8,128)(2,1)S(1)}, u32[]{:S(2)}) copy-start(bf16[8,4096]{1,0:T(8,128)(2,1)S(1)} %get-tuple-element.7) | copy-start | bytes 196612
  137.0 8.9 %collective-permute-start.8 = (bf16[8,4096]{1,0:T(8,128)(2,1)S(1)}, bf16[8,4096]{1,0:T(8,128)(2,1)S(1)}, u32[]{:S(2)}, u32[]{:S(2)}) collective-permute-start(bf16[8,4096]{1,0:T(8,128)(2,1)S(1)} %fusion.47), channel_id=1, source_target_pairs={{0,8},{2,10},{4,12},{6,14},{8,0},{10,2},{12,4},{14,6},{1,9},{3,11}... | collective-permute-start | bytes 196616 | tf_op jit(solution)/shard_map/ppermute | solution.py:183
  146.0 7.6 %collective-permute-start.9 = (bf16[16,4096]{1,0:T(8,128)(2,1)S(1)}, bf16[16,4096]{1,0:T(8,128)(2,1)S(1)}, u32[]{:S(2)}, u32[]{:S(2)}) collective-permute-start(bf16[16,4096]{1,0:T(8,128)(2,1)S(1)} %maximum_select_fusion.8), channel_id=1, source_target_pairs={{0,4},{2,6},{4,0},{6,2},{8,12},{10,14},{12,8},{14,10},{1,5},{3,7},... | collective-permute-start | bytes 393224 | tf_op jit(solution)/shard_map/ppermute | solution.py:183
  153.6 16.8 %collective-permute-start.10 = (bf16[32,4096]{1,0:T(8,128)(2,1)S(1)}, bf16[32,4096]{1,0:T(8,128)(2,1)S(1)}, u32[]{:S(2)}, u32[]{:S(2)}) collective-permute-start(bf16[32,4096]{1,0:T(8,128)(2,1)S(1)} %maximum_select_fusion.6), channel_id=1, source_target_pairs={{0,2},{2,0},{4,6},{6,4},{8,10},{10,8},{12,14},{14,12},{1,3},{3,1},... | collective-permute-start | bytes 786440 | tf_op jit(solution)/shard_map/ppermute | solution.py:183
  158.0 22.4 %all-to-all-start.1 = ((s32[16,8,8]{2,1,0:T(8,128)}), s32[16,8,8]{2,1,0:T(8,128)S(1)}, u32[]{:S(2)}, u32[]{:S(2)}) async-start(s32[16,8,8]{2,1,0:T(8,128)} %broadcast_in_dim.166), calls=%async_computation.1 | async-start | bytes 131072 | tf_op jit(solution)/shard_map/all_to_all | solution.py:173
  170.5 10.2 %collective-permute-start.11 = (bf16[64,4096]{1,0:T(8,128)(2,1)S(1)}, bf16[64,4096]{1,0:T(8,128)(2,1)S(1)}, u32[]{:S(2)}, u32[]{:S(2)}) collective-permute-start(bf16[64,4096]{1,0:T(8,128)(2,1)S(1)} %maximum_select_fusion.4), channel_id=1, source_target_pairs={{0,1},{1,0},{2,3},{3,2},{4,5},{5,4},{6,7},{7,6},{8,9},{9,8},{10,11... | collective-permute-start | bytes 1572872 | tf_op jit(solution)/shard_map/ppermute | solution.py:187
  205.4 27.0 %copy-start.11 = (f32[8,8]{1,0:T(8,128)S(1)}, f32[8,8]{1,0:T(8,128)}, u32[]{:S(2)}) copy-start(f32[8,8]{1,0:T(8,128)} %param.22) | copy-start | bytes 772
  206.3 25.3 %all-to-all-start.2 = ((bf16[16,8,768]{2,1,0:T(8,128)(2,1)}), bf16[16,8,768]{2,1,0:T(8,128)(2,1)S(1)}, u32[]{:S(2)}, u32[]{:S(2)}) async-start(bf16[16,8,768]{2,1,0:T(8,128)(2,1)} %bitcast.49), calls=%async_computation.2 | async-start | bytes 393216 | tf_op jit(solution)/shard_map/all_to_all | solution.py:223
  (5 other events, 7.3 us)
Sparse Core Ops, SparseCore 0:
  82.2 115.8 all-gather.1

commit v10 on v9

--- a/solution.py
+++ b/solution.py
@@ -207,6 +207,7 @@
     received = jnp.dot(placing, normed_all, preferred_element_type=jnp.float32).astype(
         jnp.bfloat16
     )
+    received = lax.optimization_barrier(received)
 
     ids_flat = expert_ids.reshape(-1)
     onehot = (ids_flat[:, None] == jnp.arange(EXPERTS, dtype=jnp.int32)[None, :]).astype(jnp.int32)

time: 241 us -> 240 us (level)
  local copies, waits for them, and re-layouts: 12.9 us -> 3.02 us
  waiting for transfers between devices: 53.1 us -> 62.4 us
    all_gather x1, waiting for transfers between devices: 7.19 us -> 16.5 us  [shards(): w_all = lax.all_gather(w_pair, ('x', 'y'), axis=0, tiled=True)]
    unnamed x43, local copies, waits for them, and re-layouts: 9.57 us -> 0.33 us
  transfers between devices with their start and end apart: 15 -> 15, of which waited for: 10 -> 10; matrix products, arithmetic and copies ran while one was open for 11% -> 7% of each run, Pallas kernels for 0% -> 0%
where the time goes in v10:
time: 240 us; the launch traced here: 239 us
  starting transfers between devices  100 us (42%)
  waiting for transfers between devices  62.4 us (26%)
  blocking collectives  34 us (14%)
  between operations  14.8 us (6%)
  other arithmetic  14.4 us (6%)
  matrix products  10.2 us (4%)
  local copies, waits for them, and re-layouts  3.02 us (1%)
    all_to_all x1, blocking collectives, shards(): lax.all_to_all(pair_sum, 'zl', split_axis=0, concat_axis=0, tiled=True)  34 us
    all_gather x1, waiting for transfers between devices, shards(): w_all = lax.all_gather(w_pair, ('x', 'y'), axis=0, tiled=True)  16.5 us
    ppermute x1, starting transfers between devices, shards(): lax.ppermute(kv_local, CTX, [(i, i ^ first) for i in range(n_ctx)])  16.3 us
    ppermute x4, starting transfers between devices, shards(): other = lax.ppermute(cur, CTX, [(i, i ^ bit) for i in range(n_ctx)])  14.9 us
    all_to_all x1, waiting for transfers between devices, shards(): lax.all_to_all(hidden, EXP, split_axis=0, concat_axis=0, tiled=True)  14.2 us
    ppermute x4, waiting for transfers between devices, shards(): other = lax.ppermute(cur, CTX, [(i, i ^ bit) for i in range(n_ctx)])  12.8 us
    ppermute x1, starting transfers between devices, shards(): got = lax.ppermute(give, 'c', [(0, 1), (1, 0)])  12.6 us
    ppermute x1, starting transfers between devices, shards(): w_other = lax.ppermute(w_local, 'zh', [(0, 1), (1, 0)])  12.5 us
  transfers between devices with their start and end apart: 15, of which 10 were waited for; matrix products, arithmetic and copies ran while one was open for 7% of the time, Pallas kernels for 0%

profile of v10, /device:TPU:1, one launch (start us, length us, event | category | flops | bytes accessed | tf_op | source)
XLA Modules:
  0.0 239.3 jit_solution(5873264043789563502)
XLA Ops:
  8.2 16.3 %collective-permute-start = (bf16[128,128]{1,0:T(8,128)(2,1)S(1)}, bf16[128,128]{1,0:T(8,128)(2,1)S(1)}, u32[]{:S(2)}, u32[]{:S(2)}) collective-permute-start(bf16[128,128]{1,0:T(8,128)(2,1)S(1)} %dynamic-slice_select_fusion), channel_id=1, source_target_pairs={{0,256},{16,272},{32,288},{48,304},{64,320},{80,336},{96,352},{112... | collective-permute-start | bytes 98312 | tf_op jit(solution)/shard_map/ppermute | solution.py:86
  25.9 4.7 %collective-permute-start.1 = (bf16[256,128]{1,0:T(8,128)(2,1)S(1)}, bf16[256,128]{1,0:T(8,128)(2,1)S(1)}, u32[]{:S(2)}, u32[]{:S(2)}) collective-permute-start(bf16[256,128]{1,0:T(8,128)(2,1)S(1)} %maximum_select_fusion.9), channel_id=1, source_target_pairs={{0,128},{16,144},{32,160},{48,176},{64,192},{80,208},{96,224},{112... | collective-permute-start | bytes 196616 | tf_op jit(solution)/shard_map/ppermute | solution.py:101
  32.4 3.1 %collective-permute-start.2 = (bf16[512,128]{1,0:T(8,128)(2,1)S(1)}, bf16[512,128]{1,0:T(8,128)(2,1)S(1)}, u32[]{:S(2)}, u32[]{:S(2)}) collective-permute-start(bf16[512,128]{1,0:T(8,128)(2,1)S(1)} %maximum_select_fusion.7), channel_id=1, source_target_pairs={{0,64},{16,80},{32,96},{48,112},{64,0},{80,16},{96,32},{112,48},{1... | collective-permute-start | bytes 393224 | tf_op jit(solution)/shard_map/ppermute | solution.py:101
  35.6 2.6 %collective-permute-done.2 = bf16[512,128]{1,0:T(8,128)(2,1)S(1)} collective-permute-done((bf16[512,128]{1,0:T(8,128)(2,1)S(1)}, bf16[512,128]{1,0:T(8,128)(2,1)S(1)}, u32[]{:S(2)}, u32[]{:S(2)}) %collective-permute-start.2) | collective-permute-done | bytes 131104 | tf_op jit(solution)/shard_map/ppermute | solution.py:101
  38.2 4.8 %collective-permute-start.3 = (bf16[1024,128]{1,0:T(8,128)(2,1)S(1)}, bf16[1024,128]{1,0:T(8,128)(2,1)S(1)}, u32[]{:S(2)}, u32[]{:S(2)}) collective-permute-start(bf16[1024,128]{1,0:T(8,128)(2,1)S(1)} %maximum_select_fusion.5), channel_id=1, source_target_pairs={{0,32},{16,48},{32,0},{48,16},{64,96},{80,112},{96,64},{112,80},{1... | collective-permute-start | bytes 786440 | tf_op jit(solution)/shard_map/ppermute | solution.py:101
  44.9 12.5 %collective-permute-start.7 = (bf16[48,4096]{1,0:T(8,128)(2,1)}, bf16[48,4096]{1,0:T(8,128)(2,1)}, u32[]{:S(2)}, u32[]{:S(2)}) collective-permute-start(bf16[48,4096]{1,0:T(8,128)(2,1)} %pad_maximum_fusion), channel_id=1, source_target_pairs={{0,256},{256,0},{1,257},{257,1},{2,258},{258,2},{3,259},{259,3},{4... | collective-permute-start | bytes 1179656 | tf_op jit(solution)/shard_map/ppermute | solution.py:87
  58.2 2.3 collective-permute-start.4
  60.9 8.4 %collective-permute-done.4 = bf16[2048,128]{1,0:T(8,128)(2,1)S(1)} collective-permute-done((bf16[2048,128]{1,0:T(8,128)(2,1)S(1)}, bf16[2048,128]{1,0:T(8,128)(2,1)S(1)}, u32[]{:S(2)}, u32[]{:S(2)}) %collective-permute-start.4) | collective-permute-done | bytes 524320 | tf_op jit(solution)/shard_map/ppermute | solution.py:101
  69.5 7.2 %collective-permute-start.5 = (bf16[4096,128]{1,0:T(8,128)(2,1)S(1)}, bf16[4096,128]{1,0:T(8,128)(2,1)}, u32[]{:S(2)}, u32[]{:S(2)}) collective-permute-start(bf16[4096,128]{1,0:T(8,128)(2,1)S(1)} %maximum_select_fusion), channel_id=1, source_target_pairs={{0,1},{1,0},{2,3},{3,2},{4,5},{5,4},{6,7},{7,6},{8,9},{9,8},{10,11... | collective-permute-start | bytes 3145736 | tf_op jit(solution)/shard_map/ppermute | solution.py:105
  79.9 2.2 maximum_select_fusion.2
  88.3 12.6 %collective-permute-start.6 = (bf16[8,8,4096]{2,1,0:T(8,128)(2,1)S(1)}, bf16[8,8,4096]{2,1,0:T(8,128)(2,1)S(1)}, u32[]{:S(2)}, u32[]{:S(2)}) collective-permute-start(bf16[8,8,4096]{2,1,0:T(8,128)(2,1)S(1)} %fusion.26), channel_id=1, source_target_pairs={{0,1},{1,0},{2,3},{3,2},{4,5},{5,4},{6,7},{7,6},{8,9},{9,8},{10,11... | collective-permute-start | bytes 1572872 | tf_op jit(solution)/shard_map/ppermute | solution.py:163
  102.6 34.0 %all_to_all.15 = bf16[8,8,4096]{2,1,0:T(8,128)(2,1)S(1)} all-to-all(bf16[8,8,4096]{2,1,0:T(8,128)(2,1)S(1)} %fusion.13), channel_id=1, replica_groups=mesh['zh'=2,'x'=4,'y'=4,'zl'=8,'c'=2] {'zl'}, dimensions={0} | all-to-all | bytes 1048576 | tf_op jit(solution)/shard_map/all_to_all | solution.py:166
  137.0 4.6 %collective-permute-start.8 = (bf16[8,4096]{1,0:T(8,128)(2,1)S(1)}, bf16[8,4096]{1,0:T(8,128)(2,1)S(1)}, u32[]{:S(2)}, u32[]{:S(2)}) collective-permute-start(bf16[8,4096]{1,0:T(8,128)(2,1)S(1)} %fusion.46), channel_id=1, source_target_pairs={{0,8},{2,10},{4,12},{6,14},{8,0},{10,2},{12,4},{14,6},{1,9},{3,11}... | collective-permute-start | bytes 196616 | tf_op jit(solution)/shard_map/ppermute | solution.py:183
  141.6 4.3 %collective-permute-done.8 = bf16[8,4096]{1,0:T(8,128)(2,1)S(1)} collective-permute-done((bf16[8,4096]{1,0:T(8,128)(2,1)S(1)}, bf16[8,4096]{1,0:T(8,128)(2,1)S(1)}, u32[]{:S(2)}, u32[]{:S(2)}) %collective-permute-start.8) | collective-permute-done | bytes 65568 | tf_op jit(solution)/shard_map/ppermute | solution.py:183
  146.0 3.6 %collective-permute-start.9 = (bf16[16,4096]{1,0:T(8,128)(2,1)S(1)}, bf16[16,4096]{1,0:T(8,128)(2,1)S(1)}, u32[]{:S(2)}, u32[]{:S(2)}) collective-permute-start(bf16[16,4096]{1,0:T(8,128)(2,1)S(1)} %maximum_select_fusion.8), channel_id=1, source_target_pairs={{0,4},{2,6},{4,0},{6,2},{8,12},{10,14},{12,8},{14,10},{1,5},{3,7},... | collective-permute-start | bytes 393224 | tf_op jit(solution)/shard_map/ppermute | solution.py:183
  149.6 3.9 %collective-permute-done.9 = bf16[16,4096]{1,0:T(8,128)(2,1)S(1)} collective-permute-done((bf16[16,4096]{1,0:T(8,128)(2,1)S(1)}, bf16[16,4096]{1,0:T(8,128)(2,1)S(1)}, u32[]{:S(2)}, u32[]{:S(2)}) %collective-permute-start.9) | collective-permute-done | bytes 131104 | tf_op jit(solution)/shard_map/ppermute | solution.py:183
  153.6 3.8 %collective-permute-start.10 = (bf16[32,4096]{1,0:T(8,128)(2,1)S(1)}, bf16[32,4096]{1,0:T(8,128)(2,1)S(1)}, u32[]{:S(2)}, u32[]{:S(2)}) collective-permute-start(bf16[32,4096]{1,0:T(8,128)(2,1)S(1)} %maximum_select_fusion.6), channel_id=1, source_target_pairs={{0,2},{2,0},{4,6},{6,4},{8,10},{10,8},{12,14},{14,12},{1,3},{3,1},... | collective-permute-start | bytes 786440 | tf_op jit(solution)/shard_map/ppermute | solution.py:183
  158.0 12.4 %all-to-all-start.1 = ((s32[16,8,8]{2,1,0:T(8,128)}), s32[16,8,8]{2,1,0:T(8,128)S(1)}, u32[]{:S(2)}, u32[]{:S(2)}) async-start(s32[16,8,8]{2,1,0:T(8,128)} %broadcast_in_dim.166), calls=%async_computation.1 | async-start | bytes 131072 | tf_op jit(solution)/shard_map/all_to_all | solution.py:173
  170.5 2.0 collective-permute-start.11
  172.6 7.8 %all-to-all-done.1 = s32[16,8,8]{2,1,0:T(8,128)S(1)} async-done(((s32[16,8,8]{2,1,0:T(8,128)}), s32[16,8,8]{2,1,0:T(8,128)S(1)}, u32[]{:S(2)}, u32[]{:S(2)}) %all-to-all-start.1) | async-done | bytes 4128 | tf_op jit(solution)/shard_map/all_to_all | solution.py:173
  181.6 16.5 %all-gather.2.cloned.1.call-done = bf16[1536,4096]{1,0:T(8,128)(2,1)} async-done(((bf16[96,4096]{1,0:T(8,128)(2,1)}), bf16[1536,4096]{1,0:T(8,128)(2,1)}) %all-gather.2.cloned.1.call-update) | async-done | bytes 12582928 | tf_op jit(solution)/shard_map/all_gather | solution.py:93
  198.1 6.5 %fusion.95 = f32[1536,128]{1,0:T(8,128)S(1)} fusion(bf16[1536,4096]{1,0:T(8,128)(2,1)} %all-gather.2.cloned.1.call-done, bf16[128,4096]{1,0:T(8,128)(2,1)S(1)} %convolution_convert_fusion), kind=kOutput, calls=%fused_computation.226 | convolution fusion | flops 1610612736 | bytes 14417920 | tf_op jit(solution)/shard_map/fd,sd->fs/dot_general | solution.py:218
  205.6 10.7 %all-to-all-start.2 = ((bf16[16,8,768]{2,1,0:T(8,128)(2,1)}), bf16[16,8,768]{2,1,0:T(8,128)(2,1)S(1)}, u32[]{:S(2)}, u32[]{:S(2)}) async-start(bf16[16,8,768]{2,1,0:T(8,128)(2,1)} %bitcast.49), calls=%async_computation.2 | async-start | bytes 393216 | tf_op jit(solution)/shard_map/all_to_all | solution.py:224
  216.8 14.2 %all-to-all-done.2 = bf16[16,8,768]{2,1,0:T(8,128)(2,1)S(1)} async-done(((bf16[16,8,768]{2,1,0:T(8,128)(2,1)}), bf16[16,8,768]{2,1,0:T(8,128)(2,1)S(1)}, u32[]{:S(2)}, u32[]{:S(2)}) %all-to-all-start.2) | async-done | bytes 196640 | tf_op jit(solution)/shard_map/all_to_all | solution.py:224
  (119 shorter events, 23.7 us)
Async XLA Ops:
  7.2 80.6 %copy-start = (bf16[256,4096]{1,0:T(8,128)(2,1)S(1)}, bf16[256,4096]{1,0:T(8,128)(2,1)}, u32[]{:S(2)}) copy-start(bf16[256,4096]{1,0:T(8,128)(2,1)} %param.17) | copy-start | bytes 6291460
  7.2 53.4 %copy-start.12 = (s32[64]{0:T(128)S(1)}, s32[64]{0:T(128)}, u32[]{:S(2)}) copy-start(s32[64]{0:T(128)} %param.16) | copy-start | bytes 772
  7.2 190.9 %all-gather.2.cloned.1.call-start = ((), (), s32[]{:S(2)}) async-start(), calls=%async_computation.3 | async-start | bytes 13369344 | tf_op jit(solution)/shard_map/all_gather | solution.py:93
  8.2 17.7 %collective-permute-start = (bf16[128,128]{1,0:T(8,128)(2,1)S(1)}, bf16[128,128]{1,0:T(8,128)(2,1)S(1)}, u32[]{:S(2)}, u32[]{:S(2)}) collective-permute-start(bf16[128,128]{1,0:T(8,128)(2,1)S(1)} %dynamic-slice_select_fusion), channel_id=1, source_target_pairs={{0,256},{16,272},{32,288},{48,304},{64,320},{80,336},{96,352},{112... | collective-permute-start | bytes 98312 | tf_op jit(solution)/shard_map/ppermute | solution.py:86
  25.9 6.5 %collective-permute-start.1 = (bf16[256,128]{1,0:T(8,128)(2,1)S(1)}, bf16[256,128]{1,0:T(8,128)(2,1)S(1)}, u32[]{:S(2)}, u32[]{:S(2)}) collective-permute-start(bf16[256,128]{1,0:T(8,128)(2,1)S(1)} %maximum_select_fusion.9), channel_id=1, source_target_pairs={{0,128},{16,144},{32,160},{48,176},{64,192},{80,208},{96,224},{112... | collective-permute-start | bytes 196616 | tf_op jit(solution)/shard_map/ppermute | solution.py:101
  32.4 5.7 %collective-permute-start.2 = (bf16[512,128]{1,0:T(8,128)(2,1)S(1)}, bf16[512,128]{1,0:T(8,128)(2,1)S(1)}, u32[]{:S(2)}, u32[]{:S(2)}) collective-permute-start(bf16[512,128]{1,0:T(8,128)(2,1)S(1)} %maximum_select_fusion.7), channel_id=1, source_target_pairs={{0,64},{16,80},{32,96},{48,112},{64,0},{80,16},{96,32},{112,48},{1... | collective-permute-start | bytes 393224 | tf_op jit(solution)/shard_map/ppermute | solution.py:101
  38.2 19.9 %collective-permute-start.3 = (bf16[1024,128]{1,0:T(8,128)(2,1)S(1)}, bf16[1024,128]{1,0:T(8,128)(2,1)S(1)}, u32[]{:S(2)}, u32[]{:S(2)}) collective-permute-start(bf16[1024,128]{1,0:T(8,128)(2,1)S(1)} %maximum_select_fusion.5), channel_id=1, source_target_pairs={{0,32},{16,48},{32,0},{48,16},{64,96},{80,112},{96,64},{112,80},{1... | collective-permute-start | bytes 786440 | tf_op jit(solution)/shard_map/ppermute | solution.py:101
  44.9 35.0 %copy-start.1 = (bf16[1,4096,24]{1,2,0:T(8,128)(2,1)S(1)}, bf16[1,4096,24]{1,2,0:T(8,128)(2,1)}, u32[]{:S(2)}) copy-start(bf16[1,4096,24]{1,2,0:T(8,128)(2,1)} %param.20) | copy-start | bytes 589828
  44.9 35.0 %copy-start.2 = (bf16[1,4096,24]{1,2,0:T(8,128)(2,1)S(1)}, bf16[1,4096,24]{1,2,0:T(8,128)(2,1)}, u32[]{:S(2)}) copy-start(bf16[1,4096,24]{1,2,0:T(8,128)(2,1)} %param.19) | copy-start | bytes 589828
  44.9 35.0 %collective-permute-start.7 = (bf16[48,4096]{1,0:T(8,128)(2,1)}, bf16[48,4096]{1,0:T(8,128)(2,1)}, u32[]{:S(2)}, u32[]{:S(2)}) collective-permute-start(bf16[48,4096]{1,0:T(8,128)(2,1)} %pad_maximum_fusion), channel_id=1, source_target_pairs={{0,256},{256,0},{1,257},{257,1},{2,258},{258,2},{3,259},{259,3},{4... | collective-permute-start | bytes 1179656 | tf_op jit(solution)/shard_map/ppermute | solution.py:87
  58.2 11.0 %collective-permute-start.4 = (bf16[2048,128]{1,0:T(8,128)(2,1)S(1)}, bf16[2048,128]{1,0:T(8,128)(2,1)S(1)}, u32[]{:S(2)}, u32[]{:S(2)}) collective-permute-start(bf16[2048,128]{1,0:T(8,128)(2,1)S(1)} %maximum_select_fusion.3), channel_id=1, source_target_pairs={{0,16},{16,0},{32,48},{48,32},{64,80},{80,64},{96,112},{112,96},{1... | collective-permute-start | bytes 1572872 | tf_op jit(solution)/shard_map/ppermute | solution.py:101
  69.5 12.7 %collective-permute-start.5 = (bf16[4096,128]{1,0:T(8,128)(2,1)S(1)}, bf16[4096,128]{1,0:T(8,128)(2,1)}, u32[]{:S(2)}, u32[]{:S(2)}) collective-permute-start(bf16[4096,128]{1,0:T(8,128)(2,1)S(1)} %maximum_select_fusion), channel_id=1, source_target_pairs={{0,1},{1,0},{2,3},{3,2},{4,5},{5,4},{6,7},{7,6},{8,9},{9,8},{10,11... | collective-permute-start | bytes 3145736 | tf_op jit(solution)/shard_map/ppermute | solution.py:105
  88.3 48.5 %copy-start.9 = (bf16[8,4096]{1,0:T(8,128)(2,1)S(1)}, bf16[8,4096]{1,0:T(8,128)(2,1)}, u32[]{:S(2)}) copy-start(bf16[8,4096]{1,0:T(8,128)(2,1)} %param.12) | copy-start | bytes 196612
  88.3 48.6 %copy-start.10 = (f32[4096]{0:T(1024)S(1)}, f32[4096]{0:T(1024)}, u32[]{:S(2)}) copy-start(f32[4096]{0:T(1024)} %param.18) | copy-start | bytes 49156
  88.3 69.0 %copy-start.8 = (s32[8,8]{1,0:T(8,128)S(1)}, s32[8,8]{1,0:T(8,128)}, u32[]{:S(2)}) copy-start(s32[8,8]{1,0:T(8,128)} %param.21) | copy-start | bytes 772
  88.3 14.1 %collective-permute-start.6 = (bf16[8,8,4096]{2,1,0:T(8,128)(2,1)S(1)}, bf16[8,8,4096]{2,1,0:T(8,128)(2,1)S(1)}, u32[]{:S(2)}, u32[]{:S(2)}) collective-permute-start(bf16[8,8,4096]{2,1,0:T(8,128)(2,1)S(1)} %fusion.26), channel_id=1, source_target_pairs={{0,1},{1,0},{2,3},{3,2},{4,5},{5,4},{6,7},{7,6},{8,9},{9,8},{10,11... | collective-permute-start | bytes 1572872 | tf_op jit(solution)/shard_map/ppermute | solution.py:163
  136.9 44.1 %copy-start.7 = (bf16[8,4096]{1,0:T(8,128)(2,1)}, bf16[8,4096]{1,0:T(8,128)(2,1)S(1)}, u32[]{:S(2)}) copy-start(bf16[8,4096]{1,0:T(8,128)(2,1)S(1)} %get-tuple-element.7) | copy-start | bytes 196612
  137.0 8.9 %collective-permute-start.8 = (bf16[8,4096]{1,0:T(8,128)(2,1)S(1)}, bf16[8,4096]{1,0:T(8,128)(2,1)S(1)}, u32[]{:S(2)}, u32[]{:S(2)}) collective-permute-start(bf16[8,4096]{1,0:T(8,128)(2,1)S(1)} %fusion.46), channel_id=1, source_target_pairs={{0,8},{2,10},{4,12},{6,14},{8,0},{10,2},{12,4},{14,6},{1,9},{3,11}... | collective-permute-start | bytes 196616 | tf_op jit(solution)/shard_map/ppermute | solution.py:183
  146.0 7.6 %collective-permute-start.9 = (bf16[16,4096]{1,0:T(8,128)(2,1)S(1)}, bf16[16,4096]{1,0:T(8,128)(2,1)S(1)}, u32[]{:S(2)}, u32[]{:S(2)}) collective-permute-start(bf16[16,4096]{1,0:T(8,128)(2,1)S(1)} %maximum_select_fusion.8), channel_id=1, source_target_pairs={{0,4},{2,6},{4,0},{6,2},{8,12},{10,14},{12,8},{14,10},{1,5},{3,7},... | collective-permute-start | bytes 393224 | tf_op jit(solution)/shard_map/ppermute | solution.py:183
  153.6 16.8 %collective-permute-start.10 = (bf16[32,4096]{1,0:T(8,128)(2,1)S(1)}, bf16[32,4096]{1,0:T(8,128)(2,1)S(1)}, u32[]{:S(2)}, u32[]{:S(2)}) collective-permute-start(bf16[32,4096]{1,0:T(8,128)(2,1)S(1)} %maximum_select_fusion.6), channel_id=1, source_target_pairs={{0,2},{2,0},{4,6},{6,4},{8,10},{10,8},{12,14},{14,12},{1,3},{3,1},... | collective-permute-start | bytes 786440 | tf_op jit(solution)/shard_map/ppermute | solution.py:183
  158.0 22.4 %all-to-all-start.1 = ((s32[16,8,8]{2,1,0:T(8,128)}), s32[16,8,8]{2,1,0:T(8,128)S(1)}, u32[]{:S(2)}, u32[]{:S(2)}) async-start(s32[16,8,8]{2,1,0:T(8,128)} %broadcast_in_dim.166), calls=%async_computation.1 | async-start | bytes 131072 | tf_op jit(solution)/shard_map/all_to_all | solution.py:173
  170.5 10.2 %collective-permute-start.11 = (bf16[64,4096]{1,0:T(8,128)(2,1)S(1)}, bf16[64,4096]{1,0:T(8,128)(2,1)S(1)}, u32[]{:S(2)}, u32[]{:S(2)}) collective-permute-start(bf16[64,4096]{1,0:T(8,128)(2,1)S(1)} %maximum_select_fusion.4), channel_id=1, source_target_pairs={{0,1},{1,0},{2,3},{3,2},{4,5},{5,4},{6,7},{7,6},{8,9},{9,8},{10,11... | collective-permute-start | bytes 1572872 | tf_op jit(solution)/shard_map/ppermute | solution.py:187
  204.7 27.0 %copy-start.11 = (f32[8,8]{1,0:T(8,128)S(1)}, f32[8,8]{1,0:T(8,128)}, u32[]{:S(2)}) copy-start(f32[8,8]{1,0:T(8,128)} %param.22) | copy-start | bytes 772
  205.6 25.3 %all-to-all-start.2 = ((bf16[16,8,768]{2,1,0:T(8,128)(2,1)}), bf16[16,8,768]{2,1,0:T(8,128)(2,1)S(1)}, u32[]{:S(2)}, u32[]{:S(2)}) async-start(bf16[16,8,768]{2,1,0:T(8,128)(2,1)} %bitcast.49), calls=%async_computation.2 | async-start | bytes 393216 | tf_op jit(solution)/shard_map/all_to_all | solution.py:224
  (5 other events, 7.3 us)
Sparse Core Ops, SparseCore 0:
  82.2 115.8 all-gather.1

commit v11 on v10

--- a/solution.py
+++ b/solution.py
@@ -97,11 +97,13 @@
         low, jnp.concatenate([kv_local, kv_other]), jnp.concatenate([kv_other, kv_local])
     )
     order = [0, first]
-    for bit in bits[1:]:
+    for step, bit in enumerate(bits[1:]):
         other = lax.ppermute(cur, CTX, [(i, i ^ bit) for i in range(n_ctx)])
         low = (ctx_index & bit) == 0
         cur = jnp.where(low, jnp.concatenate([cur, other]), jnp.concatenate([other, cur]))
         order = order + [o + bit for o in order]
+        if step == 2:
+            w_pair, cur = lax.optimization_barrier((w_pair, cur))
     partner = lax.ppermute(cur, "c", [(0, 1), (1, 0)])
     key_piece = jnp.where(core_index == 0, cur, partner)
     value_piece = jnp.where(core_index == 0, partner, cur)

time: 240 us -> 247 us (1.029)
  blocking collectives: 34 us -> 53.7 us
  starting transfers between devices: 100 us -> 90 us
    all_to_all x1, blocking collectives: 34 us -> 53.7 us  [shards(): lax.all_to_all(pair_sum, 'zl', split_axis=0, concat_axis=0, tiled=True)]
    ppermute x1, starting transfers between devices: 12.6 us -> 2.41 us  [shards(): got = lax.ppermute(give, 'c', [(0, 1), (1, 0)])]
  transfers between devices with their start and end apart: 15 -> 15, of which waited for: 10 -> 12; matrix products, arithmetic and copies ran while one was open for 7% -> 6% of each run, Pallas kernels for 0% -> 0%
where the time goes in v11:
time: 247 us
  starting transfers between devices  90 us (36%)
  waiting for transfers between devices  62.2 us (25%)
  blocking collectives  53.7 us (22%)
  between operations  14.8 us (6%)
  other arithmetic  13.1 us (5%)
  matrix products  10.1 us (4%)
  local copies, waits for them, and re-layouts  2.85 us (1%)
    all_to_all x1, blocking collectives, shards(): lax.all_to_all(pair_sum, 'zl', split_axis=0, concat_axis=0, tiled=True)  53.7 us
    ppermute x1, starting transfers between devices, shards(): lax.ppermute(kv_local, CTX, [(i, i ^ first) for i in range(n_ctx)])  16.3 us
    all_gather x1, waiting for transfers between devices, shards(): w_all = lax.all_gather(w_pair, ('x', 'y'), axis=0, tiled=True)  15.6 us
    ppermute x4, starting transfers between devices, shards(): other = lax.ppermute(cur, CTX, [(i, i ^ bit) for i in range(n_ctx)])  14.9 us
    all_to_all x1, waiting for transfers between devices, shards(): lax.all_to_all(hidden, EXP, split_axis=0, concat_axis=0, tiled=True)  14.2 us
    ppermute x1, starting transfers between devices, shards(): w_other = lax.ppermute(w_local, 'zh', [(0, 1), (1, 0)])  12.4 us
    all_to_all x1, starting transfers between devices, shards(): lax.all_to_all(jnp.broadcast_to(expert_ids[None], (n_exp,) + expert_ids.s...  12.4 us
    ppermute x3, starting transfers between devices, shards(): other = lax.ppermute(cur, 'zl', [(i, i ^ bit) for i in range(n_zl)])  12 us
  transfers between devices with their start and end apart: 15, of which 12 were waited for; matrix products, arithmetic and copies ran while one was open for 6% of the time, Pallas kernels for 0%

profile of v11, /device:TPU:1, one launch (start us, length us, event | category | flops | bytes accessed | tf_op | source)
XLA Modules:
  0.0 246.6 jit_solution(17924784314751922289)
XLA Ops:
  8.2 16.3 %collective-permute-start.1 = (bf16[128,128]{1,0:T(8,128)(2,1)S(1)}, bf16[128,128]{1,0:T(8,128)(2,1)S(1)}, u32[]{:S(2)}, u32[]{:S(2)}) collective-permute-start(bf16[128,128]{1,0:T(8,128)(2,1)S(1)} %dynamic-slice_select_fusion), channel_id=1, source_target_pairs={{0,256},{16,272},{32,288},{48,304},{64,320},{80,336},{96,352},{112... | collective-permute-start | bytes 98312 | tf_op jit(solution)/shard_map/ppermute | solution.py:86
  25.9 4.7 %collective-permute-start.2 = (bf16[256,128]{1,0:T(8,128)(2,1)S(1)}, bf16[256,128]{1,0:T(8,128)(2,1)S(1)}, u32[]{:S(2)}, u32[]{:S(2)}) collective-permute-start(bf16[256,128]{1,0:T(8,128)(2,1)S(1)} %maximum_select_fusion.9), channel_id=1, source_target_pairs={{0,128},{16,144},{32,160},{48,176},{64,192},{80,208},{96,224},{112... | collective-permute-start | bytes 196616 | tf_op jit(solution)/shard_map/ppermute | solution.py:101
  31.6 12.4 %collective-permute-start = (bf16[48,4096]{1,0:T(8,128)(2,1)S(1)}, bf16[48,4096]{1,0:T(8,128)(2,1)S(1)}, u32[]{:S(2)}, u32[]{:S(2)}) collective-permute-start(bf16[48,4096]{1,0:T(8,128)(2,1)S(1)} %pad_maximum_fusion), channel_id=1, source_target_pairs={{0,256},{256,0},{1,257},{257,1},{2,258},{258,2},{3,259},{259,3},{4... | collective-permute-start | bytes 1179656 | tf_op jit(solution)/shard_map/ppermute | solution.py:87
  44.1 2.2 collective-permute-start.3
  46.3 3.8 %collective-permute-done.3 = bf16[512,128]{1,0:T(8,128)(2,1)S(1)} collective-permute-done((bf16[512,128]{1,0:T(8,128)(2,1)S(1)}, bf16[512,128]{1,0:T(8,128)(2,1)S(1)}, u32[]{:S(2)}, u32[]{:S(2)}) %collective-permute-start.3) | collective-permute-done | bytes 131104 | tf_op jit(solution)/shard_map/ppermute | solution.py:101
  50.1 4.8 %collective-permute-start.4 = (bf16[1024,128]{1,0:T(8,128)(2,1)S(1)}, bf16[1024,128]{1,0:T(8,128)(2,1)S(1)}, u32[]{:S(2)}, u32[]{:S(2)}) collective-permute-start(bf16[1024,128]{1,0:T(8,128)(2,1)S(1)} %maximum_select_fusion.5), channel_id=1, source_target_pairs={{0,32},{16,48},{32,0},{48,16},{64,96},{80,112},{96,64},{112,80},{1... | collective-permute-start | bytes 786440 | tf_op jit(solution)/shard_map/ppermute | solution.py:101
  56.2 2.3 maximum_select_fusion.2
  58.9 3.2 %collective-permute-start.5 = (bf16[2048,128]{1,0:T(8,128)(2,1)S(1)}, bf16[2048,128]{1,0:T(8,128)(2,1)}, u32[]{:S(2)}, u32[]{:S(2)}) collective-permute-start(bf16[2048,128]{1,0:T(8,128)(2,1)S(1)} %maximum_select_fusion.3), channel_id=1, source_target_pairs={{0,16},{16,0},{32,48},{48,32},{64,80},{80,64},{96,112},{112,96},{1... | collective-permute-start | bytes 1572872 | tf_op jit(solution)/shard_map/ppermute | solution.py:101
  62.3 7.8 %collective-permute-done.5 = bf16[2048,128]{1,0:T(8,128)(2,1)} collective-permute-done((bf16[2048,128]{1,0:T(8,128)(2,1)S(1)}, bf16[2048,128]{1,0:T(8,128)(2,1)}, u32[]{:S(2)}, u32[]{:S(2)}) %collective-permute-start.5) | collective-permute-done | bytes 524320 | tf_op jit(solution)/shard_map/ppermute | solution.py:101
  72.0 7.0 %collective-permute-start.6 = (bf16[4096,128]{1,0:T(8,128)(2,1)S(1)}, bf16[4096,128]{1,0:T(8,128)(2,1)}, u32[]{:S(2)}, u32[]{:S(2)}) collective-permute-start(bf16[4096,128]{1,0:T(8,128)(2,1)S(1)} %maximum_select_fusion), channel_id=1, source_target_pairs={{0,1},{1,0},{2,3},{3,2},{4,5},{5,4},{6,7},{7,6},{8,9},{9,8},{10,11... | collective-permute-start | bytes 3145736 | tf_op jit(solution)/shard_map/ppermute | solution.py:107
  87.2 2.4 collective-permute-start.7
  91.3 53.7 %all_to_all.15 = bf16[8,8,4096]{2,1,0:T(8,128)(2,1)S(1)} all-to-all(bf16[8,8,4096]{2,1,0:T(8,128)(2,1)S(1)} %fusion.13), channel_id=1, replica_groups=mesh['zh'=2,'x'=4,'y'=4,'zl'=8,'c'=2] {'zl'}, dimensions={0} | all-to-all | bytes 1048576 | tf_op jit(solution)/shard_map/all_to_all | solution.py:168
  145.3 4.6 %collective-permute-start.8 = (bf16[8,4096]{1,0:T(8,128)(2,1)S(1)}, bf16[8,4096]{1,0:T(8,128)(2,1)S(1)}, u32[]{:S(2)}, u32[]{:S(2)}) collective-permute-start(bf16[8,4096]{1,0:T(8,128)(2,1)S(1)} %fusion.46), channel_id=1, source_target_pairs={{0,8},{2,10},{4,12},{6,14},{8,0},{10,2},{12,4},{14,6},{1,9},{3,11}... | collective-permute-start | bytes 196616 | tf_op jit(solution)/shard_map/ppermute | solution.py:185
  149.9 4.3 %collective-permute-done.8 = bf16[8,4096]{1,0:T(8,128)(2,1)S(1)} collective-permute-done((bf16[8,4096]{1,0:T(8,128)(2,1)S(1)}, bf16[8,4096]{1,0:T(8,128)(2,1)S(1)}, u32[]{:S(2)}, u32[]{:S(2)}) %collective-permute-start.8) | collective-permute-done | bytes 65568 | tf_op jit(solution)/shard_map/ppermute | solution.py:185
  154.2 3.6 %collective-permute-start.9 = (bf16[16,4096]{1,0:T(8,128)(2,1)S(1)}, bf16[16,4096]{1,0:T(8,128)(2,1)S(1)}, u32[]{:S(2)}, u32[]{:S(2)}) collective-permute-start(bf16[16,4096]{1,0:T(8,128)(2,1)S(1)} %maximum_select_fusion.8), channel_id=1, source_target_pairs={{0,4},{2,6},{4,0},{6,2},{8,12},{10,14},{12,8},{14,10},{1,5},{3,7},... | collective-permute-start | bytes 393224 | tf_op jit(solution)/shard_map/ppermute | solution.py:185
  157.9 3.9 %collective-permute-done.9 = bf16[16,4096]{1,0:T(8,128)(2,1)S(1)} collective-permute-done((bf16[16,4096]{1,0:T(8,128)(2,1)S(1)}, bf16[16,4096]{1,0:T(8,128)(2,1)S(1)}, u32[]{:S(2)}, u32[]{:S(2)}) %collective-permute-start.9) | collective-permute-done | bytes 131104 | tf_op jit(solution)/shard_map/ppermute | solution.py:185
  161.9 3.8 %collective-permute-start.10 = (bf16[32,4096]{1,0:T(8,128)(2,1)S(1)}, bf16[32,4096]{1,0:T(8,128)(2,1)S(1)}, u32[]{:S(2)}, u32[]{:S(2)}) collective-permute-start(bf16[32,4096]{1,0:T(8,128)(2,1)S(1)} %maximum_select_fusion.6), channel_id=1, source_target_pairs={{0,2},{2,0},{4,6},{6,4},{8,10},{10,8},{12,14},{14,12},{1,3},{3,1},... | collective-permute-start | bytes 786440 | tf_op jit(solution)/shard_map/ppermute | solution.py:185
  166.3 12.4 %all-to-all-start.1 = ((s32[16,8,8]{2,1,0:T(8,128)}), s32[16,8,8]{2,1,0:T(8,128)S(1)}, u32[]{:S(2)}, u32[]{:S(2)}) async-start(s32[16,8,8]{2,1,0:T(8,128)} %broadcast_in_dim.166), calls=%async_computation.1 | async-start | bytes 131072 | tf_op jit(solution)/shard_map/all_to_all | solution.py:175
  178.8 2.0 collective-permute-start.11
  180.9 7.8 %all-to-all-done.1 = s32[16,8,8]{2,1,0:T(8,128)S(1)} async-done(((s32[16,8,8]{2,1,0:T(8,128)}), s32[16,8,8]{2,1,0:T(8,128)S(1)}, u32[]{:S(2)}, u32[]{:S(2)}) %all-to-all-start.1) | async-done | bytes 4128 | tf_op jit(solution)/shard_map/all_to_all | solution.py:175
  189.9 15.6 %all-gather.2.cloned.1.call-done = bf16[1536,4096]{1,0:T(8,128)(2,1)} async-done(((bf16[96,4096]{1,0:T(8,128)(2,1)}), bf16[1536,4096]{1,0:T(8,128)(2,1)}) %all-gather.2.cloned.1.call-update) | async-done | bytes 12582928 | tf_op jit(solution)/shard_map/all_gather | solution.py:93
  205.6 6.4 %fusion.95 = f32[1536,128]{1,0:T(8,128)S(1)} fusion(bf16[1536,4096]{1,0:T(8,128)(2,1)} %all-gather.2.cloned.1.call-done, bf16[128,4096]{1,0:T(8,128)(2,1)S(1)} %convolution_convert_fusion), kind=kOutput, calls=%fused_computation.226 | convolution fusion | flops 1610612736 | bytes 14417920 | tf_op jit(solution)/shard_map/fd,sd->fs/dot_general | solution.py:220
  213.0 10.7 %all-to-all-start.2 = ((bf16[16,8,768]{2,1,0:T(8,128)(2,1)}), bf16[16,8,768]{2,1,0:T(8,128)(2,1)S(1)}, u32[]{:S(2)}, u32[]{:S(2)}) async-start(bf16[16,8,768]{2,1,0:T(8,128)(2,1)} %bitcast.49), calls=%async_computation.2 | async-start | bytes 393216 | tf_op jit(solution)/shard_map/all_to_all | solution.py:226
  224.1 14.2 %all-to-all-done.2 = bf16[16,8,768]{2,1,0:T(8,128)(2,1)S(1)} async-done(((bf16[16,8,768]{2,1,0:T(8,128)(2,1)}), bf16[16,8,768]{2,1,0:T(8,128)(2,1)S(1)}, u32[]{:S(2)}, u32[]{:S(2)}) %all-to-all-start.2) | async-done | bytes 196640 | tf_op jit(solution)/shard_map/all_to_all | solution.py:226
  (113 shorter events, 22.1 us)
Async XLA Ops:
  7.2 79.4 %copy-start = (bf16[256,4096]{1,0:T(8,128)(2,1)S(1)}, bf16[256,4096]{1,0:T(8,128)(2,1)}, u32[]{:S(2)}) copy-start(bf16[256,4096]{1,0:T(8,128)(2,1)} %param.17) | copy-start | bytes 6291460
  7.2 198.4 %all-gather.2.cloned.1.call-start = ((), (), s32[]{:S(2)}) async-start(), calls=%async_computation.3 | async-start | bytes 13369344 | tf_op jit(solution)/shard_map/all_gather | solution.py:93
  8.2 17.7 %collective-permute-start.1 = (bf16[128,128]{1,0:T(8,128)(2,1)S(1)}, bf16[128,128]{1,0:T(8,128)(2,1)S(1)}, u32[]{:S(2)}, u32[]{:S(2)}) collective-permute-start(bf16[128,128]{1,0:T(8,128)(2,1)S(1)} %dynamic-slice_select_fusion), channel_id=1, source_target_pairs={{0,256},{16,272},{32,288},{48,304},{64,320},{80,336},{96,352},{112... | collective-permute-start | bytes 98312 | tf_op jit(solution)/shard_map/ppermute | solution.py:86
  25.9 18.1 %collective-permute-start.2 = (bf16[256,128]{1,0:T(8,128)(2,1)S(1)}, bf16[256,128]{1,0:T(8,128)(2,1)S(1)}, u32[]{:S(2)}, u32[]{:S(2)}) collective-permute-start(bf16[256,128]{1,0:T(8,128)(2,1)S(1)} %maximum_select_fusion.9), channel_id=1, source_target_pairs={{0,128},{16,144},{32,160},{48,176},{64,192},{80,208},{96,224},{112... | collective-permute-start | bytes 196616 | tf_op jit(solution)/shard_map/ppermute | solution.py:101
  30.5 31.6 %copy-start.8 = (s32[64]{0:T(128)S(1)}, s32[64]{0:T(128)}, u32[]{:S(2)}) copy-start(s32[64]{0:T(128)} %param.16) | copy-start | bytes 772
  30.5 31.7 %copy-start.9 = (s32[32]{0:T(128)S(1)}, s32[32]{0:T(128)}, u32[]{:S(2)}) copy-start(s32[32]{0:T(128)} %constant.185) | copy-start | bytes 388
  31.6 24.6 %collective-permute-start = (bf16[48,4096]{1,0:T(8,128)(2,1)S(1)}, bf16[48,4096]{1,0:T(8,128)(2,1)S(1)}, u32[]{:S(2)}, u32[]{:S(2)}) collective-permute-start(bf16[48,4096]{1,0:T(8,128)(2,1)S(1)} %pad_maximum_fusion), channel_id=1, source_target_pairs={{0,256},{256,0},{1,257},{257,1},{2,258},{258,2},{3,259},{259,3},{4... | collective-permute-start | bytes 1179656 | tf_op jit(solution)/shard_map/ppermute | solution.py:87
  44.1 6.0 %collective-permute-start.3 = (bf16[512,128]{1,0:T(8,128)(2,1)S(1)}, bf16[512,128]{1,0:T(8,128)(2,1)S(1)}, u32[]{:S(2)}, u32[]{:S(2)}) collective-permute-start(bf16[512,128]{1,0:T(8,128)(2,1)S(1)} %maximum_select_fusion.7), channel_id=1, source_target_pairs={{0,64},{16,80},{32,96},{48,112},{64,0},{80,16},{96,32},{112,48},{1... | collective-permute-start | bytes 393224 | tf_op jit(solution)/shard_map/ppermute | solution.py:101
  50.1 8.6 %collective-permute-start.4 = (bf16[1024,128]{1,0:T(8,128)(2,1)S(1)}, bf16[1024,128]{1,0:T(8,128)(2,1)S(1)}, u32[]{:S(2)}, u32[]{:S(2)}) collective-permute-start(bf16[1024,128]{1,0:T(8,128)(2,1)S(1)} %maximum_select_fusion.5), channel_id=1, source_target_pairs={{0,32},{16,48},{32,0},{48,16},{64,96},{80,112},{96,64},{112,80},{1... | collective-permute-start | bytes 786440 | tf_op jit(solution)/shard_map/ppermute | solution.py:101
  58.9 3.4 %copy-start.1 = (bf16[2048,128]{1,0:T(8,128)(2,1)}, bf16[2048,128]{1,0:T(8,128)(2,1)S(1)}, u32[]{:S(2)}) copy-start(bf16[2048,128]{1,0:T(8,128)(2,1)S(1)} %maximum_select_fusion.3) | copy-start | bytes 1572868
  58.9 11.3 %collective-permute-start.5 = (bf16[2048,128]{1,0:T(8,128)(2,1)S(1)}, bf16[2048,128]{1,0:T(8,128)(2,1)}, u32[]{:S(2)}, u32[]{:S(2)}) collective-permute-start(bf16[2048,128]{1,0:T(8,128)(2,1)S(1)} %maximum_select_fusion.3), channel_id=1, source_target_pairs={{0,16},{16,0},{32,48},{48,32},{64,80},{80,64},{96,112},{112,96},{1... | collective-permute-start | bytes 1572872 | tf_op jit(solution)/shard_map/ppermute | solution.py:101
  72.0 9.4 %collective-permute-start.6 = (bf16[4096,128]{1,0:T(8,128)(2,1)S(1)}, bf16[4096,128]{1,0:T(8,128)(2,1)}, u32[]{:S(2)}, u32[]{:S(2)}) collective-permute-start(bf16[4096,128]{1,0:T(8,128)(2,1)S(1)} %maximum_select_fusion), channel_id=1, source_target_pairs={{0,1},{1,0},{2,3},{3,2},{4,5},{5,4},{6,7},{7,6},{8,9},{9,8},{10,11... | collective-permute-start | bytes 3145736 | tf_op jit(solution)/shard_map/ppermute | solution.py:107
  87.1 57.9 %copy-start.5 = (bf16[8,4096]{1,0:T(8,128)(2,1)S(1)}, bf16[8,4096]{1,0:T(8,128)(2,1)}, u32[]{:S(2)}) copy-start(bf16[8,4096]{1,0:T(8,128)(2,1)} %param.12) | copy-start | bytes 196612
  87.1 58.1 %copy-start.6 = (f32[4096]{0:T(1024)S(1)}, f32[4096]{0:T(1024)}, u32[]{:S(2)}) copy-start(f32[4096]{0:T(1024)} %param.18) | copy-start | bytes 49156
  87.1 78.5 %copy-start.4 = (s32[8,8]{1,0:T(8,128)S(1)}, s32[8,8]{1,0:T(8,128)}, u32[]{:S(2)}) copy-start(s32[8,8]{1,0:T(8,128)} %param.21) | copy-start | bytes 772
  87.2 3.9 %collective-permute-start.7 = (bf16[8,8,4096]{2,1,0:T(8,128)(2,1)S(1)}, bf16[8,8,4096]{2,1,0:T(8,128)(2,1)S(1)}, u32[]{:S(2)}, u32[]{:S(2)}) collective-permute-start(bf16[8,8,4096]{2,1,0:T(8,128)(2,1)S(1)} %fusion.26), channel_id=1, source_target_pairs={{0,1},{1,0},{2,3},{3,2},{4,5},{5,4},{6,7},{7,6},{8,9},{9,8},{10,11... | collective-permute-start | bytes 1572872 | tf_op jit(solution)/shard_map/ppermute | solution.py:165
  145.2 44.1 %copy-start.3 = (bf16[8,4096]{1,0:T(8,128)(2,1)}, bf16[8,4096]{1,0:T(8,128)(2,1)S(1)}, u32[]{:S(2)}) copy-start(bf16[8,4096]{1,0:T(8,128)(2,1)S(1)} %get-tuple-element.9) | copy-start | bytes 196612
  145.3 8.9 %collective-permute-start.8 = (bf16[8,4096]{1,0:T(8,128)(2,1)S(1)}, bf16[8,4096]{1,0:T(8,128)(2,1)S(1)}, u32[]{:S(2)}, u32[]{:S(2)}) collective-permute-start(bf16[8,4096]{1,0:T(8,128)(2,1)S(1)} %fusion.46), channel_id=1, source_target_pairs={{0,8},{2,10},{4,12},{6,14},{8,0},{10,2},{12,4},{14,6},{1,9},{3,11}... | collective-permute-start | bytes 196616 | tf_op jit(solution)/shard_map/ppermute | solution.py:185
  154.2 7.6 %collective-permute-start.9 = (bf16[16,4096]{1,0:T(8,128)(2,1)S(1)}, bf16[16,4096]{1,0:T(8,128)(2,1)S(1)}, u32[]{:S(2)}, u32[]{:S(2)}) collective-permute-start(bf16[16,4096]{1,0:T(8,128)(2,1)S(1)} %maximum_select_fusion.8), channel_id=1, source_target_pairs={{0,4},{2,6},{4,0},{6,2},{8,12},{10,14},{12,8},{14,10},{1,5},{3,7},... | collective-permute-start | bytes 393224 | tf_op jit(solution)/shard_map/ppermute | solution.py:185
  161.9 16.8 %collective-permute-start.10 = (bf16[32,4096]{1,0:T(8,128)(2,1)S(1)}, bf16[32,4096]{1,0:T(8,128)(2,1)S(1)}, u32[]{:S(2)}, u32[]{:S(2)}) collective-permute-start(bf16[32,4096]{1,0:T(8,128)(2,1)S(1)} %maximum_select_fusion.6), channel_id=1, source_target_pairs={{0,2},{2,0},{4,6},{6,4},{8,10},{10,8},{12,14},{14,12},{1,3},{3,1},... | collective-permute-start | bytes 786440 | tf_op jit(solution)/shard_map/ppermute | solution.py:185
  166.3 22.4 %all-to-all-start.1 = ((s32[16,8,8]{2,1,0:T(8,128)}), s32[16,8,8]{2,1,0:T(8,128)S(1)}, u32[]{:S(2)}, u32[]{:S(2)}) async-start(s32[16,8,8]{2,1,0:T(8,128)} %broadcast_in_dim.166), calls=%async_computation.1 | async-start | bytes 131072 | tf_op jit(solution)/shard_map/all_to_all | solution.py:175
  178.8 10.2 %collective-permute-start.11 = (bf16[64,4096]{1,0:T(8,128)(2,1)S(1)}, bf16[64,4096]{1,0:T(8,128)(2,1)S(1)}, u32[]{:S(2)}, u32[]{:S(2)}) collective-permute-start(bf16[64,4096]{1,0:T(8,128)(2,1)S(1)} %maximum_select_fusion.4), channel_id=1, source_target_pairs={{0,1},{1,0},{2,3},{3,2},{4,5},{5,4},{6,7},{7,6},{8,9},{9,8},{10,11... | collective-permute-start | bytes 1572872 | tf_op jit(solution)/shard_map/ppermute | solution.py:189
  212.0 27.0 %copy-start.7 = (f32[8,8]{1,0:T(8,128)S(1)}, f32[8,8]{1,0:T(8,128)}, u32[]{:S(2)}) copy-start(f32[8,8]{1,0:T(8,128)} %param.22) | copy-start | bytes 772
  213.0 25.3 %all-to-all-start.2 = ((bf16[16,8,768]{2,1,0:T(8,128)(2,1)}), bf16[16,8,768]{2,1,0:T(8,128)(2,1)S(1)}, u32[]{:S(2)}, u32[]{:S(2)}) async-start(bf16[16,8,768]{2,1,0:T(8,128)(2,1)} %bitcast.49), calls=%async_computation.2 | async-start | bytes 393216 | tf_op jit(solution)/shard_map/all_to_all | solution.py:226
  (2 other events, 2.7 us)
Sparse Core Ops, SparseCore 0:
  81.2 124.2 all-gather.1

commit v12 on v10

--- a/solution.py
+++ b/solution.py
@@ -170,13 +170,16 @@
     square = jnp.mean(mixed_f * mixed_f, axis=1, keepdims=True)
     normed = (mixed_f * lax.rsqrt(square + 1e-06) * norm_gain[None, :]).astype(jnp.bfloat16)
 
-    ids_all = lax.all_to_all(
-        jnp.broadcast_to(expert_ids[None], (n_exp,) + expert_ids.shape),
+    ids_rw = jnp.concatenate([expert_ids.astype(jnp.float32), route_weight], axis=1)
+    ids_rw_all = lax.all_to_all(
+        jnp.broadcast_to(ids_rw[None], (n_exp,) + ids_rw.shape),
         EXP,
         split_axis=0,
         concat_axis=0,
         tiled=True,
-    ).reshape(n_exp * tok_dev, TOPK)
+    ).reshape(n_exp * tok_dev, 2 * TOPK)
+    ids_all = ids_rw_all[:, :TOPK].astype(jnp.int32)
+    rw_all = ids_rw_all[:, TOPK:]
     cur = normed
     order = [0]
     for bit in doubling_bits(n_zl):
@@ -201,9 +204,10 @@
     dest = jnp.where(
         chosen == 1, jnp.arange(n_exp, dtype=jnp.int32)[:, None] * most_slots + rank, -1
     ).reshape(-1)
-    placing = (
-        jnp.arange(n_exp * most_slots, dtype=jnp.int32)[:, None] == dest[None, :]
-    ).astype(jnp.bfloat16)
+    slot_of = jnp.arange(n_exp * most_slots, dtype=jnp.int32)[:, None] == dest[None, :]
+    placing = slot_of.astype(jnp.bfloat16)
+    rw_tok = jnp.sum(jnp.where(ids_all == exp_index, rw_all, 0.0), axis=1)
+    rw_slot = jnp.sum(jnp.where(slot_of, rw_tok[None, :], 0.0), axis=1)
     received = jnp.dot(placing, normed_all, preferred_element_type=jnp.float32).astype(
         jnp.bfloat16
     )
@@ -219,14 +223,11 @@
     proj = proj.reshape(n_xy, n_zh, 2, fe_dev, EXPERTS * most_slots)
     hidden = jax.nn.silu(proj[:, :, 0]) * proj[:, :, 1]
     hidden = jnp.transpose(hidden, (1, 0, 2, 3)).reshape(FE, EXPERTS * most_slots)
-    hidden = hidden.astype(jnp.bfloat16).T.reshape(EXPERTS, most_slots, FE)
-    returned = (
-        lax.all_to_all(hidden, EXP, split_axis=0, concat_axis=0, tiled=True)
-        .astype(jnp.float32)
-        .reshape(EXPERTS * most_slots, FE)
-    )
-    picked = jnp.take(returned, target, axis=0)
-    routed = (picked * route_weight.reshape(-1)[:, None]).astype(jnp.bfloat16)
+    hidden = (hidden * rw_slot[None, :]).astype(jnp.bfloat16).T.reshape(EXPERTS, most_slots, FE)
+    returned = lax.all_to_all(hidden, EXP, split_axis=0, concat_axis=0, tiled=True).reshape(
+        EXPERTS * most_slots, FE
+    )
+    routed = jnp.take(returned, target, axis=0)
     return (mixed, routed.reshape(tok_dev, TOPK, FE))
 
 

time: 240 us -> 240 us (level)
    all_gather x1, waiting for transfers between devices: 16.5 us -> 20.8 us  [shards(): w_all = lax.all_gather(w_pair, ('x', 'y'), axis=0, tiled=True)]
    ppermute x3, waiting for transfers between devices: 8.26 us -> 4.32 us  [shards(): other = lax.ppermute(cur, 'zl', [(i, i ^ bit) for i in range(n_zl)])]
  transfers between devices with their start and end apart: 15 -> 15, of which waited for: 10 -> 10; matrix products, arithmetic and copies ran while one was open for 7% -> 8% of each run, Pallas kernels for 0% -> 0%
where the time goes in v12:
time: 240 us; the launch traced here: 239 us
  starting transfers between devices  98.8 us (41%)
  waiting for transfers between devices  62.1 us (26%)
  blocking collectives  34 us (14%)
  other arithmetic  15.4 us (6%)
  between operations  14.8 us (6%)
  matrix products  10.1 us (4%)
  local copies, waits for them, and re-layouts  3.99 us (2%)
    all_to_all x1, blocking collectives, shards(): lax.all_to_all(pair_sum, 'zl', split_axis=0, concat_axis=0, tiled=True)  34 us
    all_gather x1, waiting for transfers between devices, shards(): w_all = lax.all_gather(w_pair, ('x', 'y'), axis=0, tiled=True)  20.8 us
    ppermute x1, starting transfers between devices, shards(): lax.ppermute(kv_local, CTX, [(i, i ^ first) for i in range(n_ctx)])  16.3 us
    ppermute x4, starting transfers between devices, shards(): other = lax.ppermute(cur, CTX, [(i, i ^ bit) for i in range(n_ctx)])  14.9 us
    all_to_all x1, waiting for transfers between devices, shards(): lax.all_to_all(hidden, EXP, split_axis=0, concat_axis=0, tiled=True)  14.1 us
    ppermute x4, waiting for transfers between devices, shards(): other = lax.ppermute(cur, CTX, [(i, i ^ bit) for i in range(n_ctx)])  12.8 us
    ppermute x1, starting transfers between devices, shards(): got = lax.ppermute(give, 'c', [(0, 1), (1, 0)])  12.6 us
    ppermute x1, starting transfers between devices, shards(): w_other = lax.ppermute(w_local, 'zh', [(0, 1), (1, 0)])  12.5 us
  transfers between devices with their start and end apart: 15, of which 10 were waited for; matrix products, arithmetic and copies ran while one was open for 8% of the time, Pallas kernels for 0%

profile of v12, /device:TPU:1, one launch (start us, length us, event | category | flops | bytes accessed | tf_op | source)
XLA Modules:
  0.0 239.2 jit_solution(13024758327320912529)
XLA Ops:
  8.2 16.3 %collective-permute-start = (bf16[128,128]{1,0:T(8,128)(2,1)S(1)}, bf16[128,128]{1,0:T(8,128)(2,1)S(1)}, u32[]{:S(2)}, u32[]{:S(2)}) collective-permute-start(bf16[128,128]{1,0:T(8,128)(2,1)S(1)} %dynamic-slice_select_fusion), channel_id=1, source_target_pairs={{0,256},{16,272},{32,288},{48,304},{64,320},{80,336},{96,352},{112... | collective-permute-start | bytes 98312 | tf_op jit(solution)/shard_map/ppermute | solution.py:86
  25.9 4.7 %collective-permute-start.1 = (bf16[256,128]{1,0:T(8,128)(2,1)S(1)}, bf16[256,128]{1,0:T(8,128)(2,1)S(1)}, u32[]{:S(2)}, u32[]{:S(2)}) collective-permute-start(bf16[256,128]{1,0:T(8,128)(2,1)S(1)} %maximum_select_fusion.9), channel_id=1, source_target_pairs={{0,128},{16,144},{32,160},{48,176},{64,192},{80,208},{96,224},{112... | collective-permute-start | bytes 196616 | tf_op jit(solution)/shard_map/ppermute | solution.py:101
  32.4 3.1 %collective-permute-start.2 = (bf16[512,128]{1,0:T(8,128)(2,1)S(1)}, bf16[512,128]{1,0:T(8,128)(2,1)S(1)}, u32[]{:S(2)}, u32[]{:S(2)}) collective-permute-start(bf16[512,128]{1,0:T(8,128)(2,1)S(1)} %maximum_select_fusion.7), channel_id=1, source_target_pairs={{0,64},{16,80},{32,96},{48,112},{64,0},{80,16},{96,32},{112,48},{1... | collective-permute-start | bytes 393224 | tf_op jit(solution)/shard_map/ppermute | solution.py:101
  35.6 2.6 %collective-permute-done.2 = bf16[512,128]{1,0:T(8,128)(2,1)S(1)} collective-permute-done((bf16[512,128]{1,0:T(8,128)(2,1)S(1)}, bf16[512,128]{1,0:T(8,128)(2,1)S(1)}, u32[]{:S(2)}, u32[]{:S(2)}) %collective-permute-start.2) | collective-permute-done | bytes 131104 | tf_op jit(solution)/shard_map/ppermute | solution.py:101
  38.2 4.8 %collective-permute-start.3 = (bf16[1024,128]{1,0:T(8,128)(2,1)S(1)}, bf16[1024,128]{1,0:T(8,128)(2,1)S(1)}, u32[]{:S(2)}, u32[]{:S(2)}) collective-permute-start(bf16[1024,128]{1,0:T(8,128)(2,1)S(1)} %maximum_select_fusion.5), channel_id=1, source_target_pairs={{0,32},{16,48},{32,0},{48,16},{64,96},{80,112},{96,64},{112,80},{1... | collective-permute-start | bytes 786440 | tf_op jit(solution)/shard_map/ppermute | solution.py:101
  44.9 12.5 %collective-permute-start.7 = (bf16[48,4096]{1,0:T(8,128)(2,1)}, bf16[48,4096]{1,0:T(8,128)(2,1)}, u32[]{:S(2)}, u32[]{:S(2)}) collective-permute-start(bf16[48,4096]{1,0:T(8,128)(2,1)} %pad_maximum_fusion), channel_id=1, source_target_pairs={{0,256},{256,0},{1,257},{257,1},{2,258},{258,2},{3,259},{259,3},{4... | collective-permute-start | bytes 1179656 | tf_op jit(solution)/shard_map/ppermute | solution.py:87
  58.2 2.3 collective-permute-start.4
  60.9 8.4 %collective-permute-done.4 = bf16[2048,128]{1,0:T(8,128)(2,1)S(1)} collective-permute-done((bf16[2048,128]{1,0:T(8,128)(2,1)S(1)}, bf16[2048,128]{1,0:T(8,128)(2,1)S(1)}, u32[]{:S(2)}, u32[]{:S(2)}) %collective-permute-start.4) | collective-permute-done | bytes 524320 | tf_op jit(solution)/shard_map/ppermute | solution.py:101
  69.5 7.2 %collective-permute-start.5 = (bf16[4096,128]{1,0:T(8,128)(2,1)S(1)}, bf16[4096,128]{1,0:T(8,128)(2,1)}, u32[]{:S(2)}, u32[]{:S(2)}) collective-permute-start(bf16[4096,128]{1,0:T(8,128)(2,1)S(1)} %maximum_select_fusion), channel_id=1, source_target_pairs={{0,1},{1,0},{2,3},{3,2},{4,5},{5,4},{6,7},{7,6},{8,9},{9,8},{10,11... | collective-permute-start | bytes 3145736 | tf_op jit(solution)/shard_map/ppermute | solution.py:105
  78.0 1.9 broadcast_compare_fusion.1
  79.9 2.2 maximum_select_fusion.2
  88.3 12.6 %collective-permute-start.6 = (bf16[8,8,4096]{2,1,0:T(8,128)(2,1)S(1)}, bf16[8,8,4096]{2,1,0:T(8,128)(2,1)S(1)}, u32[]{:S(2)}, u32[]{:S(2)}) collective-permute-start(bf16[8,8,4096]{2,1,0:T(8,128)(2,1)S(1)} %fusion.26), channel_id=1, source_target_pairs={{0,1},{1,0},{2,3},{3,2},{4,5},{5,4},{6,7},{7,6},{8,9},{9,8},{10,11... | collective-permute-start | bytes 1572872 | tf_op jit(solution)/shard_map/ppermute | solution.py:163
  102.6 34.0 %all_to_all.15 = bf16[8,8,4096]{2,1,0:T(8,128)(2,1)S(1)} all-to-all(bf16[8,8,4096]{2,1,0:T(8,128)(2,1)S(1)} %fusion.13), channel_id=1, replica_groups=mesh['zh'=2,'x'=4,'y'=4,'zl'=8,'c'=2] {'zl'}, dimensions={0} | all-to-all | bytes 1048576 | tf_op jit(solution)/shard_map/all_to_all | solution.py:166
  137.0 4.6 %collective-permute-start.8 = (bf16[8,4096]{1,0:T(8,128)(2,1)S(1)}, bf16[8,4096]{1,0:T(8,128)(2,1)S(1)}, u32[]{:S(2)}, u32[]{:S(2)}) collective-permute-start(bf16[8,4096]{1,0:T(8,128)(2,1)S(1)} %fusion.44), channel_id=1, source_target_pairs={{0,8},{2,10},{4,12},{6,14},{8,0},{10,2},{12,4},{14,6},{1,9},{3,11}... | collective-permute-start | bytes 196616 | tf_op jit(solution)/shard_map/ppermute | solution.py:186
  141.6 4.3 %collective-permute-done.8 = bf16[8,4096]{1,0:T(8,128)(2,1)S(1)} collective-permute-done((bf16[8,4096]{1,0:T(8,128)(2,1)S(1)}, bf16[8,4096]{1,0:T(8,128)(2,1)S(1)}, u32[]{:S(2)}, u32[]{:S(2)}) %collective-permute-start.8) | collective-permute-done | bytes 65568 | tf_op jit(solution)/shard_map/ppermute | solution.py:186
  146.0 3.6 %collective-permute-start.9 = (bf16[16,4096]{1,0:T(8,128)(2,1)S(1)}, bf16[16,4096]{1,0:T(8,128)(2,1)S(1)}, u32[]{:S(2)}, u32[]{:S(2)}) collective-permute-start(bf16[16,4096]{1,0:T(8,128)(2,1)S(1)} %maximum_select_fusion.8), channel_id=1, source_target_pairs={{0,4},{2,6},{4,0},{6,2},{8,12},{10,14},{12,8},{14,10},{1,5},{3,7},... | collective-permute-start | bytes 393224 | tf_op jit(solution)/shard_map/ppermute | solution.py:186
  150.4 10.6 %all-to-all-start.1 = ((f32[16,1,128]{2,1,0:T(1,128)}), f32[16,1,128]{2,1,0:T(1,128)S(1)}, u32[]{:S(2)}, u32[]{:S(2)}) async-start(f32[16,1,128]{2,1,0:T(1,128)} %reshape.398), calls=%async_computation.1 | async-start | bytes 16384 | tf_op jit(solution)/shard_map/all_to_all | solution.py:174
  161.0 3.3 %collective-permute-start.10 = (bf16[32,4096]{1,0:T(8,128)(2,1)S(1)}, bf16[32,4096]{1,0:T(8,128)(2,1)S(1)}, u32[]{:S(2)}, u32[]{:S(2)}) collective-permute-start(bf16[32,4096]{1,0:T(8,128)(2,1)S(1)} %maximum_select_fusion.6), channel_id=1, source_target_pairs={{0,2},{2,0},{4,6},{6,4},{8,10},{10,8},{12,14},{14,12},{1,3},{3,1},... | collective-permute-start | bytes 786440 | tf_op jit(solution)/shard_map/ppermute | solution.py:186
  164.6 6.1 %all-to-all-done.1 = f32[16,1,128]{2,1,0:T(1,128)S(1)} async-done(((f32[16,1,128]{2,1,0:T(1,128)}), f32[16,1,128]{2,1,0:T(1,128)S(1)}, u32[]{:S(2)}, u32[]{:S(2)}) %all-to-all-start.1) | async-done | bytes 8224 | tf_op jit(solution)/shard_map/all_to_all | solution.py:174
  172.3 2.6 %collective-permute-start.11 = (bf16[64,4096]{1,0:T(8,128)(2,1)S(1)}, bf16[64,4096]{1,0:T(8,128)(2,1)S(1)}, u32[]{:S(2)}, u32[]{:S(2)}) collective-permute-start(bf16[64,4096]{1,0:T(8,128)(2,1)S(1)} %maximum_select_fusion.4), channel_id=1, source_target_pairs={{0,1},{1,0},{2,3},{3,2},{4,5},{5,4},{6,7},{7,6},{8,9},{9,8},{10,11... | collective-permute-start | bytes 1572872 | tf_op jit(solution)/shard_map/ppermute | solution.py:190
  177.3 20.8 %all-gather.2.cloned.1.call-done = bf16[1536,4096]{1,0:T(8,128)(2,1)} async-done(((bf16[96,4096]{1,0:T(8,128)(2,1)}), bf16[1536,4096]{1,0:T(8,128)(2,1)}) %all-gather.2.cloned.1.call-update) | async-done | bytes 12582928 | tf_op jit(solution)/shard_map/all_gather | solution.py:93
  198.1 6.4 %fusion.94 = f32[1536,128]{1,0:T(8,128)S(1)} fusion(bf16[1536,4096]{1,0:T(8,128)(2,1)} %all-gather.2.cloned.1.call-done, bf16[128,4096]{1,0:T(8,128)(2,1)S(1)} %convolution_convert_fusion), kind=kOutput, calls=%fused_computation.228 | convolution fusion | flops 1610612736 | bytes 14417920 | tf_op jit(solution)/shard_map/fd,sd->fs/dot_general | solution.py:222
  205.6 10.7 %all-to-all-start.2 = ((bf16[16,8,768]{2,1,0:T(8,128)(2,1)}), bf16[16,8,768]{2,1,0:T(8,128)(2,1)S(1)}, u32[]{:S(2)}, u32[]{:S(2)}) async-start(bf16[16,8,768]{2,1,0:T(8,128)(2,1)} %bitcast.50), calls=%async_computation.2 | async-start | bytes 393216 | tf_op jit(solution)/shard_map/all_to_all | solution.py:227
  216.8 14.1 %all-to-all-done.2 = bf16[16,8,768]{2,1,0:T(8,128)(2,1)S(1)} async-done(((bf16[16,8,768]{2,1,0:T(8,128)(2,1)}), bf16[16,8,768]{2,1,0:T(8,128)(2,1)S(1)}, u32[]{:S(2)}, u32[]{:S(2)}) %all-to-all-start.2) | async-done | bytes 196640 | tf_op jit(solution)/shard_map/all_to_all | solution.py:227
  (130 shorter events, 24.8 us)
Async XLA Ops:
  7.2 80.6 %copy-start = (bf16[256,4096]{1,0:T(8,128)(2,1)S(1)}, bf16[256,4096]{1,0:T(8,128)(2,1)}, u32[]{:S(2)}) copy-start(bf16[256,4096]{1,0:T(8,128)(2,1)} %param.17) | copy-start | bytes 6291460
  7.2 53.4 %copy-start.12 = (s32[64]{0:T(128)S(1)}, s32[64]{0:T(128)}, u32[]{:S(2)}) copy-start(s32[64]{0:T(128)} %param.16) | copy-start | bytes 772
  7.2 190.9 %all-gather.2.cloned.1.call-start = ((), (), s32[]{:S(2)}) async-start(), calls=%async_computation.3 | async-start | bytes 13369344 | tf_op jit(solution)/shard_map/all_gather | solution.py:93
  8.2 17.7 %collective-permute-start = (bf16[128,128]{1,0:T(8,128)(2,1)S(1)}, bf16[128,128]{1,0:T(8,128)(2,1)S(1)}, u32[]{:S(2)}, u32[]{:S(2)}) collective-permute-start(bf16[128,128]{1,0:T(8,128)(2,1)S(1)} %dynamic-slice_select_fusion), channel_id=1, source_target_pairs={{0,256},{16,272},{32,288},{48,304},{64,320},{80,336},{96,352},{112... | collective-permute-start | bytes 98312 | tf_op jit(solution)/shard_map/ppermute | solution.py:86
  25.9 6.5 %collective-permute-start.1 = (bf16[256,128]{1,0:T(8,128)(2,1)S(1)}, bf16[256,128]{1,0:T(8,128)(2,1)S(1)}, u32[]{:S(2)}, u32[]{:S(2)}) collective-permute-start(bf16[256,128]{1,0:T(8,128)(2,1)S(1)} %maximum_select_fusion.9), channel_id=1, source_target_pairs={{0,128},{16,144},{32,160},{48,176},{64,192},{80,208},{96,224},{112... | collective-permute-start | bytes 196616 | tf_op jit(solution)/shard_map/ppermute | solution.py:101
  32.4 5.7 %collective-permute-start.2 = (bf16[512,128]{1,0:T(8,128)(2,1)S(1)}, bf16[512,128]{1,0:T(8,128)(2,1)S(1)}, u32[]{:S(2)}, u32[]{:S(2)}) collective-permute-start(bf16[512,128]{1,0:T(8,128)(2,1)S(1)} %maximum_select_fusion.7), channel_id=1, source_target_pairs={{0,64},{16,80},{32,96},{48,112},{64,0},{80,16},{96,32},{112,48},{1... | collective-permute-start | bytes 393224 | tf_op jit(solution)/shard_map/ppermute | solution.py:101
  38.2 19.9 %collective-permute-start.3 = (bf16[1024,128]{1,0:T(8,128)(2,1)S(1)}, bf16[1024,128]{1,0:T(8,128)(2,1)S(1)}, u32[]{:S(2)}, u32[]{:S(2)}) collective-permute-start(bf16[1024,128]{1,0:T(8,128)(2,1)S(1)} %maximum_select_fusion.5), channel_id=1, source_target_pairs={{0,32},{16,48},{32,0},{48,16},{64,96},{80,112},{96,64},{112,80},{1... | collective-permute-start | bytes 786440 | tf_op jit(solution)/shard_map/ppermute | solution.py:101
  44.9 35.0 %copy-start.1 = (bf16[1,4096,24]{1,2,0:T(8,128)(2,1)S(1)}, bf16[1,4096,24]{1,2,0:T(8,128)(2,1)}, u32[]{:S(2)}) copy-start(bf16[1,4096,24]{1,2,0:T(8,128)(2,1)} %param.20) | copy-start | bytes 589828
  44.9 35.0 %copy-start.2 = (bf16[1,4096,24]{1,2,0:T(8,128)(2,1)S(1)}, bf16[1,4096,24]{1,2,0:T(8,128)(2,1)}, u32[]{:S(2)}) copy-start(bf16[1,4096,24]{1,2,0:T(8,128)(2,1)} %param.19) | copy-start | bytes 589828
  44.9 35.0 %collective-permute-start.7 = (bf16[48,4096]{1,0:T(8,128)(2,1)}, bf16[48,4096]{1,0:T(8,128)(2,1)}, u32[]{:S(2)}, u32[]{:S(2)}) collective-permute-start(bf16[48,4096]{1,0:T(8,128)(2,1)} %pad_maximum_fusion), channel_id=1, source_target_pairs={{0,256},{256,0},{1,257},{257,1},{2,258},{258,2},{3,259},{259,3},{4... | collective-permute-start | bytes 1179656 | tf_op jit(solution)/shard_map/ppermute | solution.py:87
  58.2 11.0 %collective-permute-start.4 = (bf16[2048,128]{1,0:T(8,128)(2,1)S(1)}, bf16[2048,128]{1,0:T(8,128)(2,1)S(1)}, u32[]{:S(2)}, u32[]{:S(2)}) collective-permute-start(bf16[2048,128]{1,0:T(8,128)(2,1)S(1)} %maximum_select_fusion.3), channel_id=1, source_target_pairs={{0,16},{16,0},{32,48},{48,32},{64,80},{80,64},{96,112},{112,96},{1... | collective-permute-start | bytes 1572872 | tf_op jit(solution)/shard_map/ppermute | solution.py:101
  69.5 12.7 %collective-permute-start.5 = (bf16[4096,128]{1,0:T(8,128)(2,1)S(1)}, bf16[4096,128]{1,0:T(8,128)(2,1)}, u32[]{:S(2)}, u32[]{:S(2)}) collective-permute-start(bf16[4096,128]{1,0:T(8,128)(2,1)S(1)} %maximum_select_fusion), channel_id=1, source_target_pairs={{0,1},{1,0},{2,3},{3,2},{4,5},{5,4},{6,7},{7,6},{8,9},{9,8},{10,11... | collective-permute-start | bytes 3145736 | tf_op jit(solution)/shard_map/ppermute | solution.py:105
  88.3 48.5 %copy-start.8 = (bf16[8,4096]{1,0:T(8,128)(2,1)S(1)}, bf16[8,4096]{1,0:T(8,128)(2,1)}, u32[]{:S(2)}) copy-start(bf16[8,4096]{1,0:T(8,128)(2,1)} %param.12) | copy-start | bytes 196612
  88.3 48.6 %copy-start.10 = (f32[4096]{0:T(1024)S(1)}, f32[4096]{0:T(1024)}, u32[]{:S(2)}) copy-start(f32[4096]{0:T(1024)} %param.18) | copy-start | bytes 49156
  88.3 61.3 %copy-start.9 = (s32[8,8]{1,0:T(8,128)S(1)}, s32[8,8]{1,0:T(8,128)}, u32[]{:S(2)}) copy-start(s32[8,8]{1,0:T(8,128)} %param.21) | copy-start | bytes 772
  88.3 61.3 %copy-start.11 = (f32[8,8]{1,0:T(8,128)S(1)}, f32[8,8]{1,0:T(8,128)}, u32[]{:S(2)}) copy-start(f32[8,8]{1,0:T(8,128)} %param.22) | copy-start | bytes 772
  88.3 14.1 %collective-permute-start.6 = (bf16[8,8,4096]{2,1,0:T(8,128)(2,1)S(1)}, bf16[8,8,4096]{2,1,0:T(8,128)(2,1)S(1)}, u32[]{:S(2)}, u32[]{:S(2)}) collective-permute-start(bf16[8,8,4096]{2,1,0:T(8,128)(2,1)S(1)} %fusion.26), channel_id=1, source_target_pairs={{0,1},{1,0},{2,3},{3,2},{4,5},{5,4},{6,7},{7,6},{8,9},{9,8},{10,11... | collective-permute-start | bytes 1572872 | tf_op jit(solution)/shard_map/ppermute | solution.py:163
  136.9 39.7 %copy-start.7 = (bf16[8,4096]{1,0:T(8,128)(2,1)}, bf16[8,4096]{1,0:T(8,128)(2,1)S(1)}, u32[]{:S(2)}) copy-start(bf16[8,4096]{1,0:T(8,128)(2,1)S(1)} %get-tuple-element.9) | copy-start | bytes 196612
  137.0 8.9 %collective-permute-start.8 = (bf16[8,4096]{1,0:T(8,128)(2,1)S(1)}, bf16[8,4096]{1,0:T(8,128)(2,1)S(1)}, u32[]{:S(2)}, u32[]{:S(2)}) collective-permute-start(bf16[8,4096]{1,0:T(8,128)(2,1)S(1)} %fusion.44), channel_id=1, source_target_pairs={{0,8},{2,10},{4,12},{6,14},{8,0},{10,2},{12,4},{14,6},{1,9},{3,11}... | collective-permute-start | bytes 196616 | tf_op jit(solution)/shard_map/ppermute | solution.py:186
  146.0 15.0 %collective-permute-start.9 = (bf16[16,4096]{1,0:T(8,128)(2,1)S(1)}, bf16[16,4096]{1,0:T(8,128)(2,1)S(1)}, u32[]{:S(2)}, u32[]{:S(2)}) collective-permute-start(bf16[16,4096]{1,0:T(8,128)(2,1)S(1)} %maximum_select_fusion.8), channel_id=1, source_target_pairs={{0,4},{2,6},{4,0},{6,2},{8,12},{10,14},{12,8},{14,10},{1,5},{3,7},... | collective-permute-start | bytes 393224 | tf_op jit(solution)/shard_map/ppermute | solution.py:186
  150.4 20.3 %all-to-all-start.1 = ((f32[16,1,128]{2,1,0:T(1,128)}), f32[16,1,128]{2,1,0:T(1,128)S(1)}, u32[]{:S(2)}, u32[]{:S(2)}) async-start(f32[16,1,128]{2,1,0:T(1,128)} %reshape.398), calls=%async_computation.1 | async-start | bytes 16384 | tf_op jit(solution)/shard_map/all_to_all | solution.py:174
  161.0 11.1 %collective-permute-start.10 = (bf16[32,4096]{1,0:T(8,128)(2,1)S(1)}, bf16[32,4096]{1,0:T(8,128)(2,1)S(1)}, u32[]{:S(2)}, u32[]{:S(2)}) collective-permute-start(bf16[32,4096]{1,0:T(8,128)(2,1)S(1)} %maximum_select_fusion.6), channel_id=1, source_target_pairs={{0,2},{2,0},{4,6},{6,4},{8,10},{10,8},{12,14},{14,12},{1,3},{3,1},... | collective-permute-start | bytes 786440 | tf_op jit(solution)/shard_map/ppermute | solution.py:186
  172.3 4.1 %collective-permute-start.11 = (bf16[64,4096]{1,0:T(8,128)(2,1)S(1)}, bf16[64,4096]{1,0:T(8,128)(2,1)S(1)}, u32[]{:S(2)}, u32[]{:S(2)}) collective-permute-start(bf16[64,4096]{1,0:T(8,128)(2,1)S(1)} %maximum_select_fusion.4), channel_id=1, source_target_pairs={{0,1},{1,0},{2,3},{3,2},{4,5},{5,4},{6,7},{7,6},{8,9},{9,8},{10,11... | collective-permute-start | bytes 1572872 | tf_op jit(solution)/shard_map/ppermute | solution.py:190
  205.6 25.3 %all-to-all-start.2 = ((bf16[16,8,768]{2,1,0:T(8,128)(2,1)}), bf16[16,8,768]{2,1,0:T(8,128)(2,1)S(1)}, u32[]{:S(2)}, u32[]{:S(2)}) async-start(bf16[16,8,768]{2,1,0:T(8,128)(2,1)} %bitcast.50), calls=%async_computation.2 | async-start | bytes 393216 | tf_op jit(solution)/shard_map/all_to_all | solution.py:227
  (5 other events, 7.3 us)
Sparse Core Ops, SparseCore 0:
  82.2 115.8 all-gather.1
